TPU v7x, 128 devices: a whole 4x4x4 slice. The times are simulated.
128 devices in a mesh: dp: 16 (over y, z_lo, core), tensor: 8 (over z_hi, x).
Axes of the slice: x: 4, y: 4, z: 4 (z_hi: 2, z_lo: 2; z = z_hi * 2 + z_lo), core: 2. Of those that a mesh axis runs over, the one named last changes fastest.
Arguments:
- stream: bfloat16 [16384, 2048], P(('dp', 'tensor')), may hold values from -6 to 6
- segment: int32 [16384], P('dp'), may hold values from -1 to 16383, as said below
- position: int32 [16384], P('dp'), may hold values from 0 to 4606, as said below
- w_qkv: bfloat16 [3, 2048, 2048], P(None, 'dp', 'tensor'), may hold values from -0.5 to 0.5
- w_out: bfloat16 [2048, 2048], P('tensor', 'dp'), may hold values from -0.125 to 0.125
- w_gate_up: bfloat16 [2, 2048, 8192], P(None, 'dp', 'tensor'), may hold values from -0.125 to 0.125
- w_down: bfloat16 [8192, 2048], P('tensor', 'dp'), may hold values from -0.0625 to 0.0625
- page_table: int32 [1024], P('dp'), may hold values from 0 to 1023, as said below
Outputs:
- layer_out: bfloat16 [16384, 2048], P(('dp', 'tensor'))
- kv_cache: bfloat16 [1024, 2, 16, 2048], P('dp', None, None, 'tensor')
Inputs may be any that keep to these rules, and one draw needn't show every extreme that they name: `segment`: each group's tokens form prompts of 64 to 512 tokens with distinct numbers, laid one after another, followed by padding -1 at the end of the group's stream; some prompt has 512 tokens in every group. Within a prompt positions rise by one from a first position below 4096; padding has position 0; in every group some prompt of 512 tokens starts at 4095. `page_table`: A permutation of all 1024 page ids. Among the 64 blocks of one request group, exactly 4 fall into each of the ranges o * 64 to (o + 1) * 64 - 1.
All inputs are finite; a program needn't handle non-finite values.
Results may differ from a plain program's by a relative error of at most 0.015.
Values may be sent and summed in bfloat16 or wider, within the bound.
No kernel may reach another device: no remote copies, remote signals or barrier semaphores. Data moves between devices by JAX's collectives and lax.ppermute only.
A program may use at most 128 MiB of HBM per device.

v0:
```python
import math

import jax
import jax.numpy as jnp
from jax import lax
from jax.sharding import PartitionSpec as P

HD = 128


def layer_norm(values):
    values = values.astype(jnp.float32)
    center = values - jnp.mean(values, axis=-1, keepdims=True)
    spread = jnp.mean(center * center, axis=-1, keepdims=True)
    return center * lax.rsqrt(spread + 1e-05)


def rotate(values, position):
    half = values.shape[-1] // 2
    freq = 10000.0 ** (-jnp.arange(half, dtype=jnp.float32) * 2.0 / values.shape[-1])
    angle = position.astype(jnp.float32)[:, None] * freq[None, :]
    cosine = jnp.cos(angle)[:, None, :]
    sine = jnp.sin(angle)[:, None, :]
    first = values[..., :half]
    second = values[..., half:]
    return jnp.concatenate(
        [first * cosine - second * sine, second * cosine + first * sine], axis=-1
    )


def row_folder(source, piece):
    return jnp.einsum("td,cdf->ctf", source, piece, preferred_element_type=jnp.float32)


def attend(query, keys, values, segment):
    tokens = query.shape[0]
    block = min(512, tokens)
    scale = 1.0 / math.sqrt(HD)
    order = jnp.arange(tokens)
    outputs = []
    for first in range(0, tokens, block):
        last = first + block
        scores = (
            jnp.einsum(
                "qhd,khd->hqk", query[first:last], keys[:last], preferred_element_type=jnp.float32
            )
            * scale
        )
        allowed = (segment[first:last, None] == segment[None, :last]) & (
            order[None, :last] <= order[first:last, None]
        )
        top = jnp.max(jnp.where(allowed[None], scores, -1e30), axis=-1, keepdims=True)
        weights = jnp.exp(jnp.where(allowed[None], scores - top, -1e30))
        total = jnp.sum(weights, axis=-1)
        mixed = jnp.einsum(
            "hqk,khd->qhd",
            weights.astype(jnp.bfloat16),
            values[:last],
            preferred_element_type=jnp.float32,
        )
        outputs.append((mixed / jnp.transpose(total)[:, :, None]).astype(jnp.bfloat16))
    return jnp.concatenate(outputs, axis=0).reshape(tokens, -1)


def write_cache(keys, values, page_table):
    tokens = keys.shape[0]
    width = keys.shape[1] * keys.shape[2]
    pages = page_table.shape[0]
    page_size = tokens // pages
    owners = lax.axis_size("dp")
    per_owner = pages // owners
    stacked = jnp.stack([keys.reshape(tokens, width), values.reshape(tokens, width)], axis=0)
    stacked = stacked.reshape(2, pages, page_size, width).transpose(1, 0, 2, 3)
    order = jnp.argsort(page_table // pages, stable=True)
    outgoing = stacked[order].reshape(owners, per_owner, 2, page_size, width)
    outgoing_ids = page_table[order].reshape(owners, per_owner)
    arrived, arrived_ids = (
        lax.all_to_all(outgoing, "dp", split_axis=0, concat_axis=0, tiled=True),
        lax.all_to_all(outgoing_ids, "dp", split_axis=0, concat_axis=0, tiled=True),
    )
    local = (arrived_ids - lax.axis_index("dp") * pages).reshape(-1)
    empty = jnp.zeros((pages, 2, page_size, width), jnp.bfloat16)
    return empty.at[local].set(arrived.reshape(pages, 2, page_size, width))


def body(stream, segment, position, w_qkv, w_out, w_gate_up, w_down, page_table):
    tok_group = segment.shape[0]
    share_rows = stream.shape[0]
    full_stream = lax.all_gather(stream, "tensor", axis=0, tiled=True)
    normed = layer_norm(full_stream).astype(jnp.bfloat16)
    local_heads = w_qkv.shape[2] // HD
    projected = row_folder(normed, lax.all_gather(w_qkv, "dp", axis=1, tiled=True))
    query = rotate(projected[0].reshape(tok_group, local_heads, HD), position).astype(jnp.bfloat16)
    keys = rotate(projected[1].reshape(tok_group, local_heads, HD), position).astype(jnp.bfloat16)
    values = projected[2].reshape(tok_group, local_heads, HD).astype(jnp.bfloat16)
    context = attend(query, keys, values, segment)
    attn_part = jnp.dot(
        context, lax.all_gather(w_out, "dp", axis=1, tiled=True), preferred_element_type=jnp.float32
    )
    attn_whole = lax.psum(attn_part.astype(jnp.bfloat16), "tensor").astype(jnp.float32)
    mid = (full_stream.astype(jnp.float32) + attn_whole).astype(jnp.bfloat16)
    normed2 = layer_norm(mid).astype(jnp.bfloat16)
    gate_up = row_folder(normed2, lax.all_gather(w_gate_up, "dp", axis=1, tiled=True))
    hidden = (jax.nn.silu(gate_up[0]) * gate_up[1]).astype(jnp.bfloat16)
    mlp_part = jnp.dot(
        hidden, lax.all_gather(w_down, "dp", axis=1, tiled=True), preferred_element_type=jnp.float32
    )
    mlp_whole = lax.psum(mlp_part.astype(jnp.bfloat16), "tensor").astype(jnp.float32)
    result = (mid.astype(jnp.float32) + mlp_whole).astype(jnp.bfloat16)
    layer_out = lax.dynamic_slice_in_dim(
        result, lax.axis_index("tensor") * share_rows, share_rows, 0
    )
    kv_cache = write_cache(keys, values, page_table)
    return (layer_out, kv_cache)


def solution(mesh):
    return jax.shard_map(
        body,
        mesh=mesh,
        in_specs=(
            P(("dp", "tensor"), None),
            P("dp"),
            P("dp"),
            P(None, "dp", "tensor"),
            P("tensor", "dp"),
            P(None, "dp", "tensor"),
            P("tensor", "dp"),
            P("dp"),
        ),
        out_specs=(P(("dp", "tensor"), None), P("dp", None, None, "tensor")),
        check_vma=False,
    )
```

profile of v0, /device:TPU:1, one launch (start us, length us, event | category | flops | bytes accessed | tf_op | source)
XLA Modules:
  0.0 515.2 jit_solution(17798327678414374484)
XLA Ops:
  7.2 0.7 all-gather.6.cloned.1.call-update
  7.9 1.7 copy.27
  9.8 0.7 all-gather.10.cloned.1.call-update
  10.5 0.7 convert_element_type.76
  11.2 0.8 fusion.83
  12.0 1.9 multiply_cosine_fusion
  13.9 0.3 compare_and_fusion
  14.2 2.1 fusion.35
  16.2 68.2 %all-gather.6.cloned.1.call-done = bf16[1024,2048]{1,0:T(8,128)(2,1)} async-done(((bf16[128,2048]{1,0:T(8,128)(2,1)}), bf16[1024,2048]{1,0:T(8,128)(2,1)}) %all-gather.6.cloned.1.call-update) | async-done | bytes 4194320 | tf_op jit(solution)/shard_map/all_gather | solution.py:89
  84.4 3.0 convert_reduce_fusion
  87.4 0.5 copy-done.2
  87.9 1.2 fusion.4
  89.1 37.2 %all-gather.8.cloned.1.call-done = bf16[3,2048,256]{1,2,0:T(8,128)(2,1)} async-done(((bf16[3,128,256]{1,2,0:T(8,128)(2,1)}), bf16[3,2048,256]{1,2,0:T(8,128)(2,1)}) %all-gather.8.cloned.1.call-update) | async-done | bytes 3145744 | tf_op jit(solution)/shard_map/all_gather | solution.py:92
  126.3 7.3 %fusion.38 = f32[3,1024,256]{1,2,0:T(8,128)S(1)} fusion(bf16[3,2048,256]{1,2,0:T(8,128)(2,1)} %all-gather.8.cloned.1.call-done, bf16[1024,2048]{1,0:T(8,128)(2,1)} %all-gather.6.cloned.1.call-done, f32[1024]{0:T(1024)S(1)} %add_rsqrt_fusion.1, f32[1024]{0:T(1024)S(1)} %broadcast_multiply_fusion.1), kind=kOutput, calls=%fused_computation.47 | convolution fusion | flops 3229614080 | bytes 10493952 | tf_op jit(solution)/shard_map/td,cdf->ctf/dot_general | solution.py:32
  133.6 0.2 fusion.80
  133.9 0.9 slice.112
  134.8 1.0 fusion.81
  135.8 1.4 copy.41
  137.2 2.4 copy.42
  139.5 1.1 fusion.82
  140.6 1.4 copy.39
  142.0 2.4 copy.40
  144.4 1.6 multiply_subtract_fusion
  145.9 0.3 maximum_convert_fusion
  146.3 0.3 subtract_convert_fusion
  146.6 0.8 copy-done.7
  147.3 0.5 fusion.60
  147.9 1.3 copy-done.6
  149.2 1.1 fusion.85
  150.3 3.4 fusion.48
  153.7 3.9 fusion.84
  157.6 2.5 fusion.49
  160.1 1.8 all-gather.10.cloned.1.call-done
  161.9 4.5 convolution_convert_fusion
  166.5 0.5 all-gather.12.cloned.1.call-update
  167.1 0.5 all-gather.14.cloned.1.call-update
  167.6 0.3 all-reduce.5.cloned.1.call-start
  167.9 108.5 %all-reduce.3.cloned.1.call-done = bf16[1024,2048]{1,0:T(8,128)(2,1)} async-done(((bf16[1024,2048]{1,0:T(8,128)(2,1)}), bf16[1024,2048]{1,0:T(8,128)(2,1)}) %all-reduce.3.cloned.1.call-update) | async-done | bytes 4194320 | tf_op jit(solution)/shard_map/psum | solution.py:100
  276.4 4.8 convert_reduce_fusion.1
  281.1 1.9 copy-done.1
  283.1 1.2 multiply_reduce_fusion
  284.3 44.9 %all-gather.12.cloned.1.call-done = bf16[2,2048,1024]{2,1,0:T(8,128)(2,1)} async-done(((bf16[2,128,1024]{2,1,0:T(8,128)(2,1)}), bf16[2,2048,1024]{2,1,0:T(8,128)(2,1)}) %all-gather.12.cloned.1.call-update) | async-done | bytes 8388624 | tf_op jit(solution)/shard_map/all_gather | solution.py:103
  329.2 14.6 %fusion.23 = f32[2,1024,1024]{2,1,0:T(8,128)} fusion(bf16[2,2048,1024]{2,1,0:T(8,128)(2,1)} %all-gather.12.cloned.1.call-done, bf16[1024,2048]{1,0:T(8,128)(2,1)} %copy-done.1, f32[1024]{0:T(1024)S(1)} %add_rsqrt_fusion, f32[1024]{0:T(1024)S(1)} %broadcast_multiply_fusion), kind=kOutput, calls=%fused_computation.34 | convolution fusion | flops 8598323200 | bytes 20979712 | tf_op jit(solution)/shard_map/td,cdf->ctf/dot_general | solution.py:32
  343.8 32.8 %all-gather.14.cloned.1.call-done = bf16[1024,2048]{1,0:T(8,128)(2,1)} async-done(((bf16[1024,128]{1,0:T(8,128)(2,1)}), bf16[1024,2048]{1,0:T(8,128)(2,1)}) %all-gather.14.cloned.1.call-update) | async-done | bytes 4194320 | tf_op jit(solution)/shard_map/all_gather | solution.py:106
  376.5 11.2 %convolution_convert_fusion.1 = bf16[1024,2048]{1,0:T(8,128)(2,1)} fusion(bf16[1024,2048]{1,0:T(8,128)(2,1)} %all-gather.14.cloned.1.call-done, f32[2,1024,1024]{2,1,0:T(8,128)} %fusion.23), kind=kOutput, calls=%fused_computation.32 | convolution fusion | flops 4303355904 | bytes 16777216 | tf_op jit(solution)/shard_map/dot_general | solution.py:105
  387.7 0.6 copy-done
  388.4 2.0 sort.17
  390.4 0.8 gather_fusion
  391.2 0.7 all_to_all.9
  391.9 4.3 all-to-all-start
  396.2 0.5 copy.34
  396.7 0.2 copy.35
  396.9 0.3 convert_element_type.92
  397.3 0.1 maximum_bitcast_fusion
  397.4 1.6 gather_fusion.1
  398.9 2.7 all-to-all-done
  401.7 4.1 all-to-all-start.1
  405.8 0.1 sub.74
  405.9 45.7 %all-to-all-done.1 = bf16[16,4,2,16,256]{4,3,2,1,0:T(8,128)(2,1)S(1)} async-done(((bf16[16,4,2,16,256]{4,3,2,1,0:T(8,128)(2,1)}), bf16[16,4,2,16,256]{4,3,2,1,0:T(8,128)(2,1)S(1)}, u32[]{:S(2)}, u32[]{:S(2)}) %all-to-all-start.1) | async-done | bytes 1048608 | tf_op jit(solution)/shard_map/all_to_all | solution.py:78
  451.6 0.1 broadcast_in_dim.40
  451.7 2.5 scatter_fusion
  454.2 6.8 %convert_element_type.86 = f32[1024,2048]{1,0:T(8,128)} convert(bf16[1024,2048]{1,0:T(8,128)(2,1)} %copy-done.1) | non-fusion elementwise | flops 2097152 | bytes 12582912 | tf_op jit(solution)/shard_map/convert_element_type | solution.py:109
  461.1 45.0 %all-reduce.5.cloned.1.call-done = bf16[1024,2048]{1,0:T(8,128)(2,1)} async-done(((bf16[1024,2048]{1,0:T(8,128)(2,1)}), bf16[1024,2048]{1,0:T(8,128)(2,1)}) %all-reduce.5.cloned.1.call-update) | async-done | bytes 4194320 | tf_op jit(solution)/shard_map/psum | solution.py:108
  506.1 2.3 fusion.52
  (42 shorter events, 0.5 us)
Async XLA Ops:
  7.2 77.3 %all-gather.6.cloned.1.call-start = ((), (), s32[]{:S(2)}) async-start(), calls=%async_computation.2 | async-start | bytes 4718592 | tf_op jit(solution)/shard_map/all_gather | solution.py:89
  7.9 118.4 %all-gather.8.cloned.1.call-start = ((), (), s32[]{:S(2)}) async-start(), calls=%async_computation.3 | async-start | bytes 3342336 | tf_op jit(solution)/shard_map/all_gather | solution.py:92
  9.7 152.2 %all-gather.10.cloned.1.call-start = ((), (), s32[]{:S(2)}) async-start(), calls=%async_computation.4 | async-start | bytes 1114112 | tf_op jit(solution)/shard_map/all_gather | solution.py:98
  10.4 265.9 %all-reduce.3.cloned.1.call-start = ((), (), s32[]{:S(2)}) async-start(), calls=%async_computation.5 | async-start | bytes 8388608 | tf_op jit(solution)/shard_map/psum | solution.py:100
  84.4 3.4 copy-start.2
  144.4 1.9 copy-start.4
  146.5 0.8 copy-start.7
  147.3 2.9 slice-start
  147.9 1.3 copy-start.6
  149.2 4.5 copy-start.8
  149.2 4.5 copy-start.9
  153.7 3.9 copy-start.5
  166.4 162.8 %all-gather.12.cloned.1.call-start = ((), (), s32[]{:S(2)}) async-start(), calls=%async_computation.6 | async-start | bytes 8912896 | tf_op jit(solution)/shard_map/all_gather | solution.py:103
  167.0 209.5 %all-gather.14.cloned.1.call-start = ((), (), s32[]{:S(2)}) async-start(), calls=%async_computation.7 | async-start | bytes 4456448 | tf_op jit(solution)/shard_map/all_gather | solution.py:106
  167.6 338.5 %all-reduce.5.cloned.1.call-start = ((), (), s32[]{:S(2)}) async-start(), calls=%async_computation.8 | async-start | bytes 8388608 | tf_op jit(solution)/shard_map/psum | solution.py:108
  281.1 1.9 copy-start.1
  387.7 0.7 copy-start
  391.9 9.8 %all-to-all-start = ((s32[16,1,4]{2,1,0:T(1,128)}), s32[16,1,4]{2,1,0:T(1,128)S(1)}, u32[]{:S(2)}, u32[]{:S(2)}) async-start(s32[16,1,4]{2,1,0:T(1,128)} %bitcast.15), calls=%async_computation | async-start | bytes 16384 | tf_op jit(solution)/shard_map/all_to_all | solution.py:79
  401.7 49.9 %all-to-all-start.1 = ((bf16[16,4,2,16,256]{4,3,2,1,0:T(8,128)(2,1)}), bf16[16,4,2,16,256]{4,3,2,1,0:T(8,128)(2,1)S(1)}, u32[]{:S(2)}, u32[]{:S(2)}) async-start(bf16[16,4,2,16,256]{4,3,2,1,0:T(8,128)(2,1)} %bitcast.21), calls=%async_computation.1 | async-start | bytes 2097152 | tf_op jit(solution)/shard_map/all_to_all | solution.py:78
  454.2 6.9 %copy-start.3 = (bf16[64,2,16,256]{3,2,1,0:T(8,128)(2,1)}, bf16[64,2,16,256]{3,2,1,0:T(8,128)(2,1)S(1)}, u32[]{:S(2)}) copy-start(bf16[64,2,16,256]{3,2,1,0:T(8,128)(2,1)S(1)} %scatter_fusion) | copy-start | bytes 3145732
Sparse Core Ops, SparseCore 0:
  10.3 74.0 all-gather.5
  86.6 39.6 all-gather.7
  127.9 33.9 all-gather.9
  166.6 109.7 all-reduce.2
  277.9 51.2 all-gather.11
  330.7 45.8 all-gather.13
  387.9 118.1 all-reduce.4
where the time goes:
time: 516 us; the launch traced here: 515 us
  waiting for transfers between devices  389 us (75%)
  matrix products  47.9 us (9%)
  other arithmetic  29.7 us (6%)
  local copies, waits for them, and re-layouts  25.2 us (5%)
  between operations  14.4 us (3%)
  starting transfers between devices  8.88 us (2%)
    psum x1, waiting for transfers between devices, body(): lax.psum(attn_part.astype(jnp.bfloat16), 'tensor').astype(jnp.float32)  108 us
    all_gather x1, waiting for transfers between devices, body(): full_stream = lax.all_gather(stream, 'tensor', axis=0, tiled=True)  68.2 us
    all_to_all x1, waiting for transfers between devices, write_cache(): lax.all_to_all(outgoing, 'dp', split_axis=0, concat_axis=0, tiled=True)  45.7 us
    psum x1, waiting for transfers between devices, body(): lax.psum(mlp_part.astype(jnp.bfloat16), 'tensor').astype(jnp.float32)  45 us
    all_gather x1, waiting for transfers between devices, body(): lax.all_gather(w_gate_up, 'dp', axis=1, tiled=True)  44.9 us
    all_gather x1, waiting for transfers between devices, body(): lax.all_gather(w_qkv, 'dp', axis=1, tiled=True)  37.2 us
    all_gather x1, waiting for transfers between devices, body(): lax.all_gather(w_down, 'dp', axis=1, tiled=True)  32.8 us
    dot_general x2, matrix products, row_folder(): jnp.einsum('td,cdf->ctf', source, piece, preferred_element_type=jnp.float32)  21.9 us
  transfers between devices with their start and end apart: 9, of which 9 were waited for; matrix products, arithmetic and copies ran while one was open for 15% of the time, Pallas kernels for 0%

commit v1 on v0

--- a/solution.py
+++ b/solution.py
@@ -83,33 +83,57 @@
     return empty.at[local].set(arrived.reshape(pages, 2, page_size, width))
 
 
+def gather_packed(pieces, axis_name):
+    rows = [piece.shape[0] for piece in pieces]
+    packed = jnp.concatenate(pieces, axis=0)
+    gathered = lax.all_gather(packed, axis_name, axis=0, tiled=False)
+    outputs, first = [], 0
+    for count in rows:
+        outputs.append(gathered[:, first:first + count])
+        first += count
+    return outputs
+
+
 def body(stream, segment, position, w_qkv, w_out, w_gate_up, w_down, page_table):
     tok_group = segment.shape[0]
     share_rows = stream.shape[0]
+    owners = lax.axis_size("dp")
+    width = w_qkv.shape[1]
+    local_cols = w_qkv.shape[2]
+    hidden_cols = w_gate_up.shape[2]
+    qkv_g, out_g = gather_packed(
+        [w_qkv.reshape(3 * width, local_cols), jnp.transpose(w_out)], "dp"
+    )
+    qkv_g = qkv_g.reshape(owners, 3, width, local_cols)
+    gu_g, down_g = gather_packed(
+        [w_gate_up.reshape(2 * width, hidden_cols), jnp.transpose(w_down)], "dp"
+    )
+    gu_g = gu_g.reshape(owners, 2, width, hidden_cols)
     full_stream = lax.all_gather(stream, "tensor", axis=0, tiled=True)
-    normed = layer_norm(full_stream).astype(jnp.bfloat16)
-    local_heads = w_qkv.shape[2] // HD
-    projected = row_folder(normed, lax.all_gather(w_qkv, "dp", axis=1, tiled=True))
+    normed = layer_norm(full_stream).astype(jnp.bfloat16).reshape(tok_group, owners, width)
+    local_heads = local_cols // HD
+    projected = jnp.einsum("tgd,gcdf->ctf", normed, qkv_g, preferred_element_type=jnp.float32)
     query = rotate(projected[0].reshape(tok_group, local_heads, HD), position).astype(jnp.bfloat16)
     keys = rotate(projected[1].reshape(tok_group, local_heads, HD), position).astype(jnp.bfloat16)
     values = projected[2].reshape(tok_group, local_heads, HD).astype(jnp.bfloat16)
     context = attend(query, keys, values, segment)
-    attn_part = jnp.dot(
-        context, lax.all_gather(w_out, "dp", axis=1, tiled=True), preferred_element_type=jnp.float32
-    )
+    attn_part = jnp.einsum(
+        "tr,gcr->tgc", context, out_g, preferred_element_type=jnp.float32
+    ).reshape(tok_group, owners * width)
+    attn_part, gu_g, down_g = lax.optimization_barrier((attn_part, gu_g, down_g))
     attn_whole = lax.psum(attn_part.astype(jnp.bfloat16), "tensor").astype(jnp.float32)
     mid = (full_stream.astype(jnp.float32) + attn_whole).astype(jnp.bfloat16)
-    normed2 = layer_norm(mid).astype(jnp.bfloat16)
-    gate_up = row_folder(normed2, lax.all_gather(w_gate_up, "dp", axis=1, tiled=True))
+    normed2 = layer_norm(mid).astype(jnp.bfloat16).reshape(tok_group, owners, width)
+    gate_up = jnp.einsum("tgd,gcdf->ctf", normed2, gu_g, preferred_element_type=jnp.float32)
     hidden = (jax.nn.silu(gate_up[0]) * gate_up[1]).astype(jnp.bfloat16)
-    mlp_part = jnp.dot(
-        hidden, lax.all_gather(w_down, "dp", axis=1, tiled=True), preferred_element_type=jnp.float32
-    )
-    mlp_whole = lax.psum(mlp_part.astype(jnp.bfloat16), "tensor").astype(jnp.float32)
-    result = (mid.astype(jnp.float32) + mlp_whole).astype(jnp.bfloat16)
-    layer_out = lax.dynamic_slice_in_dim(
-        result, lax.axis_index("tensor") * share_rows, share_rows, 0
-    )
+    mlp_part = jnp.einsum(
+        "tf,gcf->tgc", hidden, down_g, preferred_element_type=jnp.float32
+    ).reshape(tok_group, owners * width)
+    mlp_mine = lax.psum_scatter(
+        mlp_part.astype(jnp.bfloat16), "tensor", scatter_dimension=0, tiled=True
+    ).astype(jnp.float32)
+    mid_mine = lax.dynamic_slice_in_dim(mid, lax.axis_index("tensor") * share_rows, share_rows, 0)
+    layer_out = (mid_mine.astype(jnp.float32) + mlp_mine).astype(jnp.bfloat16)
     kv_cache = write_cache(keys, values, page_table)
     return (layer_out, kv_cache)
 

time: 516 us -> 459 us (0.89); the launches traced: 515 us -> 452 us
  waiting for transfers between devices: 389 us -> 314 us
  local copies, waits for them, and re-layouts: 25.2 us -> 45.4 us
  matrix products: 47.9 us -> 40.8 us
    reduce_scatter x0 -> x1, waiting for transfers between devices: none -> 54.9 us  [body(): lax.psum_scatter(mlp_part.astype(jnp.bfloat16), 'tensor', scatter_dimensi...]
    all_gather x4 -> x2, waiting for transfers between devices: 117 us -> 62.5 us  [gather_packed(): gathered = lax.all_gather(packed, axis_name, axis=0, tiled=False)]
    psum x1 -> x0, waiting for transfers between devices: 45 us -> none  [body(): lax.psum(mlp_part.astype(jnp.bfloat16), 'tensor').astype(jnp.float32)]
    all_to_all x1, waiting for transfers between devices: 45.7 us -> 15.6 us  [write_cache(): lax.all_to_all(outgoing, 'dp', split_axis=0, concat_axis=0, tiled=True)]
    slice x0 -> x4, local copies, waits for them, and re-layouts: none -> 16.2 us  [gather_packed(): outputs.append(gathered[:, first:first + count])]
    dot_general x4, matrix products: 37.6 us -> 28.8 us  [the longest x1 12.2 us: body(): jnp.einsum('tgd,gcdf->ctf', normed2, gu_g, preferred_element_type=jnp.flo...]
    convert_element_type x2 -> x1, other arithmetic: 9.1 us -> 2.12 us  [body(): layer_out = (mid_mine.astype(jnp.float32) + mlp_mine).astype(jnp.bfloat16)]
    unnamed x25 -> x46, local copies, waits for them, and re-layouts: 14.4 us -> 17.1 us
  transfers between devices with their start and end apart: 9 -> 7, of which waited for: 9 -> 7; matrix products, arithmetic and copies ran while one was open for 15% -> 14% of each run, Pallas kernels for 0% -> 0%
where the time goes in v1:
time: 459 us; the launch traced here: 452 us
  waiting for transfers between devices  314 us (68%)
  local copies, waits for them, and re-layouts  45.4 us (10%)
  matrix products  40.8 us (9%)
  other arithmetic  28.5 us (6%)
  between operations  14.6 us (3%)
  starting transfers between devices  9.46 us (2%)
    psum x1, waiting for transfers between devices, body(): lax.psum(attn_part.astype(jnp.bfloat16), 'tensor').astype(jnp.float32)  110 us
    all_gather x1, waiting for transfers between devices, body(): full_stream = lax.all_gather(stream, 'tensor', axis=0, tiled=True)  66.9 us
    all_gather x2, waiting for transfers between devices, gather_packed(): gathered = lax.all_gather(packed, axis_name, axis=0, tiled=False)  62.5 us
    reduce_scatter x1, waiting for transfers between devices, body(): lax.psum_scatter(mlp_part.astype(jnp.bfloat16), 'tensor', scatter_dimensi...  54.9 us
    unnamed x46, local copies, waits for them, and re-layouts  17.1 us
    slice x4, local copies, waits for them, and re-layouts, gather_packed(): outputs.append(gathered[:, first:first + count])  16.2 us
    all_to_all x1, waiting for transfers between devices, write_cache(): lax.all_to_all(outgoing, 'dp', split_axis=0, concat_axis=0, tiled=True)  15.6 us
    dot_general x1, matrix products, body(): jnp.einsum('tgd,gcdf->ctf', normed2, gu_g, preferred_element_type=jnp.flo...  12.2 us
  transfers between devices with their start and end apart: 7, of which 7 were waited for; matrix products, arithmetic and copies ran while one was open for 14% of the time, Pallas kernels for 0%

profile of v1, /device:TPU:1, one launch (start us, length us, event | category | flops | bytes accessed | tf_op | source)
XLA Modules:
  0.0 452.4 jit_solution(6801956161445747458)
XLA Ops:
  7.2 0.7 all-gather.6.cloned.1.call-update
  8.0 0.9 copy.35
  8.9 1.6 pad_maximum_fusion.3
  10.6 1.1 copy.43
  11.7 2.0 pad_maximum_fusion
  13.9 0.3 compare_and_fusion
  14.2 1.4 fusion.34
  15.6 1.9 multiply_cosine_fusion
  17.5 66.9 %all-gather.6.cloned.1.call-done = bf16[1024,2048]{1,0:T(8,128)(2,1)} async-done(((bf16[128,2048]{1,0:T(8,128)(2,1)}), bf16[1024,2048]{1,0:T(8,128)(2,1)}) %all-gather.6.cloned.1.call-update) | async-done | bytes 4194320 | tf_op jit(solution)/shard_map/all_gather | solution.py:112
  84.5 3.0 convert_reduce_fusion
  87.4 0.5 copy-done.1
  87.9 1.2 fusion.6
  89.1 1.6 fusion.12
  90.8 3.3 copy.64
  94.1 28.7 %all-gather.8.cloned.1.call-done = bf16[8192,256]{1,0:T(8,128)(2,1)} async-done(((bf16[512,256]{1,0:T(8,128)(2,1)}), bf16[8192,256]{1,0:T(8,128)(2,1)}) %all-gather.8.cloned.1.call-update) | async-done | bytes 4194320 | tf_op jit(solution)/shard_map/all_gather | solution.py:89
  122.8 2.3 slice.94
  125.1 1.3 slice.106
  126.4 3.5 fusion.37
  129.9 0.9 slice.132
  130.7 0.2 fusion.78
  131.0 1.0 fusion.79
  132.0 2.4 copy.62
  134.4 2.4 copy.63
  136.8 1.0 fusion.80
  137.8 1.4 copy.60
  139.2 2.4 copy.61
  141.6 2.0 multiply_subtract_fusion
  143.6 0.3 maximum_convert_fusion
  143.9 0.3 subtract_convert_fusion
  144.2 0.5 copy-done.8
  144.7 0.5 fusion.58
  145.3 1.3 copy-done.10
  146.6 1.1 fusion.83
  147.7 3.6 fusion.47
  151.4 5.2 %fusion.82 = (f32[2,512]{1,0:T(2,128)S(1)}, bf16[2,512,1024]{2,1,0:T(8,128)(2,1)}) fusion(pred[512,1024]{1,0:T(8,128)(4,1)} %fusion.34, bf16[1024,2,128]{2,0,1:T(8,128)(2,1)S(1)} %copy-done.9, bf16[1024,2,64]{2,0,1:T(8,128)(2,1)S(1)} %copy-done.14, bf16[1024,2,64]{2,0,1:T(8,128)(2,1)S(1)} %copy-done.12), kind=kOutput, calls=%fused_computation.104 | convolution fusion | flops 545260544 | bytes 3674112 | tf_op jit(solution)/shard_map/sub | solution.py:53
  156.6 2.7 fusion.48
  159.4 3.3 fusion.84
  162.6 33.8 %all-gather.10.cloned.1.call-done = bf16[6144,1024]{1,0:T(8,128)(2,1)} async-done(((bf16[384,1024]{1,0:T(8,128)(2,1)}), bf16[6144,1024]{1,0:T(8,128)(2,1)}) %all-gather.10.cloned.1.call-update) | async-done | bytes 12582928 | tf_op jit(solution)/shard_map/all_gather | solution.py:89
  196.4 7.9 %slice.107 = bf16[16,256,1024]{2,1,0:T(8,128)(2,1)} slice(bf16[16,384,1024]{2,1,0:T(8,128)(2,1)} %bitcast.71), slice={[0:16], [0:256], [0:1024]} | slice | bytes 16777216 | tf_op jit(solution)/shard_map/slice | solution.py:92
  204.3 4.8 %slice.108 = bf16[16,128,1024]{2,1,0:T(8,128)(2,1)} slice(bf16[16,384,1024]{2,1,0:T(8,128)(2,1)} %bitcast.72), slice={[0:16], [256:384], [0:1024]} | slice | bytes 8388608 | tf_op jit(solution)/shard_map/slice | solution.py:92
  209.2 110.2 %all-reduce.2.cloned.1.call-done = bf16[1024,2048]{1,0:T(8,128)(2,1)} async-done(((bf16[1024,2048]{1,0:T(8,128)(2,1)}), bf16[1024,2048]{1,0:T(8,128)(2,1)}) %all-reduce.2.cloned.1.call-update) | async-done | bytes 4194320 | tf_op jit(solution)/shard_map/psum | solution.py:124
  319.4 4.8 %convert_reduce_fusion.1 = (f32[1024]{0:T(1024)S(1)}, bf16[1024,2048]{1,0:T(8,128)(2,1)S(1)}) fusion(bf16[1024,2048]{1,0:T(8,128)(2,1)} %all-reduce.2.cloned.1.call-done, bf16[1024,2048]{1,0:T(8,128)(2,1)} %all-gather.6.cloned.1.call-done), kind=kLoop, calls=%fused_computation.9 | loop fusion | flops 12581888 | bytes 12587008 | tf_op jit(solution)/shard_map/reduce_sum | solution.py:13
  324.2 1.2 fusion.8
  325.4 1.5 fusion.11
  326.9 1.4 copy.65
  328.3 0.8 slice-done.1
  329.1 12.2 %fusion.22 = f32[2,1024,1024]{1,2,0:T(8,128)} fusion(bf16[16,2,128,1024]{3,2,1,0:T(8,128)(2,1)S(1)} %bitcast.75, bf16[1024,16,128,1]{2,1,0,3:T(8,128)(2,1)S(1)} %bitcast.81), kind=kOutput, calls=%fused_computation.32 | convolution fusion | flops 8589934592 | bytes 20971520 | tf_op jit(solution)/shard_map/tgd,gcdf->ctf/dot_general | solution.py:127
  341.3 9.9 %convolution_convert_fusion = bf16[1024,2048]{1,0:T(8,128)(2,1)} fusion(bf16[2048,1024]{1,0:T(8,128)(2,1)S(1)} %bitcast.79, f32[2,1024,1024]{1,2,0:T(8,128)} %fusion.22), kind=kOutput, calls=%fused_computation.30 | convolution fusion | flops 4303355904 | bytes 16777216 | tf_op jit(solution)/shard_map/tf,gcf->tgc/dot_general | solution.py:129
  351.2 0.6 copy-done
  351.9 2.0 sort.17
  353.9 0.8 gather_fusion
  354.7 0.7 all_to_all.9
  355.4 5.2 %all-to-all-start = ((s32[16,1,4]{2,1,0:T(1,128)}), s32[16,1,4]{2,1,0:T(1,128)S(1)}, u32[]{:S(2)}, u32[]{:S(2)}) async-start(s32[16,1,4]{2,1,0:T(1,128)} %bitcast.28), calls=%async_computation.1 | async-start | bytes 16384 | tf_op jit(solution)/shard_map/all_to_all | solution.py:79
  360.6 0.5 copy.47
  361.2 0.2 copy.48
  361.4 0.3 convert_element_type.99
  361.8 1.6 gather_fusion.1
  363.4 2.8 all-to-all-done
  366.1 4.0 all-to-all-start.1
  370.3 15.6 %all-to-all-done.1 = bf16[16,4,2,16,256]{4,3,2,1,0:T(8,128)(2,1)S(1)} async-done(((bf16[16,4,2,16,256]{4,3,2,1,0:T(8,128)(2,1)}), bf16[16,4,2,16,256]{4,3,2,1,0:T(8,128)(2,1)S(1)}, u32[]{:S(2)}, u32[]{:S(2)}) %all-to-all-start.1) | async-done | bytes 1048608 | tf_op jit(solution)/shard_map/all_to_all | solution.py:78
  385.8 0.1 broadcast_in_dim.40
  386.0 2.5 scatter_fusion
  388.5 54.9 %reduce-scatter.2.cloned.1.call-done = bf16[128,2048]{1,0:T(8,128)(2,1)} async-done(((bf16[1024,2048]{1,0:T(8,128)(2,1)}), bf16[128,2048]{1,0:T(8,128)(2,1)}) %reduce-scatter.2.cloned.1.call-update) | async-done | bytes 524304 | tf_op jit(solution)/shard_map/reduce_scatter | solution.py:132
  443.4 2.1 add_convert_fusion
  (67 shorter events, 0.7 us)
Async XLA Ops:
  7.2 6.7 %copy-start.17 = (s32[1024]{0:T(1024)S(1)}, s32[1024]{0:T(1024)}, u32[]{:S(2)}) copy-start(s32[1024]{0:T(1024)} %param.10) | copy-start | bytes 12292
  7.2 6.7 %copy-start.16 = (s32[1024]{0:T(1024)S(1)}, s32[1024]{0:T(1024)}, u32[]{:S(2)}) copy-start(s32[1024]{0:T(1024)} %param.9) | copy-start | bytes 12292
  7.2 77.3 %all-gather.6.cloned.1.call-start = ((), (), s32[]{:S(2)}) async-start(), calls=%async_computation.3 | async-start | bytes 4718592 | tf_op jit(solution)/shard_map/all_gather | solution.py:112
  7.9 114.9 %all-gather.8.cloned.1.call-start = ((), (), s32[]{:S(2)}) async-start(), calls=%async_computation.6 | async-start | bytes 4456448 | tf_op jit(solution)/shard_map/all_gather | solution.py:89
  10.6 185.8 %all-gather.10.cloned.1.call-start = ((), (), s32[]{:S(2)}) async-start(), calls=%async_computation.7 | async-start | bytes 13369344 | tf_op jit(solution)/shard_map/all_gather | solution.py:89
  13.8 305.6 %all-reduce.2.cloned.1.call-start = ((), (), s32[]{:S(2)}) async-start(), calls=%async_computation.4 | async-start | bytes 8388608 | tf_op jit(solution)/shard_map/psum | solution.py:124
  14.2 131.0 %copy-start.15 = (pred[512,512]{0,1:T(8,128)(4,1)}, pred[512,512]{0,1:T(8,128)(4,1)S(1)}, u32[]{:S(2)}) copy-start(pred[512,512]{0,1:T(8,128)(4,1)S(1)} %compare_and_fusion) | copy-start | bytes 786436
  84.4 3.4 copy-start.1
  122.8 3.6 copy-start.4
  141.6 2.3 copy-start.6
  143.9 0.8 copy-start.8
  144.2 3.4 copy-start.11
  144.2 3.4 copy-start.13
  144.7 3.0 slice-start.2
  145.2 1.3 copy-start.10
  146.6 4.8 %copy-start.9 = (bf16[1024,2,128]{2,0,1:T(8,128)(2,1)S(1)}, bf16[1024,2,128]{2,0,1:T(8,128)(2,1)}, u32[]{:S(2)}) copy-start(bf16[1024,2,128]{2,0,1:T(8,128)(2,1)} %copy-done.8) | copy-start | bytes 1572868
  147.7 3.7 copy-start.12
  147.7 3.7 copy-start.14
  151.4 5.2 %copy-start.7 = (bf16[1,1024,256]{1,2,0:T(8,128)(2,1)S(1)}, bf16[1,1024,256]{1,2,0:T(8,128)(2,1)}, u32[]{:S(2)}) copy-start(bf16[1,1024,256]{1,2,0:T(8,128)(2,1)} %slice.132) | copy-start | bytes 1572868
  209.1 234.2 %reduce-scatter.2.cloned.1.call-start = ((), (), s32[]{:S(2)}) async-start(), calls=%async_computation.5 | async-start | bytes 4718592 | tf_op jit(solution)/shard_map/reduce_scatter | solution.py:132
  324.2 2.8 copy-start.2
  324.2 4.2 slice-start
  325.4 3.7 slice-start.1
  329.1 12.2 %copy-start.3 = (bf16[16,128,1024]{2,1,0:T(8,128)(2,1)S(1)}, bf16[16,128,1024]{2,1,0:T(8,128)(2,1)}, u32[]{:S(2)}) copy-start(bf16[16,128,1024]{2,1,0:T(8,128)(2,1)} %slice.108) | copy-start | bytes 12582916
  351.2 0.7 copy-start
  355.4 10.8 %all-to-all-start = ((s32[16,1,4]{2,1,0:T(1,128)}), s32[16,1,4]{2,1,0:T(1,128)S(1)}, u32[]{:S(2)}, u32[]{:S(2)}) async-start(s32[16,1,4]{2,1,0:T(1,128)} %bitcast.28), calls=%async_computation.1 | async-start | bytes 16384 | tf_op jit(solution)/shard_map/all_to_all | solution.py:79
  366.1 19.7 %all-to-all-start.1 = ((bf16[16,4,2,16,256]{4,3,2,1,0:T(8,128)(2,1)}), bf16[16,4,2,16,256]{4,3,2,1,0:T(8,128)(2,1)S(1)}, u32[]{:S(2)}, u32[]{:S(2)}) async-start(bf16[16,4,2,16,256]{4,3,2,1,0:T(8,128)(2,1)} %bitcast.34), calls=%async_computation.2 | async-start | bytes 2097152 | tf_op jit(solution)/shard_map/all_to_all | solution.py:78
  388.5 57.0 %copy-start.5 = (bf16[64,2,16,256]{3,2,1,0:T(8,128)(2,1)}, bf16[64,2,16,256]{3,2,1,0:T(8,128)(2,1)S(1)}, u32[]{:S(2)}) copy-start(bf16[64,2,16,256]{3,2,1,0:T(8,128)(2,1)S(1)} %scatter_fusion) | copy-start | bytes 3145732
Sparse Core Ops, SparseCore 0:
  10.3 74.0 all-gather.5
  86.7 36.0 all-gather.7
  124.5 71.8 all-gather.9
  209.2 110.1 all-reduce.1
  351.3 91.9 reduce-scatter.1

commit v2 on v1

--- a/solution.py
+++ b/solution.py
@@ -94,9 +94,23 @@
     return outputs
 
 
+def gather_rows(rows, axis_name):
+    count = lax.axis_size(axis_name)
+    copies = jnp.broadcast_to(rows[None], (count,) + rows.shape)
+    gathered = lax.all_to_all(copies, axis_name, 0, 0, tiled=True)
+    return gathered.reshape(count * rows.shape[0], rows.shape[1])
+
+
+def sum_rows(terms, axis_name):
+    count = lax.axis_size(axis_name)
+    arrived = lax.all_to_all(
+        terms.reshape(count, terms.shape[0] // count, terms.shape[1]), axis_name, 0, 0, tiled=True
+    )
+    return jnp.sum(arrived.astype(jnp.float32), axis=0)
+
+
 def body(stream, segment, position, w_qkv, w_out, w_gate_up, w_down, page_table):
     tok_group = segment.shape[0]
-    share_rows = stream.shape[0]
     owners = lax.axis_size("dp")
     width = w_qkv.shape[1]
     local_cols = w_qkv.shape[2]
@@ -109,7 +123,7 @@
         [w_gate_up.reshape(2 * width, hidden_cols), jnp.transpose(w_down)], "dp"
     )
     gu_g = gu_g.reshape(owners, 2, width, hidden_cols)
-    full_stream = lax.all_gather(stream, "tensor", axis=0, tiled=True)
+    full_stream = gather_rows(stream, "tensor")
     normed = layer_norm(full_stream).astype(jnp.bfloat16).reshape(tok_group, owners, width)
     local_heads = local_cols // HD
     projected = jnp.einsum("tgd,gcdf->ctf", normed, qkv_g, preferred_element_type=jnp.float32)
@@ -120,20 +134,17 @@
     attn_part = jnp.einsum(
         "tr,gcr->tgc", context, out_g, preferred_element_type=jnp.float32
     ).reshape(tok_group, owners * width)
-    attn_part, gu_g, down_g = lax.optimization_barrier((attn_part, gu_g, down_g))
-    attn_whole = lax.psum(attn_part.astype(jnp.bfloat16), "tensor").astype(jnp.float32)
-    mid = (full_stream.astype(jnp.float32) + attn_whole).astype(jnp.bfloat16)
-    normed2 = layer_norm(mid).astype(jnp.bfloat16).reshape(tok_group, owners, width)
+    attn_mine = sum_rows(attn_part.astype(jnp.bfloat16), "tensor")
+    mid = (stream.astype(jnp.float32) + attn_mine).astype(jnp.bfloat16)
+    normed2_mine = layer_norm(mid).astype(jnp.bfloat16)
+    normed2 = gather_rows(normed2_mine, "tensor").reshape(tok_group, owners, width)
     gate_up = jnp.einsum("tgd,gcdf->ctf", normed2, gu_g, preferred_element_type=jnp.float32)
     hidden = (jax.nn.silu(gate_up[0]) * gate_up[1]).astype(jnp.bfloat16)
     mlp_part = jnp.einsum(
         "tf,gcf->tgc", hidden, down_g, preferred_element_type=jnp.float32
     ).reshape(tok_group, owners * width)
-    mlp_mine = lax.psum_scatter(
-        mlp_part.astype(jnp.bfloat16), "tensor", scatter_dimension=0, tiled=True
-    ).astype(jnp.float32)
-    mid_mine = lax.dynamic_slice_in_dim(mid, lax.axis_index("tensor") * share_rows, share_rows, 0)
-    layer_out = (mid_mine.astype(jnp.float32) + mlp_mine).astype(jnp.bfloat16)
+    mlp_mine = sum_rows(mlp_part.astype(jnp.bfloat16), "tensor")
+    layer_out = (mid.astype(jnp.float32) + mlp_mine).astype(jnp.bfloat16)
     kv_cache = write_cache(keys, values, page_table)
     return (layer_out, kv_cache)
 

time: 459 us -> 417 us (0.908)
  the two profiles are of different devices: /device:TPU:1 before, /device:TPU:38 now
where the time goes in v2:
time: 417 us; the launch traced here: 410 us
  waiting for transfers between devices  170 us (41%)
  blocking collectives  65.2 us (16%)
  local copies, waits for them, and re-layouts  55.7 us (13%)
  matrix products  43.2 us (10%)
  starting transfers between devices  31.6 us (8%)
  other arithmetic  30 us (7%)
  between operations  14.9 us (4%)
    all_to_all x2, waiting for transfers between devices, gather_rows(): gathered = lax.all_to_all(copies, axis_name, 0, 0, tiled=True)  107 us
    all_to_all x1, blocking collectives, sum_rows(): lax.all_to_all(terms.reshape(count, terms.shape[0] // count, terms.shape[...  65.2 us
    all_to_all x1, waiting for transfers between devices, sum_rows(): lax.all_to_all(terms.reshape(count, terms.shape[0] // count, terms.shape[...  59.6 us
    unnamed x42, local copies, waits for them, and re-layouts  20.7 us
    slice x4, local copies, waits for them, and re-layouts, gather_packed(): outputs.append(gathered[:, first:first + count])  17 us
    dot_general x1, matrix products, body(): jnp.einsum('tgd,gcdf->ctf', normed2, gu_g, preferred_element_type=jnp.flo...  14.6 us
    all_to_all x2, starting transfers between devices, gather_rows(): gathered = lax.all_to_all(copies, axis_name, 0, 0, tiled=True)  13.5 us
    dot_general x1, matrix products, body(): jnp.einsum('tf,gcf->tgc', hidden, down_g, preferred_element_type=jnp.floa...  11.2 us
  transfers between devices with their start and end apart: 7, of which 4 were waited for; matrix products, arithmetic and copies ran while one was open for 29% of the time, Pallas kernels for 0%

profile of v2, /device:TPU:38, one launch (start us, length us, event | category | flops | bytes accessed | tf_op | source)
XLA Modules:
  0.0 410.4 jit_solution(2369631074379633333)
XLA Ops:
  7.2 0.9 copy.33
  8.2 1.6 pad_maximum_fusion.3
  9.9 1.1 copy.41
  11.0 2.0 pad_maximum_fusion
  13.0 3.5 broadcast_in_dim.36
  16.6 7.3 %all-to-all-start = ((bf16[8,128,2048]{2,1,0:T(8,128)(2,1)}), bf16[8,128,2048]{2,1,0:T(8,128)(2,1)}, u32[]{:S(2)}, u32[]{:S(2)}) async-start(bf16[8,128,2048]{2,1,0:T(8,128)(2,1)} %broadcast_in_dim.36), calls=%async_computation | async-start | bytes 8388608 | tf_op jit(solution)/shard_map/all_to_all | solution.py:100
  24.0 0.3 compare_and_fusion
  24.3 1.4 fusion.25
  25.7 1.9 multiply_cosine_fusion
  27.5 57.7 %all-to-all-done = bf16[8,128,2048]{2,1,0:T(8,128)(2,1)} async-done(((bf16[8,128,2048]{2,1,0:T(8,128)(2,1)}), bf16[8,128,2048]{2,1,0:T(8,128)(2,1)}, u32[]{:S(2)}, u32[]{:S(2)}) %all-to-all-start) | async-done | bytes 4194336 | tf_op jit(solution)/shard_map/all_to_all | solution.py:100
  85.2 3.6 copy.62
  88.8 2.8 convert_reduce_fusion.2
  91.7 3.4 multiply_reduce_fusion
  95.1 5.2 %fusion.3 = bf16[1024,16,128]{2,1,0:T(8,128)(2,1)} fusion(f32[128,8,16,128]{3,2,1,0:T(8,128)S(1)} %copy.62, f32[1024]{0:T(1024)S(1)} %rsqrt_bitcast_fusion, f32[1024]{0:T(1024)S(1)} %get-tuple-element.20), kind=kLoop, calls=%fused_computation.7 | loop fusion | flops 6291456 | bytes 12591104 | tf_op jit(solution)/shard_map/convert_element_type | solution.py:127
  100.4 1.4 slice.106
  101.8 2.7 slice.94
  104.6 3.5 fusion.28
  108.1 0.8 copy-done.4
  108.9 0.7 slice.96
  109.6 0.2 fusion.74
  109.9 1.1 fusion.75
  110.9 2.4 copy.61
  113.3 1.0 fusion.76
  114.3 1.4 copy.59
  115.7 2.4 copy.60
  118.2 2.4 copy.58
  120.6 1.9 multiply_subtract_fusion
  122.5 0.3 maximum_convert_fusion
  122.8 0.3 subtract_convert_fusion
  123.1 0.5 copy-done.6
  123.6 0.5 fusion.54
  124.1 1.4 copy-done.9
  125.5 1.1 fusion.79
  126.6 4.2 %fusion.40 = bf16[512,2,128]{0,2,1:T(8,128)(2,1)} fusion(bf16[512,2,128]{0,2,1:T(8,128)(2,1)S(1)} %bitcast.104, f32[512,2]{0,1:T(2,128)S(1)} %bitcast.108, f32[2,512,512]{1,2,0:T(8,128)} %copy-done.9, pred[512,512]{0,1:T(8,128)(4,1)S(1)} %compare_and_fusion), kind=kOutput, calls=%fused_computation.47 | convolution fusion | flops 137627136 | bytes 2887680 | tf_op jit(solution)/shard_map/hqk,khd->qhd/dot_general | solution.py:55
  130.8 5.2 %fusion.78 = (f32[2,512]{1,0:T(2,128)S(1)}, bf16[2,512,1024]{2,1,0:T(8,128)(2,1)}) fusion(pred[512,1024]{1,0:T(8,128)(4,1)} %fusion.25, bf16[1024,2,128]{2,0,1:T(8,128)(2,1)S(1)} %copy-done.7, bf16[1024,2,64]{2,0,1:T(8,128)(2,1)S(1)} %copy-done.13, bf16[1024,2,64]{2,0,1:T(8,128)(2,1)S(1)} %copy-done.11), kind=kOutput, calls=%fused_computation.105 | convolution fusion | flops 545260544 | bytes 3674112 | tf_op jit(solution)/shard_map/sub | solution.py:53
  136.0 2.5 fusion.41
  138.6 1.6 convolution_convert_fusion
  140.1 65.2 %all_to_all.34 = bf16[8,128,2048]{2,1,0:T(8,128)(2,1)S(1)} all-to-all(bf16[8,128,2048]{2,1,0:T(8,128)(2,1)S(1)} %bitcast.83), channel_id=1, replica_groups=mesh['dp'=16,'tensor'=8] {'tensor'}, dimensions={0} | all-to-all | bytes 8388608 | tf_op jit(solution)/shard_map/all_to_all | solution.py:106
  205.3 0.7 convert_reduce_fusion.1
  206.0 0.3 copy-done.8
  206.6 0.3 fusion.44
  206.9 0.3 fusion.45
  207.2 2.5 broadcast_in_dim.45
  209.7 6.2 %all-to-all-start.2 = ((bf16[8,128,2048]{2,1,0:T(8,128)(2,1)}), bf16[8,128,2048]{2,1,0:T(8,128)(2,1)}, u32[]{:S(2)}, u32[]{:S(2)}) async-start(bf16[8,128,2048]{2,1,0:T(8,128)(2,1)} %broadcast_in_dim.45), calls=%async_computation.2 | async-start | bytes 8388608 | tf_op jit(solution)/shard_map/all_to_all | solution.py:100
  215.9 2.0 sort.17
  217.9 0.8 gather_fusion
  218.7 0.7 all_to_all.25
  219.6 0.5 copy.45
  220.2 0.3 convert_element_type.110
  220.6 1.6 gather_fusion.1
  222.2 48.8 %all-to-all-done.2 = bf16[8,128,2048]{2,1,0:T(8,128)(2,1)} async-done(((bf16[8,128,2048]{2,1,0:T(8,128)(2,1)}), bf16[8,128,2048]{2,1,0:T(8,128)(2,1)}, u32[]{:S(2)}, u32[]{:S(2)}) %all-to-all-start.2) | async-done | bytes 4194336 | tf_op jit(solution)/shard_map/all_to_all | solution.py:100
  271.0 5.3 %all-to-all-start.4 = ((s32[16,1,4]{2,1,0:T(1,128)}), s32[16,1,4]{2,1,0:T(1,128)S(1)}, u32[]{:S(2)}, u32[]{:S(2)}) async-start(s32[16,1,4]{2,1,0:T(1,128)} %bitcast.32), calls=%async_computation.4 | async-start | bytes 16384 | tf_op jit(solution)/shard_map/all_to_all | solution.py:79
  276.4 5.5 %copy.63 = bf16[128,8,16,128]{3,2,1,0:T(8,128)(2,1)} copy(bf16[128,8,16,128]{3,1,2,0:T(8,128)(2,1)} %bitcast.45) | data formatting | bytes 8388608
  281.9 8.0 %slice.107 = bf16[16,256,1024]{2,1,0:T(8,128)(2,1)} slice(bf16[16,384,1024]{2,1,0:T(8,128)(2,1)} %bitcast.84), slice={[0:16], [0:256], [0:1024]} | slice | bytes 16777216 | tf_op jit(solution)/shard_map/slice | solution.py:92
  289.9 14.6 %fusion.13 = f32[2,1024,1024]{1,2,0:T(8,128)} fusion(bf16[16,2,128,1024]{3,2,1,0:T(8,128)(2,1)} %bitcast.86, bf16[1024,16,128,1]{2,1,0,3:T(8,128)(2,1)} %bitcast.92), kind=kOutput, calls=%fused_computation.24 | convolution fusion | flops 8589934592 | bytes 20971520 | tf_op jit(solution)/shard_map/tgd,gcdf->ctf/dot_general | solution.py:141
  304.5 4.8 %slice.110 = bf16[16,128,1024]{2,1,0:T(8,128)(2,1)} slice(bf16[16,384,1024]{2,1,0:T(8,128)(2,1)} %bitcast.85), slice={[0:16], [256:384], [0:1024]} | slice | bytes 8388608 | tf_op jit(solution)/shard_map/slice | solution.py:92
  309.3 6.1 %all-to-all-start.5 = ((bf16[16,4,2,16,256]{4,3,2,1,0:T(8,128)(2,1)}), bf16[16,4,2,16,256]{4,3,2,1,0:T(8,128)(2,1)S(1)}, u32[]{:S(2)}, u32[]{:S(2)}) async-start(bf16[16,4,2,16,256]{4,3,2,1,0:T(8,128)(2,1)} %bitcast.38), calls=%async_computation.5 | async-start | bytes 2097152 | tf_op jit(solution)/shard_map/all_to_all | solution.py:78
  315.4 11.2 %convolution_convert_fusion.1 = bf16[1024,2048]{1,0:T(8,128)(2,1)} fusion(bf16[2048,1024]{1,0:T(8,128)(2,1)} %bitcast.91, f32[2,1024,1024]{1,2,0:T(8,128)} %fusion.13), kind=kOutput, calls=%fused_computation.22 | convolution fusion | flops 4303355904 | bytes 16777216 | tf_op jit(solution)/shard_map/tf,gcf->tgc/dot_general | solution.py:143
  326.6 3.5 all-to-all-done.5
  330.1 6.6 %all-to-all-start.3 = ((bf16[8,128,2048]{2,1,0:T(8,128)(2,1)}), bf16[8,128,2048]{2,1,0:T(8,128)(2,1)}, u32[]{:S(2)}, u32[]{:S(2)}) async-start(bf16[8,128,2048]{2,1,0:T(8,128)(2,1)} %bitcast.90), calls=%async_computation.3 | async-start | bytes 8388608 | tf_op jit(solution)/shard_map/all_to_all | solution.py:106
  337.0 2.5 scatter_fusion
  339.6 59.6 %all-to-all-done.3 = bf16[8,128,2048]{2,1,0:T(8,128)(2,1)} async-done(((bf16[8,128,2048]{2,1,0:T(8,128)(2,1)}), bf16[8,128,2048]{2,1,0:T(8,128)(2,1)}, u32[]{:S(2)}, u32[]{:S(2)}) %all-to-all-start.3) | async-done | bytes 4194336 | tf_op jit(solution)/shard_map/all_to_all | solution.py:106
  399.2 3.0 convert_reduce_fusion
  402.2 0.9 fusion.46
  (63 shorter events, 1.1 us)
Async XLA Ops:
  7.2 93.2 %all-gather.5.cloned.1.call-start = ((), (), s32[]{:S(2)}) async-start(), calls=%async_computation.6 | async-start | bytes 4456448 | tf_op jit(solution)/shard_map/all_gather | solution.py:89
  9.8 272.1 %all-gather.7.cloned.1.call-start = ((), (), s32[]{:S(2)}) async-start(), calls=%async_computation.7 | async-start | bytes 13369344 | tf_op jit(solution)/shard_map/all_gather | solution.py:89
  16.6 7.3 %copy-start.17 = (s32[1024]{0:T(1024)S(1)}, s32[1024]{0:T(1024)}, u32[]{:S(2)}) copy-start(s32[1024]{0:T(1024)} %param.10) | copy-start | bytes 12292
  16.6 7.4 %copy-start.16 = (s32[1024]{0:T(1024)S(1)}, s32[1024]{0:T(1024)}, u32[]{:S(2)}) copy-start(s32[1024]{0:T(1024)} %param.9) | copy-start | bytes 12292
  16.6 68.7 %all-to-all-start = ((bf16[8,128,2048]{2,1,0:T(8,128)(2,1)}), bf16[8,128,2048]{2,1,0:T(8,128)(2,1)}, u32[]{:S(2)}, u32[]{:S(2)}) async-start(bf16[8,128,2048]{2,1,0:T(8,128)(2,1)} %broadcast_in_dim.36), calls=%async_computation | async-start | bytes 8388608 | tf_op jit(solution)/shard_map/all_to_all | solution.py:100
  100.3 4.2 %copy-start.3 = (bf16[1024,16,128]{2,1,0:T(8,128)(2,1)S(1)}, bf16[1024,16,128]{2,1,0:T(8,128)(2,1)}, u32[]{:S(2)}) copy-start(bf16[1024,16,128]{2,1,0:T(8,128)(2,1)} %fusion.3) | copy-start | bytes 12582916
  108.1 0.8 copy-start.4
  120.6 2.2 copy-start.2
  122.8 0.8 copy-start.6
  123.1 3.5 copy-start.10
  123.1 3.5 copy-start.12
  123.6 3.0 copy-start.14
  124.1 1.4 copy-start.9
  125.5 5.3 %copy-start.7 = (bf16[1024,2,128]{2,0,1:T(8,128)(2,1)S(1)}, bf16[1024,2,128]{2,0,1:T(8,128)(2,1)}, u32[]{:S(2)}) copy-start(bf16[1024,2,128]{2,0,1:T(8,128)(2,1)} %copy-done.6) | copy-start | bytes 1572868
  126.6 4.2 %copy-start.11 = (bf16[1024,2,64]{2,0,1:T(8,128)(2,1)S(1)}, bf16[1024,2,64]{2,0,1:T(8,128)(2,1)}, u32[]{:S(2)}) copy-start(bf16[1024,2,64]{2,0,1:T(8,128)(2,1)} %copy-done.10) | copy-start | bytes 786436
  126.6 4.2 %copy-start.13 = (bf16[1024,2,64]{2,0,1:T(8,128)(2,1)S(1)}, bf16[1024,2,64]{2,0,1:T(8,128)(2,1)}, u32[]{:S(2)}) copy-start(bf16[1024,2,64]{2,0,1:T(8,128)(2,1)} %copy-done.12) | copy-start | bytes 786436
  130.8 5.2 %copy-start.5 = (bf16[1,1024,256]{1,2,0:T(8,128)(2,1)S(1)}, bf16[1,1024,256]{1,2,0:T(8,128)(2,1)}, u32[]{:S(2)}) copy-start(bf16[1,1024,256]{1,2,0:T(8,128)(2,1)} %copy-done.4) | copy-start | bytes 1572868
  136.0 2.5 copy-start.15
  205.3 1.0 copy-start.8
  209.7 6.2 %copy-start = (s32[64]{0:T(128)S(1)}, s32[64]{0:T(128)}, u32[]{:S(2)}) copy-start(s32[64]{0:T(128)} %param.15) | copy-start | bytes 772
  209.7 61.4 %all-to-all-start.2 = ((bf16[8,128,2048]{2,1,0:T(8,128)(2,1)}), bf16[8,128,2048]{2,1,0:T(8,128)(2,1)}, u32[]{:S(2)}, u32[]{:S(2)}) async-start(bf16[8,128,2048]{2,1,0:T(8,128)(2,1)} %broadcast_in_dim.45), calls=%async_computation.2 | async-start | bytes 8388608 | tf_op jit(solution)/shard_map/all_to_all | solution.py:100
  271.0 38.3 %all-to-all-start.4 = ((s32[16,1,4]{2,1,0:T(1,128)}), s32[16,1,4]{2,1,0:T(1,128)S(1)}, u32[]{:S(2)}, u32[]{:S(2)}) async-start(s32[16,1,4]{2,1,0:T(1,128)} %bitcast.32), calls=%async_computation.4 | async-start | bytes 16384 | tf_op jit(solution)/shard_map/all_to_all | solution.py:79
  309.3 20.8 %all-to-all-start.5 = ((bf16[16,4,2,16,256]{4,3,2,1,0:T(8,128)(2,1)}), bf16[16,4,2,16,256]{4,3,2,1,0:T(8,128)(2,1)S(1)}, u32[]{:S(2)}, u32[]{:S(2)}) async-start(bf16[16,4,2,16,256]{4,3,2,1,0:T(8,128)(2,1)} %bitcast.38), calls=%async_computation.5 | async-start | bytes 2097152 | tf_op jit(solution)/shard_map/all_to_all | solution.py:78
  330.1 69.0 %all-to-all-start.3 = ((bf16[8,128,2048]{2,1,0:T(8,128)(2,1)}), bf16[8,128,2048]{2,1,0:T(8,128)(2,1)}, u32[]{:S(2)}, u32[]{:S(2)}) async-start(bf16[8,128,2048]{2,1,0:T(8,128)(2,1)} %bitcast.90), calls=%async_computation.3 | async-start | bytes 8388608 | tf_op jit(solution)/shard_map/all_to_all | solution.py:106
  339.6 63.5 %copy-start.1 = (bf16[64,2,16,256]{3,2,1,0:T(8,128)(2,1)}, bf16[64,2,16,256]{3,2,1,0:T(8,128)(2,1)S(1)}, u32[]{:S(2)}) copy-start(bf16[64,2,16,256]{3,2,1,0:T(8,128)(2,1)S(1)} %scatter_fusion) | copy-start | bytes 3145732
Sparse Core Ops, SparseCore 0:
  10.2 79.4 all-gather.4
  91.4 117.7 all-gather.6

commit v3 on v2

--- a/solution.py
+++ b/solution.py
@@ -111,39 +111,36 @@
 
 def body(stream, segment, position, w_qkv, w_out, w_gate_up, w_down, page_table):
     tok_group = segment.shape[0]
-    owners = lax.axis_size("dp")
-    width = w_qkv.shape[1]
+    share_rows = stream.shape[0]
     local_cols = w_qkv.shape[2]
-    hidden_cols = w_gate_up.shape[2]
-    qkv_g, out_g = gather_packed(
-        [w_qkv.reshape(3 * width, local_cols), jnp.transpose(w_out)], "dp"
+    attn_w = lax.all_gather(
+        jnp.concatenate([w_qkv, jnp.transpose(w_out)[None]], axis=0), "dp", axis=1, tiled=True
     )
-    qkv_g = qkv_g.reshape(owners, 3, width, local_cols)
-    gu_g, down_g = gather_packed(
-        [w_gate_up.reshape(2 * width, hidden_cols), jnp.transpose(w_down)], "dp"
+    mlp_w = lax.all_gather(
+        jnp.concatenate([w_gate_up, jnp.transpose(w_down)[None]], axis=0), "dp", axis=1, tiled=True
     )
-    gu_g = gu_g.reshape(owners, 2, width, hidden_cols)
     full_stream = gather_rows(stream, "tensor")
-    normed = layer_norm(full_stream).astype(jnp.bfloat16).reshape(tok_group, owners, width)
+    normed = layer_norm(full_stream).astype(jnp.bfloat16)
     local_heads = local_cols // HD
-    projected = jnp.einsum("tgd,gcdf->ctf", normed, qkv_g, preferred_element_type=jnp.float32)
+    projected = jnp.einsum("td,cdf->ctf", normed, attn_w[:3], preferred_element_type=jnp.float32)
     query = rotate(projected[0].reshape(tok_group, local_heads, HD), position).astype(jnp.bfloat16)
     keys = rotate(projected[1].reshape(tok_group, local_heads, HD), position).astype(jnp.bfloat16)
     values = projected[2].reshape(tok_group, local_heads, HD).astype(jnp.bfloat16)
     context = attend(query, keys, values, segment)
-    attn_part = jnp.einsum(
-        "tr,gcr->tgc", context, out_g, preferred_element_type=jnp.float32
-    ).reshape(tok_group, owners * width)
+    attn_part = jnp.einsum("tr,dr->td", context, attn_w[3], preferred_element_type=jnp.float32)
     attn_mine = sum_rows(attn_part.astype(jnp.bfloat16), "tensor")
     mid = (stream.astype(jnp.float32) + attn_mine).astype(jnp.bfloat16)
     normed2_mine = layer_norm(mid).astype(jnp.bfloat16)
-    normed2 = gather_rows(normed2_mine, "tensor").reshape(tok_group, owners, width)
-    gate_up = jnp.einsum("tgd,gcdf->ctf", normed2, gu_g, preferred_element_type=jnp.float32)
-    hidden = (jax.nn.silu(gate_up[0]) * gate_up[1]).astype(jnp.bfloat16)
-    mlp_part = jnp.einsum(
-        "tf,gcf->tgc", hidden, down_g, preferred_element_type=jnp.float32
-    ).reshape(tok_group, owners * width)
-    mlp_mine = sum_rows(mlp_part.astype(jnp.bfloat16), "tensor")
+    pieces = 2
+    piece = share_rows // pieces
+    mlp_pieces = []
+    for first in range(0, share_rows, piece):
+        rows = gather_rows(normed2_mine[first:first + piece], "tensor")
+        gate_up = jnp.einsum("td,cdf->ctf", rows, mlp_w[:2], preferred_element_type=jnp.float32)
+        hidden = (jax.nn.silu(gate_up[0]) * gate_up[1]).astype(jnp.bfloat16)
+        mlp_part = jnp.einsum("tf,df->td", hidden, mlp_w[2], preferred_element_type=jnp.float32)
+        mlp_pieces.append(sum_rows(mlp_part.astype(jnp.bfloat16), "tensor"))
+    mlp_mine = jnp.concatenate(mlp_pieces, axis=0)
     layer_out = (mid.astype(jnp.float32) + mlp_mine).astype(jnp.bfloat16)
     kv_cache = write_cache(keys, values, page_table)
     return (layer_out, kv_cache)

time: 417 us -> 380 us (0.911)
  the two profiles are of different devices: /device:TPU:38 before, /device:TPU:1 now
where the time goes in v3:
time: 380 us; the launch traced here: 378 us
  waiting for transfers between devices  177 us (47%)
  matrix products  48.8 us (13%)
  starting transfers between devices  37.3 us (10%)
  local copies, waits for them, and re-layouts  35.5 us (9%)
  blocking collectives  35.4 us (9%)
  other arithmetic  30.1 us (8%)
  between operations  14.5 us (4%)
    all_to_all x3, waiting for transfers between devices, sum_rows(): lax.all_to_all(terms.reshape(count, terms.shape[0] // count, terms.shape[...  84.5 us
    all_to_all x2, waiting for transfers between devices, gather_rows(): gathered = lax.all_to_all(copies, axis_name, 0, 0, tiled=True)  65.9 us
    all_to_all x1, blocking collectives, gather_rows(): gathered = lax.all_to_all(copies, axis_name, 0, 0, tiled=True)  35.4 us
    dot_general x2, matrix products, body(): jnp.einsum('td,cdf->ctf', rows, mlp_w[:2], preferred_element_type=jnp.flo...  15.3 us
    all_to_all x1, waiting for transfers between devices, write_cache(): lax.all_to_all(outgoing, 'dp', split_axis=0, concat_axis=0, tiled=True)  15.2 us
    all_to_all x3, starting transfers between devices, sum_rows(): lax.all_to_all(terms.reshape(count, terms.shape[0] // count, terms.shape[...  14.9 us
    unnamed x32, local copies, waits for them, and re-layouts  13.4 us
    dot_general x2, matrix products, body(): jnp.einsum('tf,df->td', hidden, mlp_w[2], preferred_element_type=jnp.floa...  12.3 us
  transfers between devices with their start and end apart: 9, of which 8 were waited for; matrix products, arithmetic and copies ran while one was open for 28% of the time, Pallas kernels for 0%

profile of v3, /device:TPU:1, one launch (start us, length us, event | category | flops | bytes accessed | tf_op | source)
XLA Modules:
  0.0 378.4 jit_solution(9202541788211394279)
XLA Ops:
  7.2 1.1 copy.29
  8.4 1.6 pad_maximum_fusion.3
  10.0 1.3 copy.35
  11.3 2.0 pad_maximum_fusion
  13.3 2.5 broadcast_in_dim.47
  15.8 8.3 %all-to-all-start = ((bf16[8,128,2048]{2,1,0:T(8,128)(2,1)}), bf16[8,128,2048]{2,1,0:T(8,128)(2,1)}, u32[]{:S(2)}, u32[]{:S(2)}) async-start(bf16[8,128,2048]{2,1,0:T(8,128)(2,1)} %broadcast_in_dim.47), calls=%async_computation | async-start | bytes 8388608 | tf_op jit(solution)/shard_map/all_to_all | solution.py:100
  24.5 1.4 fusion.23
  25.9 1.9 multiply_cosine_fusion
  27.8 51.2 %all-to-all-done = bf16[8,128,2048]{2,1,0:T(8,128)(2,1)} async-done(((bf16[8,128,2048]{2,1,0:T(8,128)(2,1)}), bf16[8,128,2048]{2,1,0:T(8,128)(2,1)}, u32[]{:S(2)}, u32[]{:S(2)}) %all-to-all-start) | async-done | bytes 4194336 | tf_op jit(solution)/shard_map/all_to_all | solution.py:100
  79.0 2.8 convert_reduce_fusion.1
  81.8 3.4 multiply_reduce_fusion
  85.2 4.2 %fusion.3 = bf16[1024,2048]{1,0:T(8,128)(2,1)} fusion(bf16[8,128,2048]{2,1,0:T(8,128)(2,1)} %all-to-all-done, f32[1024]{0:T(1024)S(1)} %rsqrt_bitcast_fusion, f32[1024]{0:T(1024)S(1)} %get-tuple-element.22), kind=kLoop, calls=%fused_computation.7 | loop fusion | flops 8388608 | bytes 8396800 | tf_op jit(solution)/shard_map/convert_element_type | solution.py:123
  89.4 9.2 %all-gather.3.cloned.1.call-done = bf16[4,2048,256]{1,2,0:T(8,128)(2,1)} async-done(((bf16[4,128,256]{1,2,0:T(8,128)(2,1)}), bf16[4,2048,256]{1,2,0:T(8,128)(2,1)}) %all-gather.3.cloned.1.call-update) | async-done | bytes 4194320 | tf_op jit(solution)/shard_map/all_gather | solution.py:116
  98.7 6.4 %fusion.26 = f32[3,1024,256]{1,2,0:T(8,128)S(1)} fusion(bf16[4,2048,256]{1,2,0:T(8,128)(2,1)} %all-gather.3.cloned.1.call-done, bf16[1024,2048]{1,0:T(8,128)(2,1)} %fusion.3), kind=kOutput, calls=%fused_computation.42 | convolution fusion | flops 3221225472 | bytes 11534336 | tf_op jit(solution)/shard_map/td,cdf->ctf/dot_general | solution.py:125
  105.1 0.9 slice.171
  106.2 1.0 fusion.78
  107.2 1.4 copy.44
  108.6 2.4 copy.45
  111.0 1.0 fusion.79
  112.0 1.4 copy.42
  113.4 2.4 copy.43
  115.8 1.6 multiply_subtract_fusion
  117.3 0.3 maximum_convert_fusion
  118.0 0.8 copy-done.8
  118.7 0.5 fusion.56
  119.3 1.3 copy-done.7
  120.6 1.1 fusion.83
  121.7 3.4 fusion.38
  125.2 3.9 %fusion.82 = (f32[2,512]{1,0:T(2,128)S(1)}, bf16[2,512,1024]{2,1,0:T(8,128)(2,1)}) fusion(pred[512,1024]{1,0:T(8,128)(4,1)S(1)} %copy-done.10, bf16[1024,2,128]{2,0,1:T(8,128)(2,1)S(1)} %maximum_convert_fusion, bf16[1024,2,64]{2,0,1:T(8,128)(2,1)S(1)} %copy-done.9, bf16[1024,2,64]{2,0,1:T(8,128)(2,1)S(1)} %get-tuple-element.10), kind=kOutput, calls=%fused_computation.115 | convolution fusion | flops 545260544 | bytes 3674112 | tf_op jit(solution)/shard_map/sub | solution.py:53
  129.1 2.5 fusion.39
  131.6 4.5 %convolution_convert_fusion = bf16[1024,2048]{1,0:T(8,128)(2,1)} fusion(bf16[1024,256]{0,1:T(8,128)(2,1)S(1)} %bitcast.100, bf16[4,2048,256]{1,2,0:T(8,128)(2,1)} %all-gather.3.cloned.1.call-done), kind=kOutput, calls=%fused_computation.19 | convolution fusion | flops 1075838976 | bytes 5767168 | tf_op jit(solution)/shard_map/tr,dr->td/dot_general | solution.py:130
  136.1 5.7 %all-to-all-start.1 = ((bf16[8,128,2048]{2,1,0:T(8,128)(2,1)}), bf16[8,128,2048]{2,1,0:T(8,128)(2,1)}, u32[]{:S(2)}, u32[]{:S(2)}) async-start(bf16[8,128,2048]{2,1,0:T(8,128)(2,1)} %bitcast.94), calls=%async_computation.1 | async-start | bytes 8388608 | tf_op jit(solution)/shard_map/all_to_all | solution.py:106
  141.9 2.0 sort.17
  143.9 0.8 gather_fusion
  144.7 0.7 all_to_all.33
  145.4 0.5 copy.37
  146.2 0.3 convert_element_type.124
  146.6 1.6 gather_fusion.1
  148.2 51.7 %all-to-all-done.1 = bf16[8,128,2048]{2,1,0:T(8,128)(2,1)} async-done(((bf16[8,128,2048]{2,1,0:T(8,128)(2,1)}), bf16[8,128,2048]{2,1,0:T(8,128)(2,1)}, u32[]{:S(2)}, u32[]{:S(2)}) %all-to-all-start.1) | async-done | bytes 4194336 | tf_op jit(solution)/shard_map/all_to_all | solution.py:106
  199.9 6.3 %all-to-all-start.6 = ((s32[16,1,4]{2,1,0:T(1,128)}), s32[16,1,4]{2,1,0:T(1,128)S(1)}, u32[]{:S(2)}, u32[]{:S(2)}) async-start(s32[16,1,4]{2,1,0:T(1,128)} %bitcast.31), calls=%async_computation.6 | async-start | bytes 16384 | tf_op jit(solution)/shard_map/all_to_all | solution.py:79
  206.3 3.0 convert_reduce_fusion
  209.5 0.3 fusion.42
  209.8 2.0 all-to-all-done.6
  211.8 4.1 %all-to-all-start.7 = ((bf16[16,4,2,16,256]{4,3,2,1,0:T(8,128)(2,1)}), bf16[16,4,2,16,256]{4,3,2,1,0:T(8,128)(2,1)S(1)}, u32[]{:S(2)}, u32[]{:S(2)}) async-start(bf16[16,4,2,16,256]{4,3,2,1,0:T(8,128)(2,1)} %bitcast.37), calls=%async_computation.7 | async-start | bytes 2097152 | tf_op jit(solution)/shard_map/all_to_all | solution.py:78
  215.9 0.3 fusion.43
  216.3 15.2 %all-to-all-done.7 = bf16[16,4,2,16,256]{4,3,2,1,0:T(8,128)(2,1)S(1)} async-done(((bf16[16,4,2,16,256]{4,3,2,1,0:T(8,128)(2,1)}), bf16[16,4,2,16,256]{4,3,2,1,0:T(8,128)(2,1)S(1)}, u32[]{:S(2)}, u32[]{:S(2)}) %all-to-all-start.7) | async-done | bytes 1048608 | tf_op jit(solution)/shard_map/all_to_all | solution.py:78
  231.7 35.4 %all_to_all.44 = bf16[8,64,2048]{2,1,0:T(8,128)(2,1)} all-to-all(bf16[8,64,2048]{2,1,0:T(8,128)(2,1)S(1)} %broadcast_in_dim.53), channel_id=1, replica_groups=mesh['dp'=16,'tensor'=8] {'tensor'}, dimensions={0} | all-to-all | bytes 4194304 | tf_op jit(solution)/shard_map/all_to_all | solution.py:100
  267.2 1.6 broadcast_in_dim.54
  268.7 3.6 all-to-all-start.4
  272.4 7.6 %convolution_bitcast_fusion.1 = f32[2,512,1024]{1,2,0:T(8,128)S(1)} fusion(bf16[3,2048,1024]{1,2,0:T(8,128)(2,1)} %all-gather.5.cloned.1.call-done, bf16[512,2048,1]{1,0,2:T(8,128)(2,1)} %bitcast.104), kind=kOutput, calls=%fused_computation.26 | convolution fusion | flops 4294967296 | bytes 18874368 | tf_op jit(solution)/shard_map/td,cdf->ctf/dot_general | solution.py:139
  280.0 6.2 %fusion.12 = bf16[512,2048]{1,0:T(8,128)(2,1)} fusion(bf16[3,2048,1024]{1,2,0:T(8,128)(2,1)} %all-gather.5.cloned.1.call-done, f32[2,512,1024]{1,2,0:T(8,128)S(1)} %convolution_bitcast_fusion.1), kind=kOutput, calls=%fused_computation.23 | convolution fusion | flops 2151677952 | bytes 10485760 | tf_op jit(solution)/shard_map/tf,df->td/dot_general | solution.py:141
  286.2 14.7 %all-to-all-done.4 = bf16[8,64,2048]{2,1,0:T(8,128)(2,1)S(1)} async-done(((bf16[8,64,2048]{2,1,0:T(8,128)(2,1)}), bf16[8,64,2048]{2,1,0:T(8,128)(2,1)S(1)}, u32[]{:S(2)}, u32[]{:S(2)}) %all-to-all-start.4) | async-done | bytes 2097184 | tf_op jit(solution)/shard_map/all_to_all | solution.py:100
  300.9 1.3 copy-done.6
  302.2 3.6 all-to-all-start.3
  305.8 7.6 %convolution_bitcast_fusion = f32[2,512,1024]{1,2,0:T(8,128)S(1)} fusion(bf16[3,2048,1024]{1,2,0:T(8,128)(2,1)} %all-gather.5.cloned.1.call-done, bf16[512,2048,1]{1,0,2:T(8,128)(2,1)} %bitcast.102), kind=kOutput, calls=%fused_computation.25 | convolution fusion | flops 4294967296 | bytes 18874368 | tf_op jit(solution)/shard_map/td,cdf->ctf/dot_general | solution.py:139
  313.5 6.2 %fusion.13 = bf16[512,2048]{1,0:T(8,128)(2,1)} fusion(bf16[3,2048,1024]{1,2,0:T(8,128)(2,1)} %all-gather.5.cloned.1.call-done, f32[2,512,1024]{1,2,0:T(8,128)S(1)} %convolution_bitcast_fusion), kind=kOutput, calls=%fused_computation.24 | convolution fusion | flops 2151677952 | bytes 10485760 | tf_op jit(solution)/shard_map/tf,df->td/dot_general | solution.py:141
  319.7 14.7 %all-to-all-done.3 = bf16[8,64,2048]{2,1,0:T(8,128)(2,1)S(1)} async-done(((bf16[8,64,2048]{2,1,0:T(8,128)(2,1)}), bf16[8,64,2048]{2,1,0:T(8,128)(2,1)S(1)}, u32[]{:S(2)}, u32[]{:S(2)}) %all-to-all-start.3) | async-done | bytes 2097184 | tf_op jit(solution)/shard_map/all_to_all | solution.py:106
  334.4 5.6 %all-to-all-start.5 = ((bf16[8,64,2048]{2,1,0:T(8,128)(2,1)}), bf16[8,64,2048]{2,1,0:T(8,128)(2,1)}, u32[]{:S(2)}, u32[]{:S(2)}) async-start(bf16[8,64,2048]{2,1,0:T(8,128)(2,1)} %bitcast.101), calls=%async_computation.5 | async-start | bytes 4194304 | tf_op jit(solution)/shard_map/all_to_all | solution.py:106
  340.1 1.1 broadcast_in_dim.55
  341.2 9.1 %scatter_fusion = bf16[64,2,16,256]{3,2,1,0:T(8,128)(2,1)} fusion(bf16[64,2,16,256]{3,2,1,0:T(8,128)(2,1)} %broadcast_in_dim.55, s32[64]{0:T(128)S(1)} %fusion.63, bf16[64,2,16,256]{3,2,1,0:T(8,128)(2,1)} %bitcast.95), kind=kCustom, calls=%fused_computation.2 | custom fusion | bytes 3145984 | tf_op jit(solution)/shard_map/scatter | solution.py:83
  350.3 0.3 convert_reduce_fusion.3
  350.6 18.0 %all-to-all-done.5 = bf16[8,64,2048]{2,1,0:T(8,128)(2,1)} async-done(((bf16[8,64,2048]{2,1,0:T(8,128)(2,1)}), bf16[8,64,2048]{2,1,0:T(8,128)(2,1)}, u32[]{:S(2)}, u32[]{:S(2)}) %all-to-all-start.5) | async-done | bytes 2097184 | tf_op jit(solution)/shard_map/all_to_all | solution.py:106
  368.7 2.0 convert_reduce_fusion.2
  370.7 0.9 fusion.44
  (57 shorter events, 2.0 us)
Async XLA Ops:
  7.2 6.1 %copy-start.4 = (bf16[128,2048]{1,0:T(8,128)(2,1)S(1)}, bf16[128,2048]{1,0:T(8,128)(2,1)}, u32[]{:S(2)}) copy-start(bf16[128,2048]{1,0:T(8,128)(2,1)} %param.8) | copy-start | bytes 1572868
  7.2 91.5 %all-gather.3.cloned.1.call-start = ((), (), s32[]{:S(2)}) async-start(), calls=%async_computation.8 | async-start | bytes 4456448 | tf_op jit(solution)/shard_map/all_gather | solution.py:116
  10.0 262.4 %all-gather.5.cloned.1.call-start = ((), (), s32[]{:S(2)}) async-start(), calls=%async_computation.9 | async-start | bytes 13369344 | tf_op jit(solution)/shard_map/all_gather | solution.py:119
  15.8 8.3 %copy-start.12 = (s32[1024]{0:T(1024)S(1)}, s32[1024]{0:T(1024)}, u32[]{:S(2)}) copy-start(s32[1024]{0:T(1024)} %param.10) | copy-start | bytes 12292
  15.8 8.4 %copy-start.11 = (s32[1024]{0:T(1024)S(1)}, s32[1024]{0:T(1024)}, u32[]{:S(2)}) copy-start(s32[1024]{0:T(1024)} %param.9) | copy-start | bytes 12292
  15.8 63.1 %all-to-all-start = ((bf16[8,128,2048]{2,1,0:T(8,128)(2,1)}), bf16[8,128,2048]{2,1,0:T(8,128)(2,1)}, u32[]{:S(2)}, u32[]{:S(2)}) async-start(bf16[8,128,2048]{2,1,0:T(8,128)(2,1)} %broadcast_in_dim.47), calls=%async_computation | async-start | bytes 8388608 | tf_op jit(solution)/shard_map/all_to_all | solution.py:100
  115.8 1.9 copy-start.2
  117.9 0.8 copy-start.8
  119.3 1.4 copy-start.7
  120.6 1.1 slice-start
  121.7 3.5 copy-start.9
  121.7 3.5 copy-start.10
  125.2 3.9 %copy-start.3 = (bf16[1,1024,256]{1,2,0:T(8,128)(2,1)S(1)}, bf16[1,1024,256]{1,2,0:T(8,128)(2,1)}, u32[]{:S(2)}) copy-start(bf16[1,1024,256]{1,2,0:T(8,128)(2,1)} %slice.171) | copy-start | bytes 1572868
  136.1 5.7 %copy-start = (s32[64]{0:T(128)S(1)}, s32[64]{0:T(128)}, u32[]{:S(2)}) copy-start(s32[64]{0:T(128)} %param.15) | copy-start | bytes 772
  136.1 63.8 %all-to-all-start.1 = ((bf16[8,128,2048]{2,1,0:T(8,128)(2,1)}), bf16[8,128,2048]{2,1,0:T(8,128)(2,1)}, u32[]{:S(2)}, u32[]{:S(2)}) async-start(bf16[8,128,2048]{2,1,0:T(8,128)(2,1)} %bitcast.94), calls=%async_computation.1 | async-start | bytes 8388608 | tf_op jit(solution)/shard_map/all_to_all | solution.py:106
  148.2 61.1 %copy-start.5 = (bf16[128,2048]{1,0:T(8,128)(2,1)S(1)}, bf16[128,2048]{1,0:T(8,128)(2,1)}, u32[]{:S(2)}) copy-start(bf16[128,2048]{1,0:T(8,128)(2,1)} %param.8) | copy-start | bytes 1572868
  199.9 11.9 %all-to-all-start.6 = ((s32[16,1,4]{2,1,0:T(1,128)}), s32[16,1,4]{2,1,0:T(1,128)S(1)}, u32[]{:S(2)}, u32[]{:S(2)}) async-start(s32[16,1,4]{2,1,0:T(1,128)} %bitcast.31), calls=%async_computation.6 | async-start | bytes 16384 | tf_op jit(solution)/shard_map/all_to_all | solution.py:79
  211.8 19.7 %all-to-all-start.7 = ((bf16[16,4,2,16,256]{4,3,2,1,0:T(8,128)(2,1)}), bf16[16,4,2,16,256]{4,3,2,1,0:T(8,128)(2,1)S(1)}, u32[]{:S(2)}, u32[]{:S(2)}) async-start(bf16[16,4,2,16,256]{4,3,2,1,0:T(8,128)(2,1)} %bitcast.37), calls=%async_computation.7 | async-start | bytes 2097152 | tf_op jit(solution)/shard_map/all_to_all | solution.py:78
  231.5 35.7 %copy-start.1 = (bf16[16,4,2,16,256]{4,3,2,1,0:T(8,128)(2,1)}, bf16[16,4,2,16,256]{4,3,2,1,0:T(8,128)(2,1)S(1)}, u32[]{:S(2)}) copy-start(bf16[16,4,2,16,256]{4,3,2,1,0:T(8,128)(2,1)S(1)} %all-to-all-done.7) | copy-start | bytes 3145732
  268.7 32.2 %all-to-all-start.4 = ((bf16[8,64,2048]{2,1,0:T(8,128)(2,1)}), bf16[8,64,2048]{2,1,0:T(8,128)(2,1)S(1)}, u32[]{:S(2)}, u32[]{:S(2)}) async-start(bf16[8,64,2048]{2,1,0:T(8,128)(2,1)} %broadcast_in_dim.54), calls=%async_computation.4 | async-start | bytes 4194304 | tf_op jit(solution)/shard_map/all_to_all | solution.py:100
  300.9 1.3 copy-start.6
  302.2 32.2 %all-to-all-start.3 = ((bf16[8,64,2048]{2,1,0:T(8,128)(2,1)}), bf16[8,64,2048]{2,1,0:T(8,128)(2,1)S(1)}, u32[]{:S(2)}, u32[]{:S(2)}) async-start(bf16[8,64,2048]{2,1,0:T(8,128)(2,1)} %bitcast.103), calls=%async_computation.3 | async-start | bytes 4194304 | tf_op jit(solution)/shard_map/all_to_all | solution.py:106
  334.4 34.3 %all-to-all-start.5 = ((bf16[8,64,2048]{2,1,0:T(8,128)(2,1)}), bf16[8,64,2048]{2,1,0:T(8,128)(2,1)}, u32[]{:S(2)}, u32[]{:S(2)}) async-start(bf16[8,64,2048]{2,1,0:T(8,128)(2,1)} %bitcast.101), calls=%async_computation.5 | async-start | bytes 4194304 | tf_op jit(solution)/shard_map/all_to_all | solution.py:106
Sparse Core Ops, SparseCore 0:
  10.2 88.4 all-gather.2
  100.3 120.6 all-gather.4

commit v4 on v3

--- a/solution.py
+++ b/solution.py
@@ -1,4 +1,6 @@
 import math
+
+import numpy as np
 
 import jax
 import jax.numpy as jnp
@@ -109,9 +111,28 @@
     return jnp.sum(arrived.astype(jnp.float32), axis=0)
 
 
+def attend_block(query, keys, values, seg_q, seg_k, q_index):
+    scale = 1.0 / math.sqrt(HD)
+    scores = (
+        jnp.einsum("qhd,khd->hqk", query, keys, preferred_element_type=jnp.float32) * scale
+    )
+    allowed = (seg_q[:, None] == seg_k[None, :]) & (
+        jnp.arange(keys.shape[0])[None, :] <= jnp.asarray(q_index)[:, None]
+    )
+    top = jnp.max(jnp.where(allowed[None], scores, -1e30), axis=-1, keepdims=True)
+    weights = jnp.exp(jnp.where(allowed[None], scores - top, -1e30))
+    total = jnp.sum(weights, axis=-1)
+    mixed = jnp.einsum(
+        "hqk,khd->qhd", weights.astype(jnp.bfloat16), values, preferred_element_type=jnp.float32
+    )
+    mixed = (mixed / jnp.transpose(total)[:, :, None]).astype(jnp.bfloat16)
+    return mixed.reshape(query.shape[0], -1)
+
+
 def body(stream, segment, position, w_qkv, w_out, w_gate_up, w_down, page_table):
     tok_group = segment.shape[0]
     share_rows = stream.shape[0]
+    shares = tok_group // share_rows
     local_cols = w_qkv.shape[2]
     attn_w = lax.all_gather(
         jnp.concatenate([w_qkv, jnp.transpose(w_out)[None]], axis=0), "dp", axis=1, tiled=True
@@ -126,23 +147,42 @@
     query = rotate(projected[0].reshape(tok_group, local_heads, HD), position).astype(jnp.bfloat16)
     keys = rotate(projected[1].reshape(tok_group, local_heads, HD), position).astype(jnp.bfloat16)
     values = projected[2].reshape(tok_group, local_heads, HD).astype(jnp.bfloat16)
-    context = attend(query, keys, values, segment)
-    attn_part = jnp.einsum("tr,dr->td", context, attn_w[3], preferred_element_type=jnp.float32)
-    attn_mine = sum_rows(attn_part.astype(jnp.bfloat16), "tensor")
-    mid = (stream.astype(jnp.float32) + attn_mine).astype(jnp.bfloat16)
-    normed2_mine = layer_norm(mid).astype(jnp.bfloat16)
+    kv_cache = write_cache(keys, values, page_table)
+
     pieces = 2
     piece = share_rows // pieces
-    mlp_pieces = []
-    for first in range(0, share_rows, piece):
-        rows = gather_rows(normed2_mine[first:first + piece], "tensor")
+    span = 2
+    query_grid = query.reshape(shares, pieces, piece, local_heads, HD)
+    segment_grid = segment.reshape(shares, pieces, piece)
+    index_grid = np.arange(tok_group).reshape(shares, pieces, piece)
+    outputs = []
+    for p in range(pieces):
+        blocks = []
+        for s in range(0, shares, span):
+            k_len = (s + span) * share_rows
+            blocks.append(
+                attend_block(
+                    query_grid[s:s + span, p].reshape(span * piece, local_heads, HD),
+                    keys[:k_len],
+                    values[:k_len],
+                    segment_grid[s:s + span, p].reshape(span * piece),
+                    segment[:k_len],
+                    index_grid[s:s + span, p].reshape(span * piece),
+                )
+            )
+        context = jnp.concatenate(blocks, axis=0)
+        attn_part = jnp.einsum("tr,dr->td", context, attn_w[3], preferred_element_type=jnp.float32)
+        attn_mine = sum_rows(attn_part.astype(jnp.bfloat16), "tensor")
+        mid = (stream[p * piece:(p + 1) * piece].astype(jnp.float32) + attn_mine).astype(
+            jnp.bfloat16
+        )
+        rows = gather_rows(layer_norm(mid).astype(jnp.bfloat16), "tensor")
         gate_up = jnp.einsum("td,cdf->ctf", rows, mlp_w[:2], preferred_element_type=jnp.float32)
         hidden = (jax.nn.silu(gate_up[0]) * gate_up[1]).astype(jnp.bfloat16)
         mlp_part = jnp.einsum("tf,df->td", hidden, mlp_w[2], preferred_element_type=jnp.float32)
-        mlp_pieces.append(sum_rows(mlp_part.astype(jnp.bfloat16), "tensor"))
-    mlp_mine = jnp.concatenate(mlp_pieces, axis=0)
-    layer_out = (mid.astype(jnp.float32) + mlp_mine).astype(jnp.bfloat16)
-    kv_cache = write_cache(keys, values, page_table)
+        mlp_mine = sum_rows(mlp_part.astype(jnp.bfloat16), "tensor")
+        outputs.append((mid.astype(jnp.float32) + mlp_mine).astype(jnp.bfloat16))
+    layer_out = jnp.concatenate(outputs, axis=0)
     return (layer_out, kv_cache)
 
 

time: 380 us -> 386 us (1.016)
  blocking collectives: 35.4 us -> 0 us
  matrix products: 48.8 us -> 59.7 us
  starting transfers between devices: 37.3 us -> 46.6 us
  waiting for transfers between devices: 177 us -> 186 us
  other arithmetic: 30.1 us -> 36.3 us
    all_to_all x1 -> x0, blocking collectives: 35.4 us -> none  [gather_rows(): gathered = lax.all_to_all(copies, axis_name, 0, 0, tiled=True)]
    all_to_all x2 -> x3, waiting for transfers between devices: 65.9 us -> 91.1 us  [gather_rows(): gathered = lax.all_to_all(copies, axis_name, 0, 0, tiled=True)]
    all_to_all x3 -> x4, waiting for transfers between devices: 84.5 us -> 66.7 us  [sum_rows(): lax.all_to_all(terms.reshape(count, terms.shape[0] // count, terms.shape[...]
    dot_general x3 -> x16, matrix products: 6.43 us -> 18.9 us  [the longest x8 16 us: attend_block(): jnp.einsum('hqk,khd->qhd', weights.astype(jnp.bfloat16), values, preferre...]
    all_to_all x2 -> x3, starting transfers between devices: 11.9 us -> 16.8 us  [gather_rows(): gathered = lax.all_to_all(copies, axis_name, 0, 0, tiled=True)]
    all_to_all x3 -> x4, starting transfers between devices: 14.9 us -> 19.1 us  [sum_rows(): lax.all_to_all(terms.reshape(count, terms.shape[0] // count, terms.shape[...]
    sub x1 -> x0, matrix products: 3.9 us -> none  [attend(): weights = jnp.exp(jnp.where(allowed[None], scores - top, -1e+30))]
    unnamed x32 -> x72, local copies, waits for them, and re-layouts: 13.4 us -> 11.6 us
  transfers between devices with their start and end apart: 9 -> 11, of which waited for: 8 -> 10; matrix products, arithmetic and copies ran while one was open for 28% -> 33% of each run, Pallas kernels for 0% -> 0%
where the time goes in v4:
time: 386 us; the launch traced here: 382 us
  waiting for transfers between devices  186 us (48%)
  matrix products  59.7 us (15%)
  starting transfers between devices  46.6 us (12%)
  local copies, waits for them, and re-layouts  39.2 us (10%)
  other arithmetic  36.3 us (9%)
  between operations  14.7 us (4%)
    all_to_all x3, waiting for transfers between devices, gather_rows(): gathered = lax.all_to_all(copies, axis_name, 0, 0, tiled=True)  91.1 us
    all_to_all x4, waiting for transfers between devices, sum_rows(): lax.all_to_all(terms.reshape(count, terms.shape[0] // count, terms.shape[...  66.7 us
    all_to_all x4, starting transfers between devices, sum_rows(): lax.all_to_all(terms.reshape(count, terms.shape[0] // count, terms.shape[...  19.1 us
    all_to_all x3, starting transfers between devices, gather_rows(): gathered = lax.all_to_all(copies, axis_name, 0, 0, tiled=True)  16.8 us
    dot_general x8, matrix products, attend_block(): jnp.einsum('hqk,khd->qhd', weights.astype(jnp.bfloat16), values, preferre...  16 us
    dot_general x2, matrix products, body(): jnp.einsum('td,cdf->ctf', rows, mlp_w[:2], preferred_element_type=jnp.flo...  15.3 us
    all_to_all x1, waiting for transfers between devices, write_cache(): lax.all_to_all(outgoing, 'dp', split_axis=0, concat_axis=0, tiled=True)  15.2 us
    dot_general x2, matrix products, body(): jnp.einsum('tf,df->td', hidden, mlp_w[2], preferred_element_type=jnp.floa...  12.3 us
  transfers between devices with their start and end apart: 11, of which 10 were waited for; matrix products, arithmetic and copies ran while one was open for 33% of the time, Pallas kernels for 0%

profile of v4, /device:TPU:1, one launch (start us, length us, event | category | flops | bytes accessed | tf_op | source)
XLA Modules:
  0.0 382.3 jit_solution(8507718372368850025)
XLA Ops:
  7.2 1.1 copy.35
  8.4 1.6 pad_maximum_fusion.2
  10.0 1.3 copy.40
  11.3 2.0 pad_maximum_fusion
  13.3 2.5 broadcast_in_dim.119
  16.0 8.3 %all-to-all-start = ((bf16[8,128,2048]{2,1,0:T(8,128)(2,1)}), bf16[8,128,2048]{2,1,0:T(8,128)(2,1)}, u32[]{:S(2)}, u32[]{:S(2)}) async-start(bf16[8,128,2048]{2,1,0:T(8,128)(2,1)} %broadcast_in_dim.119), calls=%async_computation | async-start | bytes 8388608 | tf_op jit(solution)/shard_map/all_to_all | solution.py:102
  27.6 1.1 fusion.93
  28.7 1.9 multiply_cosine_fusion
  30.6 48.2 %all-to-all-done = bf16[8,128,2048]{2,1,0:T(8,128)(2,1)} async-done(((bf16[8,128,2048]{2,1,0:T(8,128)(2,1)}), bf16[8,128,2048]{2,1,0:T(8,128)(2,1)}, u32[]{:S(2)}, u32[]{:S(2)}) %all-to-all-start) | async-done | bytes 4194336 | tf_op jit(solution)/shard_map/all_to_all | solution.py:102
  78.7 2.8 convert_reduce_fusion
  81.5 3.4 multiply_reduce_fusion
  85.0 4.2 %fusion.9 = bf16[1024,2048]{1,0:T(8,128)(2,1)} fusion(bf16[8,128,2048]{2,1,0:T(8,128)(2,1)} %all-to-all-done, f32[1024]{0:T(1024)S(1)} %rsqrt_bitcast_fusion, f32[1024]{0:T(1024)S(1)} %get-tuple-element.42), kind=kLoop, calls=%fused_computation.13 | loop fusion | flops 8388608 | bytes 8396800 | tf_op jit(solution)/shard_map/convert_element_type | solution.py:144
  89.2 9.4 %all-gather.3.cloned.1.call-done = bf16[4,2048,256]{1,2,0:T(8,128)(2,1)} async-done(((bf16[4,128,256]{1,2,0:T(8,128)(2,1)}), bf16[4,2048,256]{1,2,0:T(8,128)(2,1)}) %all-gather.3.cloned.1.call-update) | async-done | bytes 4194320 | tf_op jit(solution)/shard_map/all_gather | solution.py:137
  98.7 6.4 %fusion.18 = f32[3,1024,256]{1,2,0:T(8,128)S(1)} fusion(bf16[4,2048,256]{1,2,0:T(8,128)(2,1)} %all-gather.3.cloned.1.call-done, bf16[1024,2048]{1,0:T(8,128)(2,1)} %fusion.9), kind=kOutput, calls=%fused_computation.35 | convolution fusion | flops 3221225472 | bytes 11534336 | tf_op jit(solution)/shard_map/td,cdf->ctf/dot_general | solution.py:146
  108.4 2.4 copy.48
  110.9 1.3 copy.49
  113.1 1.4 copy.46
  114.5 1.3 copy.47
  115.8 1.9 multiply_subtract_fusion
  121.5 2.0 fusion.67
  123.5 2.0 fusion.71
  125.5 1.5 fusion.72
  127.0 1.5 fusion.65
  128.6 3.4 convolution_convert_fusion
  131.9 4.7 %all-to-all-start.4 = ((bf16[8,64,2048]{2,1,0:T(8,128)(2,1)}), bf16[8,64,2048]{2,1,0:T(8,128)(2,1)S(1)}, u32[]{:S(2)}, u32[]{:S(2)}) async-start(bf16[8,64,2048]{2,1,0:T(8,128)(2,1)} %bitcast.175), calls=%async_computation.4 | async-start | bytes 4194304 | tf_op jit(solution)/shard_map/all_to_all | solution.py:108
  137.5 1.2 convolution_multiply_fusion.5
  141.2 2.0 fusion.68
  143.1 2.3 fusion.69
  145.5 2.5 fusion.70
  148.0 2.1 fusion.66
  150.2 3.4 convolution_convert_fusion.1
  153.5 14.0 %all-to-all-done.4 = bf16[8,64,2048]{2,1,0:T(8,128)(2,1)S(1)} async-done(((bf16[8,64,2048]{2,1,0:T(8,128)(2,1)}), bf16[8,64,2048]{2,1,0:T(8,128)(2,1)S(1)}, u32[]{:S(2)}, u32[]{:S(2)}) %all-to-all-start.4) | async-done | bytes 2097184 | tf_op jit(solution)/shard_map/all_to_all | solution.py:108
  167.5 5.3 %all-to-all-start.1 = ((bf16[8,64,2048]{2,1,0:T(8,128)(2,1)}), bf16[8,64,2048]{2,1,0:T(8,128)(2,1)}, u32[]{:S(2)}, u32[]{:S(2)}) async-start(bf16[8,64,2048]{2,1,0:T(8,128)(2,1)} %bitcast.176), calls=%async_computation.1 | async-start | bytes 4194304 | tf_op jit(solution)/shard_map/all_to_all | solution.py:108
  172.9 2.0 sort.17
  176.4 1.3 copy.42
  177.7 1.0 copy.43
  178.7 2.2 convert_element_type.202
  180.9 1.3 maximum_bitcast_fusion
  182.2 1.6 gather_fusion.1
  184.2 20.0 %all-to-all-done.1 = bf16[8,64,2048]{2,1,0:T(8,128)(2,1)} async-done(((bf16[8,64,2048]{2,1,0:T(8,128)(2,1)}), bf16[8,64,2048]{2,1,0:T(8,128)(2,1)}, u32[]{:S(2)}, u32[]{:S(2)}) %all-to-all-start.1) | async-done | bytes 2097184 | tf_op jit(solution)/shard_map/all_to_all | solution.py:108
  204.2 6.6 %all-to-all-start.7 = ((s32[16,1,4]{2,1,0:T(1,128)}), s32[16,1,4]{2,1,0:T(1,128)S(1)}, u32[]{:S(2)}, u32[]{:S(2)}) async-start(s32[16,1,4]{2,1,0:T(1,128)} %bitcast.63), calls=%async_computation.7 | async-start | bytes 16384 | tf_op jit(solution)/shard_map/all_to_all | solution.py:81
  210.8 2.0 convert_reduce_fusion.4
  213.0 3.2 all-to-all-done.7
  216.3 4.0 %all-to-all-start.8 = ((bf16[16,4,2,16,256]{4,3,2,1,0:T(8,128)(2,1)}), bf16[16,4,2,16,256]{4,3,2,1,0:T(8,128)(2,1)S(1)}, u32[]{:S(2)}, u32[]{:S(2)}) async-start(bf16[16,4,2,16,256]{4,3,2,1,0:T(8,128)(2,1)} %bitcast.69), calls=%async_computation.8 | async-start | bytes 2097152 | tf_op jit(solution)/shard_map/all_to_all | solution.py:80
  220.6 15.2 %all-to-all-done.8 = bf16[16,4,2,16,256]{4,3,2,1,0:T(8,128)(2,1)S(1)} async-done(((bf16[16,4,2,16,256]{4,3,2,1,0:T(8,128)(2,1)}), bf16[16,4,2,16,256]{4,3,2,1,0:T(8,128)(2,1)S(1)}, u32[]{:S(2)}, u32[]{:S(2)}) %all-to-all-start.8) | async-done | bytes 1048608 | tf_op jit(solution)/shard_map/all_to_all | solution.py:80
  235.8 1.6 broadcast_in_dim.217
  237.4 4.4 %all-to-all-start.2 = ((bf16[8,64,2048]{2,1,0:T(8,128)(2,1)}), bf16[8,64,2048]{2,1,0:T(8,128)(2,1)}, u32[]{:S(2)}, u32[]{:S(2)}) async-start(bf16[8,64,2048]{2,1,0:T(8,128)(2,1)} %broadcast_in_dim.217), calls=%async_computation.2 | async-start | bytes 4194304 | tf_op jit(solution)/shard_map/all_to_all | solution.py:102
  242.2 28.2 %all-to-all-done.2 = bf16[8,64,2048]{2,1,0:T(8,128)(2,1)} async-done(((bf16[8,64,2048]{2,1,0:T(8,128)(2,1)}), bf16[8,64,2048]{2,1,0:T(8,128)(2,1)}, u32[]{:S(2)}, u32[]{:S(2)}) %all-to-all-start.2) | async-done | bytes 2097184 | tf_op jit(solution)/shard_map/all_to_all | solution.py:102
  270.4 1.6 broadcast_in_dim.222
  272.0 4.2 %all-to-all-start.5 = ((bf16[8,64,2048]{2,1,0:T(8,128)(2,1)}), bf16[8,64,2048]{2,1,0:T(8,128)(2,1)S(1)}, u32[]{:S(2)}, u32[]{:S(2)}) async-start(bf16[8,64,2048]{2,1,0:T(8,128)(2,1)} %broadcast_in_dim.222), calls=%async_computation.5 | async-start | bytes 4194304 | tf_op jit(solution)/shard_map/all_to_all | solution.py:102
  276.2 7.6 %convolution_bitcast_fusion.1 = f32[2,512,1024]{1,2,0:T(8,128)S(1)} fusion(bf16[3,2048,1024]{1,2,0:T(8,128)(2,1)} %all-gather.5.cloned.1.call-done, bf16[512,2048,1]{1,0,2:T(8,128)(2,1)} %bitcast.36), kind=kOutput, calls=%fused_computation.30 | convolution fusion | flops 4294967296 | bytes 18874368 | tf_op jit(solution)/shard_map/td,cdf->ctf/dot_general | solution.py:180
  283.8 6.2 %fusion.14 = bf16[512,2048]{1,0:T(8,128)(2,1)} fusion(bf16[3,2048,1024]{1,2,0:T(8,128)(2,1)} %all-gather.5.cloned.1.call-done, f32[2,512,1024]{1,2,0:T(8,128)S(1)} %convolution_bitcast_fusion.1), kind=kOutput, calls=%fused_computation.25 | convolution fusion | flops 2151677952 | bytes 10485760 | tf_op jit(solution)/shard_map/tf,df->td/dot_general | solution.py:182
  290.0 14.7 %all-to-all-done.5 = bf16[8,64,2048]{2,1,0:T(8,128)(2,1)S(1)} async-done(((bf16[8,64,2048]{2,1,0:T(8,128)(2,1)}), bf16[8,64,2048]{2,1,0:T(8,128)(2,1)S(1)}, u32[]{:S(2)}, u32[]{:S(2)}) %all-to-all-start.5) | async-done | bytes 2097184 | tf_op jit(solution)/shard_map/all_to_all | solution.py:102
  304.8 1.3 copy-done.3
  306.1 3.6 all-to-all-start.3
  309.7 7.6 %convolution_bitcast_fusion = f32[2,512,1024]{1,2,0:T(8,128)S(1)} fusion(bf16[3,2048,1024]{1,2,0:T(8,128)(2,1)} %all-gather.5.cloned.1.call-done, bf16[512,2048,1]{1,0,2:T(8,128)(2,1)} %bitcast.178), kind=kOutput, calls=%fused_computation.29 | convolution fusion | flops 4294967296 | bytes 18874368 | tf_op jit(solution)/shard_map/td,cdf->ctf/dot_general | solution.py:180
  317.4 6.1 %fusion.15 = bf16[512,2048]{1,0:T(8,128)(2,1)} fusion(bf16[3,2048,1024]{1,2,0:T(8,128)(2,1)} %all-gather.5.cloned.1.call-done, f32[2,512,1024]{1,2,0:T(8,128)S(1)} %convolution_bitcast_fusion), kind=kOutput, calls=%fused_computation.26 | convolution fusion | flops 2151677952 | bytes 10485760 | tf_op jit(solution)/shard_map/tf,df->td/dot_general | solution.py:182
  323.5 14.8 %all-to-all-done.3 = bf16[8,64,2048]{2,1,0:T(8,128)(2,1)S(1)} async-done(((bf16[8,64,2048]{2,1,0:T(8,128)(2,1)}), bf16[8,64,2048]{2,1,0:T(8,128)(2,1)S(1)}, u32[]{:S(2)}, u32[]{:S(2)}) %all-to-all-start.3) | async-done | bytes 2097184 | tf_op jit(solution)/shard_map/all_to_all | solution.py:108
  338.3 5.5 %all-to-all-start.6 = ((bf16[8,64,2048]{2,1,0:T(8,128)(2,1)}), bf16[8,64,2048]{2,1,0:T(8,128)(2,1)}, u32[]{:S(2)}, u32[]{:S(2)}) async-start(bf16[8,64,2048]{2,1,0:T(8,128)(2,1)} %bitcast.177), calls=%async_computation.6 | async-start | bytes 4194304 | tf_op jit(solution)/shard_map/all_to_all | solution.py:108
  343.9 1.1 broadcast_in_dim.223
  345.0 8.1 %scatter_fusion = bf16[64,2,16,256]{3,2,1,0:T(8,128)(2,1)} fusion(bf16[64,2,16,256]{3,2,1,0:T(8,128)(2,1)} %broadcast_in_dim.223, s32[64]{0:T(128)S(1)} %fusion.190, bf16[64,2,16,256]{3,2,1,0:T(8,128)(2,1)S(1)} %bitcast.172), kind=kCustom, calls=%fused_computation.2 | custom fusion | bytes 3145984 | tf_op jit(solution)/shard_map/scatter | solution.py:85
  353.5 1.0 fusion.87
  354.5 18.0 %all-to-all-done.6 = bf16[8,64,2048]{2,1,0:T(8,128)(2,1)} async-done(((bf16[8,64,2048]{2,1,0:T(8,128)(2,1)}), bf16[8,64,2048]{2,1,0:T(8,128)(2,1)}, u32[]{:S(2)}, u32[]{:S(2)}) %all-to-all-start.6) | async-done | bytes 2097184 | tf_op jit(solution)/shard_map/all_to_all | solution.py:108
  372.5 2.0 convert_reduce_fusion.1
  (138 shorter events, 18.9 us)
Async XLA Ops:
  7.2 6.1 %copy-start.4 = (bf16[128,2048]{1,0:T(8,128)(2,1)S(1)}, bf16[128,2048]{1,0:T(8,128)(2,1)}, u32[]{:S(2)}) copy-start(bf16[128,2048]{1,0:T(8,128)(2,1)} %param.16) | copy-start | bytes 1572868
  7.2 91.5 %all-gather.3.cloned.1.call-start = ((), (), s32[]{:S(2)}) async-start(), calls=%async_computation.9 | async-start | bytes 4456448 | tf_op jit(solution)/shard_map/all_gather | solution.py:137
  10.0 266.2 %all-gather.5.cloned.1.call-start = ((), (), s32[]{:S(2)}) async-start(), calls=%async_computation.10 | async-start | bytes 13369344 | tf_op jit(solution)/shard_map/all_gather | solution.py:140
  15.8 8.4 %copy-start.19 = (s32[1024]{0:T(1024)S(1)}, s32[1024]{0:T(1024)}, u32[]{:S(2)}) copy-start(s32[1024]{0:T(1024)} %param.17) | copy-start | bytes 12292
  15.8 8.5 %copy-start.22 = (s32[1024]{0:T(1024)S(1)}, s32[1024]{0:T(1024)}, u32[]{:S(2)}) copy-start(s32[1024]{0:T(1024)} %param.18) | copy-start | bytes 12292
  15.8 9.2 %slice-start = ((s32[1024]{0:T(1024)}), s32[256]{0:T(256)S(1)}, s32[]{:S(2)}) async-start(s32[1024]{0:T(1024)} %param.17), calls=%async_computation.11 | async-start | bytes 2048 | tf_op jit(solution)/shard_map/slice | solution.py:169
  15.8 9.2 %copy-start.27 = (s32[128]{0:T(128)S(1)}, s32[128]{0:T(128)}, u32[]{:S(2)}) copy-start(s32[128]{0:T(128)} %constant.77.clone) | copy-start | bytes 1540
  15.9 9.2 %copy-start.30 = (s32[128]{0:T(128)S(1)}, s32[128]{0:T(128)}, u32[]{:S(2)}) copy-start(s32[128]{0:T(128)} %constant.81.clone) | copy-start | bytes 1540
  15.9 9.9 %slice-start.1 = ((s32[1024]{0:T(1024)}), s32[512]{0:T(512)S(1)}, s32[]{:S(2)}) async-start(s32[1024]{0:T(1024)} %param.17), calls=%async_computation.12 | async-start | bytes 4096 | tf_op jit(solution)/shard_map/slice | solution.py:169
  15.9 9.9 %copy-start.28 = (s32[128]{0:T(128)S(1)}, s32[128]{0:T(128)}, u32[]{:S(2)}) copy-start(s32[128]{0:T(128)} %constant.78.clone) | copy-start | bytes 1540
  15.9 9.9 %copy-start.29 = (s32[128]{0:T(128)S(1)}, s32[128]{0:T(128)}, u32[]{:S(2)}) copy-start(s32[128]{0:T(128)} %constant.82.clone) | copy-start | bytes 1540
  15.9 10.7 %copy-start.25 = (s32[128]{0:T(128)S(1)}, s32[128]{0:T(128)}, u32[]{:S(2)}) copy-start(s32[128]{0:T(128)} %constant.79.clone) | copy-start | bytes 1540
  15.9 10.7 %copy-start.26 = (s32[128]{0:T(128)S(1)}, s32[128]{0:T(128)}, u32[]{:S(2)}) copy-start(s32[128]{0:T(128)} %constant.83.clone) | copy-start | bytes 1540
  15.9 11.7 %copy-start.23 = (s32[128]{0:T(128)S(1)}, s32[128]{0:T(128)}, u32[]{:S(2)}) copy-start(s32[128]{0:T(128)} %constant.80.clone) | copy-start | bytes 1540
  15.9 11.7 %copy-start.24 = (s32[128]{0:T(128)S(1)}, s32[128]{0:T(128)}, u32[]{:S(2)}) copy-start(s32[128]{0:T(128)} %constant.84.clone) | copy-start | bytes 1540
  16.0 62.8 %all-to-all-start = ((bf16[8,128,2048]{2,1,0:T(8,128)(2,1)}), bf16[8,128,2048]{2,1,0:T(8,128)(2,1)}, u32[]{:S(2)}, u32[]{:S(2)}) async-start(bf16[8,128,2048]{2,1,0:T(8,128)(2,1)} %broadcast_in_dim.119), calls=%async_computation | async-start | bytes 8388608 | tf_op jit(solution)/shard_map/all_to_all | solution.py:102
  25.8 93.6 %copy-start.21 = (pred[128,256]{1,0:T(8,128)(4,1)}, pred[128,256]{1,0:T(8,128)(4,1)S(1)}, u32[]{:S(2)}) copy-start(pred[128,256]{1,0:T(8,128)(4,1)S(1)} %get-tuple-element.47) | copy-start | bytes 98308
  115.8 2.2 copy-start.1
  118.0 1.9 copy-start.18
  118.0 2.4 copy-start.16
  118.3 2.8 copy-start.14
  119.4 1.3 copy-start.12
  125.5 3.0 copy-start.31
  125.5 3.0 copy-start.32
  128.5 8.4 %copy-start.15 = (pred[128,768]{1,0:T(8,128)(4,1)S(1)}, pred[128,768]{1,0:T(8,128)(4,1)}, u32[]{:S(2)}) copy-start(pred[128,768]{1,0:T(8,128)(4,1)} %get-tuple-element.38) | copy-start | bytes 294916
  131.9 35.6 %all-to-all-start.4 = ((bf16[8,64,2048]{2,1,0:T(8,128)(2,1)}), bf16[8,64,2048]{2,1,0:T(8,128)(2,1)S(1)}, u32[]{:S(2)}, u32[]{:S(2)}) async-start(bf16[8,64,2048]{2,1,0:T(8,128)(2,1)} %bitcast.175), calls=%async_computation.4 | async-start | bytes 4194304 | tf_op jit(solution)/shard_map/all_to_all | solution.py:108
  136.6 2.1 copy-start.17
  136.6 2.4 copy-start.20
  136.6 2.9 copy-start.10
  136.6 4.1 %copy-start.13 = (pred[128,1024]{1,0:T(8,128)(4,1)S(1)}, pred[128,1024]{1,0:T(8,128)(4,1)}, u32[]{:S(2)}) copy-start(pred[128,1024]{1,0:T(8,128)(4,1)} %get-tuple-element.40) | copy-start | bytes 393220
  136.9 2.3 copy-start.7
  137.4 2.3 copy-start.11
  137.4 8.0 %copy-start.9 = (bf16[1,768,256]{1,2,0:T(8,128)(2,1)S(1)}, bf16[1,768,256]{1,2,0:T(8,128)(2,1)}, u32[]{:S(2)}) copy-start(bf16[1,768,256]{1,2,0:T(8,128)(2,1)} %slice.213) | copy-start | bytes 1179652
  138.7 0.8 copy-start.8
  139.8 1.0 copy-start.6
  150.1 22.7 %copy-start = (s32[64]{0:T(128)S(1)}, s32[64]{0:T(128)}, u32[]{:S(2)}) copy-start(s32[64]{0:T(128)} %param.23) | copy-start | bytes 772
  167.5 36.7 %all-to-all-start.1 = ((bf16[8,64,2048]{2,1,0:T(8,128)(2,1)}), bf16[8,64,2048]{2,1,0:T(8,128)(2,1)}, u32[]{:S(2)}, u32[]{:S(2)}) async-start(bf16[8,64,2048]{2,1,0:T(8,128)(2,1)} %bitcast.176), calls=%async_computation.1 | async-start | bytes 4194304 | tf_op jit(solution)/shard_map/all_to_all | solution.py:108
  183.8 29.0 %copy-start.5 = (bf16[128,2048]{1,0:T(8,128)(2,1)S(1)}, bf16[128,2048]{1,0:T(8,128)(2,1)}, u32[]{:S(2)}) copy-start(bf16[128,2048]{1,0:T(8,128)(2,1)} %param.16) | copy-start | bytes 1572868
  204.2 12.1 %all-to-all-start.7 = ((s32[16,1,4]{2,1,0:T(1,128)}), s32[16,1,4]{2,1,0:T(1,128)S(1)}, u32[]{:S(2)}, u32[]{:S(2)}) async-start(s32[16,1,4]{2,1,0:T(1,128)} %bitcast.63), calls=%async_computation.7 | async-start | bytes 16384 | tf_op jit(solution)/shard_map/all_to_all | solution.py:81
  213.0 24.4 %copy-start.2 = (bf16[64,2048]{1,0:T(8,128)(2,1)}, bf16[64,2048]{1,0:T(8,128)(2,1)S(1)}, u32[]{:S(2)}) copy-start(bf16[64,2048]{1,0:T(8,128)(2,1)S(1)} %get-tuple-element.13) | copy-start | bytes 786436
  216.3 19.5 %all-to-all-start.8 = ((bf16[16,4,2,16,256]{4,3,2,1,0:T(8,128)(2,1)}), bf16[16,4,2,16,256]{4,3,2,1,0:T(8,128)(2,1)S(1)}, u32[]{:S(2)}, u32[]{:S(2)}) async-start(bf16[16,4,2,16,256]{4,3,2,1,0:T(8,128)(2,1)} %bitcast.69), calls=%async_computation.8 | async-start | bytes 2097152 | tf_op jit(solution)/shard_map/all_to_all | solution.py:80
  237.4 33.0 %all-to-all-start.2 = ((bf16[8,64,2048]{2,1,0:T(8,128)(2,1)}), bf16[8,64,2048]{2,1,0:T(8,128)(2,1)}, u32[]{:S(2)}, u32[]{:S(2)}) async-start(bf16[8,64,2048]{2,1,0:T(8,128)(2,1)} %broadcast_in_dim.217), calls=%async_computation.2 | async-start | bytes 4194304 | tf_op jit(solution)/shard_map/all_to_all | solution.py:102
  272.0 32.8 %all-to-all-start.5 = ((bf16[8,64,2048]{2,1,0:T(8,128)(2,1)}), bf16[8,64,2048]{2,1,0:T(8,128)(2,1)S(1)}, u32[]{:S(2)}, u32[]{:S(2)}) async-start(bf16[8,64,2048]{2,1,0:T(8,128)(2,1)} %broadcast_in_dim.222), calls=%async_computation.5 | async-start | bytes 4194304 | tf_op jit(solution)/shard_map/all_to_all | solution.py:102
  304.8 1.3 copy-start.3
  306.1 32.2 %all-to-all-start.3 = ((bf16[8,64,2048]{2,1,0:T(8,128)(2,1)}), bf16[8,64,2048]{2,1,0:T(8,128)(2,1)S(1)}, u32[]{:S(2)}, u32[]{:S(2)}) async-start(bf16[8,64,2048]{2,1,0:T(8,128)(2,1)} %bitcast.179), calls=%async_computation.3 | async-start | bytes 4194304 | tf_op jit(solution)/shard_map/all_to_all | solution.py:108
  338.3 34.2 %all-to-all-start.6 = ((bf16[8,64,2048]{2,1,0:T(8,128)(2,1)}), bf16[8,64,2048]{2,1,0:T(8,128)(2,1)}, u32[]{:S(2)}, u32[]{:S(2)}) async-start(bf16[8,64,2048]{2,1,0:T(8,128)(2,1)} %bitcast.177), calls=%async_computation.6 | async-start | bytes 4194304 | tf_op jit(solution)/shard_map/all_to_all | solution.py:108
Sparse Core Ops, SparseCore 0:
  10.2 88.4 all-gather.2
  100.3 119.4 all-gather.4

commit v5 on v4

--- a/solution.py
+++ b/solution.py
@@ -155,8 +155,8 @@
     query_grid = query.reshape(shares, pieces, piece, local_heads, HD)
     segment_grid = segment.reshape(shares, pieces, piece)
     index_grid = np.arange(tok_group).reshape(shares, pieces, piece)
-    outputs = []
-    for p in range(pieces):
+
+    def attention_piece(p):
         blocks = []
         for s in range(0, shares, span):
             k_len = (s + span) * share_rows
@@ -172,16 +172,35 @@
             )
         context = jnp.concatenate(blocks, axis=0)
         attn_part = jnp.einsum("tr,dr->td", context, attn_w[3], preferred_element_type=jnp.float32)
-        attn_mine = sum_rows(attn_part.astype(jnp.bfloat16), "tensor")
+        return attn_part.astype(jnp.bfloat16)
+
+    def mid_of(p, attn_part):
+        attn_mine = sum_rows(attn_part, "tensor")
         mid = (stream[p * piece:(p + 1) * piece].astype(jnp.float32) + attn_mine).astype(
             jnp.bfloat16
         )
-        rows = gather_rows(layer_norm(mid).astype(jnp.bfloat16), "tensor")
+        return mid, gather_rows(layer_norm(mid).astype(jnp.bfloat16), "tensor")
+
+    def mlp_of(rows):
         gate_up = jnp.einsum("td,cdf->ctf", rows, mlp_w[:2], preferred_element_type=jnp.float32)
         hidden = (jax.nn.silu(gate_up[0]) * gate_up[1]).astype(jnp.bfloat16)
         mlp_part = jnp.einsum("tf,df->td", hidden, mlp_w[2], preferred_element_type=jnp.float32)
-        mlp_mine = sum_rows(mlp_part.astype(jnp.bfloat16), "tensor")
-        outputs.append((mid.astype(jnp.float32) + mlp_mine).astype(jnp.bfloat16))
+        return mlp_part.astype(jnp.bfloat16)
+
+    attn_part0 = attention_piece(0)
+    attn_part0, kv_cache = lax.optimization_barrier((attn_part0, kv_cache))
+    mid0, rows0 = mid_of(0, attn_part0)
+    attn_part1 = attention_piece(1)
+    attn_part1, rows0 = lax.optimization_barrier((attn_part1, rows0))
+    mid1, rows1 = mid_of(1, attn_part1)
+    mlp_part0 = mlp_of(rows0)
+    mlp_part0, rows1 = lax.optimization_barrier((mlp_part0, rows1))
+    mlp_mine0 = sum_rows(mlp_part0, "tensor")
+    mlp_mine1 = sum_rows(mlp_of(rows1), "tensor")
+    outputs = [
+        (mid0.astype(jnp.float32) + mlp_mine0).astype(jnp.bfloat16),
+        (mid1.astype(jnp.float32) + mlp_mine1).astype(jnp.bfloat16),
+    ]
     layer_out = jnp.concatenate(outputs, axis=0)
     return (layer_out, kv_cache)
 

time: 386 us -> 390 us (1.010)
  blocking collectives: 0 us -> 41.6 us
  waiting for transfers between devices: 186 us -> 155 us
  starting transfers between devices: 46.6 us -> 41.1 us
  local copies, waits for them, and re-layouts: 39.2 us -> 34.3 us
    all_to_all x0 -> x2, blocking collectives: none -> 41.6 us  [the longest x1 28.8 us: sum_rows(): lax.all_to_all(terms.reshape(count, terms.shape[0] // count, terms.shape[...]
    all_to_all x1, waiting for transfers between devices: 15.2 us -> 2.04 us  [write_cache(): lax.all_to_all(outgoing, 'dp', split_axis=0, concat_axis=0, tiled=True)]
    all_gather x1, waiting for transfers between devices: 9.44 us -> 0.01 us  [body(): lax.all_gather(jnp.concatenate([w_qkv, jnp.transpose(w_out)[None]], axis=...]
    all_to_all x3, waiting for transfers between devices: 91.1 us -> 84 us  [gather_rows(): gathered = lax.all_to_all(copies, axis_name, 0, 0, tiled=True)]
    all_to_all x1 -> x0, starting transfers between devices: 6.58 us -> none  [write_cache(): lax.all_to_all(outgoing_ids, 'dp', split_axis=0, concat_axis=0, tiled=True)]
    scatter x1, local copies, waits for them, and re-layouts: 8.14 us -> 2.5 us  [write_cache(): return empty.at[local].set(arrived.reshape(pages, 2, page_size, width))]
    sub x8, other arithmetic: 2.36 us -> 6.31 us  [attend_block(): weights = jnp.exp(jnp.where(allowed[None], scores - top, -1e+30))]
    all_to_all x4 -> x3, waiting for transfers between devices: 66.7 us -> 69.2 us  [sum_rows(): lax.all_to_all(terms.reshape(count, terms.shape[0] // count, terms.shape[...]
  transfers between devices with their start and end apart: 11 -> 9, of which waited for: 10 -> 7; matrix products, arithmetic and copies ran while one was open for 33% -> 32% of each run, Pallas kernels for 0% -> 0%
where the time goes in v5:
time: 390 us; the launch traced here: 385 us
  waiting for transfers between devices  155 us (40%)
  matrix products  58.4 us (15%)
  blocking collectives  41.6 us (11%)
  starting transfers between devices  41.1 us (11%)
  other arithmetic  39.9 us (10%)
  local copies, waits for them, and re-layouts  34.3 us (9%)
  between operations  14.7 us (4%)
    all_to_all x3, waiting for transfers between devices, gather_rows(): gathered = lax.all_to_all(copies, axis_name, 0, 0, tiled=True)  84 us
    all_to_all x3, waiting for transfers between devices, sum_rows(): lax.all_to_all(terms.reshape(count, terms.shape[0] // count, terms.shape[...  69.2 us
    all_to_all x1, blocking collectives, sum_rows(): lax.all_to_all(terms.reshape(count, terms.shape[0] // count, terms.shape[...  28.8 us
    all_to_all x3, starting transfers between devices, sum_rows(): lax.all_to_all(terms.reshape(count, terms.shape[0] // count, terms.shape[...  20.5 us
    all_to_all x3, starting transfers between devices, gather_rows(): gathered = lax.all_to_all(copies, axis_name, 0, 0, tiled=True)  15.4 us
    dot_general x2, matrix products, mlp_of(): jnp.einsum('td,cdf->ctf', rows, mlp_w[:2], preferred_element_type=jnp.flo...  15.3 us
    unnamed x58, local copies, waits for them, and re-layouts  13.6 us
    dot_general x8, matrix products, attend_block(): jnp.einsum('hqk,khd->qhd', weights.astype(jnp.bfloat16), values, preferre...  13.2 us
  transfers between devices with their start and end apart: 9, of which 7 were waited for; matrix products, arithmetic and copies ran while one was open for 32% of the time, Pallas kernels for 0%

profile of v5, /device:TPU:1, one launch (start us, length us, event | category | flops | bytes accessed | tf_op | source)
XLA Modules:
  0.0 385.3 jit_solution(8672249362688641605)
XLA Ops:
  7.2 1.1 copy.35
  8.4 1.6 pad_maximum_fusion.2
  10.0 1.3 copy.45
  11.4 2.0 pad_maximum_fusion
  13.4 2.0 sort.17
  16.3 12.8 %all_to_all.49 = s32[16,1,4]{2,1,0:T(1,128)S(1)} all-to-all(s32[16,1,4]{2,1,0:T(1,128)S(1)} %bitcast.201), channel_id=1, replica_groups=mesh['dp'=16,'tensor'=8] {'dp'}, dimensions={0} | all-to-all | bytes 512 | tf_op jit(solution)/shard_map/all_to_all | solution.py:81
  29.1 2.5 broadcast_in_dim.119
  31.7 7.1 %all-to-all-start = ((bf16[8,128,2048]{2,1,0:T(8,128)(2,1)}), bf16[8,128,2048]{2,1,0:T(8,128)(2,1)}, u32[]{:S(2)}, u32[]{:S(2)}) async-start(bf16[8,128,2048]{2,1,0:T(8,128)(2,1)} %broadcast_in_dim.119), calls=%async_computation | async-start | bytes 8388608 | tf_op jit(solution)/shard_map/all_to_all | solution.py:102
  42.2 1.1 fusion.95
  43.3 1.9 multiply_cosine_fusion
  45.3 49.9 %all-to-all-done = bf16[8,128,2048]{2,1,0:T(8,128)(2,1)} async-done(((bf16[8,128,2048]{2,1,0:T(8,128)(2,1)}), bf16[8,128,2048]{2,1,0:T(8,128)(2,1)}, u32[]{:S(2)}, u32[]{:S(2)}) %all-to-all-start) | async-done | bytes 4194336 | tf_op jit(solution)/shard_map/all_to_all | solution.py:102
  95.2 2.8 convert_reduce_fusion
  98.0 3.4 multiply_reduce_fusion
  101.4 4.2 %fusion.9 = bf16[1024,2048]{1,0:T(8,128)(2,1)} fusion(bf16[8,128,2048]{2,1,0:T(8,128)(2,1)} %all-to-all-done, f32[1024]{0:T(1024)S(1)} %rsqrt_bitcast_fusion, f32[1024]{0:T(1024)S(1)} %get-tuple-element.52), kind=kLoop, calls=%fused_computation.13 | loop fusion | flops 8388608 | bytes 8396800 | tf_op jit(solution)/shard_map/convert_element_type | solution.py:144
  105.6 6.2 %fusion.20 = f32[3,1024,256]{1,2,0:T(8,128)S(1)} fusion(bf16[4,2048,256]{1,2,0:T(8,128)(2,1)} %all-gather.3.cloned.1.call-done, bf16[1024,2048]{1,0:T(8,128)(2,1)} %fusion.9), kind=kOutput, calls=%fused_computation.37 | convolution fusion | flops 3221225472 | bytes 11534336 | tf_op jit(solution)/shard_map/td,cdf->ctf/dot_general | solution.py:146
  111.8 1.7 copy-done.2
  115.2 2.7 fusion.222
  118.8 1.4 copy.48
  120.2 1.4 copy.49
  121.6 2.1 fusion.224
  123.7 2.4 copy.46
  126.1 1.3 copy.47
  127.4 1.5 multiply_subtract_fusion
  129.7 1.1 convert_element_type.174
  130.8 1.3 maximum_bitcast_fusion
  132.2 1.6 gather_fusion.1
  133.8 5.1 %all-to-all-start.2 = ((bf16[16,4,2,16,256]{4,3,2,1,0:T(8,128)(2,1)}), bf16[16,4,2,16,256]{4,3,2,1,0:T(8,128)(2,1)S(1)}, u32[]{:S(2)}, u32[]{:S(2)}) async-start(bf16[16,4,2,16,256]{4,3,2,1,0:T(8,128)(2,1)} %bitcast.38), calls=%async_computation.2 | async-start | bytes 2097152 | tf_op jit(solution)/shard_map/all_to_all | solution.py:80
  138.9 1.8 subtract_convert_fusion
  143.4 1.8 fusion.70
  147.4 1.3 fusion.230
  148.7 1.4 fusion.229
  150.1 2.6 fusion.72
  152.7 2.1 fusion.68
  154.8 3.5 convolution_convert_fusion.1
  158.2 2.0 all-to-all-done.2
  160.4 2.5 scatter_fusion
  163.9 11.3 %all-to-all-start.3 = ((bf16[8,64,2048]{2,1,0:T(8,128)(2,1)}), bf16[8,64,2048]{2,1,0:T(8,128)(2,1)S(1)}, u32[]{:S(2)}, u32[]{:S(2)}) async-start(bf16[8,64,2048]{2,1,0:T(8,128)(2,1)} %bitcast.175), calls=%async_computation.3 | async-start | bytes 4194304 | tf_op jit(solution)/shard_map/all_to_all | solution.py:108
  175.2 1.1 convolution_multiply_fusion.2
  176.3 1.5 fusion.226
  177.8 1.8 convolution_multiply_fusion.6
  179.5 1.9 convolution_multiply_fusion.4
  181.4 26.2 %all-to-all-done.3 = bf16[8,64,2048]{2,1,0:T(8,128)(2,1)S(1)} async-done(((bf16[8,64,2048]{2,1,0:T(8,128)(2,1)}), bf16[8,64,2048]{2,1,0:T(8,128)(2,1)S(1)}, u32[]{:S(2)}, u32[]{:S(2)}) %all-to-all-start.3) | async-done | bytes 2097184 | tf_op jit(solution)/shard_map/all_to_all | solution.py:108
  208.0 1.2 convert_reduce_fusion.6
  209.6 1.6 broadcast_in_dim.223
  211.2 4.5 %all-to-all-start.4 = ((bf16[8,64,2048]{2,1,0:T(8,128)(2,1)}), bf16[8,64,2048]{2,1,0:T(8,128)(2,1)}, u32[]{:S(2)}, u32[]{:S(2)}) async-start(bf16[8,64,2048]{2,1,0:T(8,128)(2,1)} %broadcast_in_dim.223), calls=%async_computation.4 | async-start | bytes 4194304 | tf_op jit(solution)/shard_map/all_to_all | solution.py:102
  216.9 1.4 fusion.69
  218.2 2.0 fusion.73
  220.2 1.9 fusion.74
  222.6 2.0 convolution_convert_fusion
  224.6 19.7 %all-to-all-done.4 = bf16[8,64,2048]{2,1,0:T(8,128)(2,1)} async-done(((bf16[8,64,2048]{2,1,0:T(8,128)(2,1)}), bf16[8,64,2048]{2,1,0:T(8,128)(2,1)}, u32[]{:S(2)}, u32[]{:S(2)}) %all-to-all-start.4) | async-done | bytes 2097184 | tf_op jit(solution)/shard_map/all_to_all | solution.py:102
  244.3 28.8 %all_to_all.50 = bf16[8,64,2048]{2,1,0:T(8,128)(2,1)S(1)} all-to-all(bf16[8,64,2048]{2,1,0:T(8,128)(2,1)S(1)} %bitcast.179), channel_id=1, replica_groups=mesh['dp'=16,'tensor'=8] {'tensor'}, dimensions={0} | all-to-all | bytes 4194304 | tf_op jit(solution)/shard_map/all_to_all | solution.py:108
  274.0 1.6 broadcast_in_dim.224
  275.6 3.8 all-to-all-start.6
  279.5 7.6 %convolution_bitcast_fusion.1 = f32[2,512,1024]{1,2,0:T(8,128)S(1)} fusion(bf16[3,2048,1024]{1,2,0:T(8,128)(2,1)} %all-gather.5.cloned.1.call-done, bf16[512,2048]{1,0:T(8,128)(2,1)} %bitcast.59), kind=kOutput, calls=%fused_computation.30 | convolution fusion | flops 4294967296 | bytes 18874368 | tf_op jit(solution)/shard_map/td,cdf->ctf/dot_general | solution.py:185
  287.1 6.2 %fusion.14 = bf16[512,2048]{1,0:T(8,128)(2,1)} fusion(bf16[3,2048,1024]{1,2,0:T(8,128)(2,1)} %all-gather.5.cloned.1.call-done, f32[2,512,1024]{1,2,0:T(8,128)S(1)} %convolution_bitcast_fusion.1), kind=kOutput, calls=%fused_computation.25 | convolution fusion | flops 2151677952 | bytes 10485760 | tf_op jit(solution)/shard_map/tf,df->td/dot_general | solution.py:187
  293.3 14.5 %all-to-all-done.6 = bf16[8,64,2048]{2,1,0:T(8,128)(2,1)S(1)} async-done(((bf16[8,64,2048]{2,1,0:T(8,128)(2,1)}), bf16[8,64,2048]{2,1,0:T(8,128)(2,1)S(1)}, u32[]{:S(2)}, u32[]{:S(2)}) %all-to-all-start.6) | async-done | bytes 2097184 | tf_op jit(solution)/shard_map/all_to_all | solution.py:102
  307.8 1.3 copy-done.3
  309.1 3.6 all-to-all-start.7
  312.7 7.6 %convolution_bitcast_fusion = f32[2,512,1024]{1,2,0:T(8,128)S(1)} fusion(bf16[3,2048,1024]{1,2,0:T(8,128)(2,1)} %all-gather.5.cloned.1.call-done, bf16[512,2048]{1,0:T(8,128)(2,1)} %bitcast.176), kind=kOutput, calls=%fused_computation.29 | convolution fusion | flops 4294967296 | bytes 18874368 | tf_op jit(solution)/shard_map/td,cdf->ctf/dot_general | solution.py:185
  320.4 6.1 %fusion.15 = bf16[512,2048]{1,0:T(8,128)(2,1)} fusion(bf16[3,2048,1024]{1,2,0:T(8,128)(2,1)} %all-gather.5.cloned.1.call-done, f32[2,512,1024]{1,2,0:T(8,128)S(1)} %convolution_bitcast_fusion), kind=kOutput, calls=%fused_computation.26 | convolution fusion | flops 2151677952 | bytes 10485760 | tf_op jit(solution)/shard_map/tf,df->td/dot_general | solution.py:187
  326.5 14.8 %all-to-all-done.7 = bf16[8,64,2048]{2,1,0:T(8,128)(2,1)S(1)} async-done(((bf16[8,64,2048]{2,1,0:T(8,128)(2,1)}), bf16[8,64,2048]{2,1,0:T(8,128)(2,1)S(1)}, u32[]{:S(2)}, u32[]{:S(2)}) %all-to-all-start.7) | async-done | bytes 2097184 | tf_op jit(solution)/shard_map/all_to_all | solution.py:108
  341.2 5.6 %all-to-all-start.8 = ((bf16[8,64,2048]{2,1,0:T(8,128)(2,1)}), bf16[8,64,2048]{2,1,0:T(8,128)(2,1)}, u32[]{:S(2)}, u32[]{:S(2)}) async-start(bf16[8,64,2048]{2,1,0:T(8,128)(2,1)} %bitcast.177), calls=%async_computation.8 | async-start | bytes 4194304 | tf_op jit(solution)/shard_map/all_to_all | solution.py:108
  347.2 28.3 %all-to-all-done.8 = bf16[8,64,2048]{2,1,0:T(8,128)(2,1)} async-done(((bf16[8,64,2048]{2,1,0:T(8,128)(2,1)}), bf16[8,64,2048]{2,1,0:T(8,128)(2,1)}, u32[]{:S(2)}, u32[]{:S(2)}) %all-to-all-start.8) | async-done | bytes 2097184 | tf_op jit(solution)/shard_map/all_to_all | solution.py:108
  375.5 2.0 convert_reduce_fusion.1
  (123 shorter events, 18.6 us)
Async XLA Ops:
  7.2 6.2 %copy-start = (s32[64]{0:T(128)S(1)}, s32[64]{0:T(128)}, u32[]{:S(2)}) copy-start(s32[64]{0:T(128)} %param.23) | copy-start | bytes 772
  7.2 22.0 %copy-start.4 = (bf16[128,2048]{1,0:T(8,128)(2,1)S(1)}, bf16[128,2048]{1,0:T(8,128)(2,1)}, u32[]{:S(2)}) copy-start(bf16[128,2048]{1,0:T(8,128)(2,1)} %param.16) | copy-start | bytes 1572868
  7.2 98.4 %all-gather.3.cloned.1.call-start = ((), (), s32[]{:S(2)}) async-start(), calls=%async_computation.9 | async-start | bytes 4456448 | tf_op jit(solution)/shard_map/all_gather | solution.py:137
  10.0 269.5 %all-gather.5.cloned.1.call-start = ((), (), s32[]{:S(2)}) async-start(), calls=%async_computation.10 | async-start | bytes 13369344 | tf_op jit(solution)/shard_map/all_gather | solution.py:140
  31.6 7.2 %copy-start.14 = (s32[1024]{0:T(1024)S(1)}, s32[1024]{0:T(1024)}, u32[]{:S(2)}) copy-start(s32[1024]{0:T(1024)} %param.17) | copy-start | bytes 12292
  31.6 7.3 %copy-start.16 = (s32[1024]{0:T(1024)S(1)}, s32[1024]{0:T(1024)}, u32[]{:S(2)}) copy-start(s32[1024]{0:T(1024)} %param.18) | copy-start | bytes 12292
  31.6 8.0 %slice-start = ((s32[1024]{0:T(1024)}), s32[256]{0:T(256)S(1)}, s32[]{:S(2)}) async-start(s32[1024]{0:T(1024)} %param.17), calls=%async_computation.11 | async-start | bytes 2048 | tf_op jit(solution)/shard_map/slice | solution.py:169
  31.6 8.0 %copy-start.23 = (s32[128]{0:T(128)S(1)}, s32[128]{0:T(128)}, u32[]{:S(2)}) copy-start(s32[128]{0:T(128)} %constant.77.clone) | copy-start | bytes 1540
  31.6 8.0 %copy-start.24 = (s32[128]{0:T(128)S(1)}, s32[128]{0:T(128)}, u32[]{:S(2)}) copy-start(s32[128]{0:T(128)} %constant.81.clone) | copy-start | bytes 1540
  31.7 8.8 %slice-start.1 = ((s32[1024]{0:T(1024)}), s32[512]{0:T(512)S(1)}, s32[]{:S(2)}) async-start(s32[1024]{0:T(1024)} %param.17), calls=%async_computation.12 | async-start | bytes 4096 | tf_op jit(solution)/shard_map/slice | solution.py:169
  31.7 8.7 %copy-start.21 = (s32[128]{0:T(128)S(1)}, s32[128]{0:T(128)}, u32[]{:S(2)}) copy-start(s32[128]{0:T(128)} %constant.78.clone) | copy-start | bytes 1540
  31.7 8.7 %copy-start.22 = (s32[128]{0:T(128)S(1)}, s32[128]{0:T(128)}, u32[]{:S(2)}) copy-start(s32[128]{0:T(128)} %constant.82.clone) | copy-start | bytes 1540
  31.7 9.5 %copy-start.19 = (s32[128]{0:T(128)S(1)}, s32[128]{0:T(128)}, u32[]{:S(2)}) copy-start(s32[128]{0:T(128)} %constant.79.clone) | copy-start | bytes 1540
  31.7 9.5 %copy-start.20 = (s32[128]{0:T(128)S(1)}, s32[128]{0:T(128)}, u32[]{:S(2)}) copy-start(s32[128]{0:T(128)} %constant.83.clone) | copy-start | bytes 1540
  31.7 10.5 %copy-start.17 = (s32[128]{0:T(128)S(1)}, s32[128]{0:T(128)}, u32[]{:S(2)}) copy-start(s32[128]{0:T(128)} %constant.80.clone) | copy-start | bytes 1540
  31.7 10.4 %copy-start.18 = (s32[128]{0:T(128)S(1)}, s32[128]{0:T(128)}, u32[]{:S(2)}) copy-start(s32[128]{0:T(128)} %constant.84.clone) | copy-start | bytes 1540
  31.7 63.4 %all-to-all-start = ((bf16[8,128,2048]{2,1,0:T(8,128)(2,1)}), bf16[8,128,2048]{2,1,0:T(8,128)(2,1)}, u32[]{:S(2)}, u32[]{:S(2)}) async-start(bf16[8,128,2048]{2,1,0:T(8,128)(2,1)} %broadcast_in_dim.119), calls=%async_computation | async-start | bytes 8388608 | tf_op jit(solution)/shard_map/all_to_all | solution.py:102
  111.8 1.7 copy-start.2
  114.2 31.0 %copy-start.11 = (bf16[1,512,256]{1,2,0:T(8,128)(2,1)}, bf16[1,512,256]{1,2,0:T(8,128)(2,1)S(1)}, u32[]{:S(2)}) copy-start(bf16[1,512,256]{1,2,0:T(8,128)(2,1)S(1)} %slice.208) | copy-start | bytes 786436
  133.8 26.5 %all-to-all-start.2 = ((bf16[16,4,2,16,256]{4,3,2,1,0:T(8,128)(2,1)}), bf16[16,4,2,16,256]{4,3,2,1,0:T(8,128)(2,1)S(1)}, u32[]{:S(2)}, u32[]{:S(2)}) async-start(bf16[16,4,2,16,256]{4,3,2,1,0:T(8,128)(2,1)} %bitcast.38), calls=%async_computation.2 | async-start | bytes 2097152 | tf_op jit(solution)/shard_map/all_to_all | solution.py:80
  146.5 0.9 copy-start.7
  162.9 1.0 copy-start.1
  163.9 43.7 %all-to-all-start.3 = ((bf16[8,64,2048]{2,1,0:T(8,128)(2,1)}), bf16[8,64,2048]{2,1,0:T(8,128)(2,1)S(1)}, u32[]{:S(2)}, u32[]{:S(2)}) async-start(bf16[8,64,2048]{2,1,0:T(8,128)(2,1)} %bitcast.175), calls=%async_computation.3 | async-start | bytes 4194304 | tf_op jit(solution)/shard_map/all_to_all | solution.py:108
  176.3 3.3 copy-start.6
  207.9 7.7 %copy-start.8 = (f32[2,128,512]{2,1,0:T(8,128)S(1)}, f32[2,128,512]{2,1,0:T(8,128)}, u32[]{:S(2)}) copy-start(f32[2,128,512]{2,1,0:T(8,128)} %convolution_multiply_fusion.4) | copy-start | bytes 1572868
  208.0 7.7 %copy-start.13 = (pred[128,512]{1,0:T(8,128)(4,1)S(1)}, pred[128,512]{1,0:T(8,128)(4,1)}, u32[]{:S(2)}) copy-start(pred[128,512]{1,0:T(8,128)(4,1)} %get-tuple-element.55) | copy-start | bytes 196612
  209.2 6.8 %copy-start.10 = (f32[2,128,256]{2,1,0:T(8,128)S(1)}, f32[2,128,256]{2,1,0:T(8,128)}, u32[]{:S(2)}) copy-start(f32[2,128,256]{2,1,0:T(8,128)} %convolution_multiply_fusion.6) | copy-start | bytes 786436
  209.2 6.8 %copy-start.15 = (pred[128,256]{1,0:T(8,128)(4,1)S(1)}, pred[128,256]{1,0:T(8,128)(4,1)}, u32[]{:S(2)}) copy-start(pred[128,256]{1,0:T(8,128)(4,1)} %get-tuple-element.57) | copy-start | bytes 98308
  209.6 6.6 %copy-start.9 = (bf16[2,1,64,2,128]{4,2,1,0,3:T(8,128)(2,1)S(1)}, bf16[2,1,64,2,128]{4,2,1,0,3:T(8,128)(2,1)}, u32[]{:S(2)}) copy-start(bf16[2,1,64,2,128]{4,2,1,0,3:T(8,128)(2,1)} %get-tuple-element.40) | copy-start | bytes 196612
  211.2 5.3 %copy-start.12 = (pred[128,1024]{1,0:T(8,128)(4,1)S(1)}, pred[128,1024]{1,0:T(8,128)(4,1)}, u32[]{:S(2)}) copy-start(pred[128,1024]{1,0:T(8,128)(4,1)} %get-tuple-element.51) | copy-start | bytes 393220
  211.2 33.1 %all-to-all-start.4 = ((bf16[8,64,2048]{2,1,0:T(8,128)(2,1)}), bf16[8,64,2048]{2,1,0:T(8,128)(2,1)}, u32[]{:S(2)}, u32[]{:S(2)}) async-start(bf16[8,64,2048]{2,1,0:T(8,128)(2,1)} %broadcast_in_dim.223), calls=%async_computation.4 | async-start | bytes 4194304 | tf_op jit(solution)/shard_map/all_to_all | solution.py:102
  220.2 2.4 copy-start.25
  224.6 48.8 %copy-start.5 = (bf16[128,2048]{1,0:T(8,128)(2,1)S(1)}, bf16[128,2048]{1,0:T(8,128)(2,1)}, u32[]{:S(2)}) copy-start(bf16[128,2048]{1,0:T(8,128)(2,1)} %param.16) | copy-start | bytes 1572868
  275.6 32.2 %all-to-all-start.6 = ((bf16[8,64,2048]{2,1,0:T(8,128)(2,1)}), bf16[8,64,2048]{2,1,0:T(8,128)(2,1)S(1)}, u32[]{:S(2)}, u32[]{:S(2)}) async-start(bf16[8,64,2048]{2,1,0:T(8,128)(2,1)} %broadcast_in_dim.224), calls=%async_computation.6 | async-start | bytes 4194304 | tf_op jit(solution)/shard_map/all_to_all | solution.py:102
  307.8 1.3 copy-start.3
  309.1 32.2 %all-to-all-start.7 = ((bf16[8,64,2048]{2,1,0:T(8,128)(2,1)}), bf16[8,64,2048]{2,1,0:T(8,128)(2,1)S(1)}, u32[]{:S(2)}, u32[]{:S(2)}) async-start(bf16[8,64,2048]{2,1,0:T(8,128)(2,1)} %bitcast.178), calls=%async_computation.7 | async-start | bytes 4194304 | tf_op jit(solution)/shard_map/all_to_all | solution.py:108
  341.2 34.3 %all-to-all-start.8 = ((bf16[8,64,2048]{2,1,0:T(8,128)(2,1)}), bf16[8,64,2048]{2,1,0:T(8,128)(2,1)}, u32[]{:S(2)}, u32[]{:S(2)}) async-start(bf16[8,64,2048]{2,1,0:T(8,128)(2,1)} %bitcast.177), calls=%async_computation.8 | async-start | bytes 4194304 | tf_op jit(solution)/shard_map/all_to_all | solution.py:108
Sparse Core Ops, SparseCore 0:
  10.2 86.4 all-gather.2
  98.3 113.5 all-gather.4

commit v6 on v3

--- a/solution.py
+++ b/solution.py
@@ -71,6 +71,7 @@
     per_owner = pages // owners
     stacked = jnp.stack([keys.reshape(tokens, width), values.reshape(tokens, width)], axis=0)
     stacked = stacked.reshape(2, pages, page_size, width).transpose(1, 0, 2, 3)
+    page_table, stacked = lax.optimization_barrier((page_table, stacked))
     order = jnp.argsort(page_table // pages, stable=True)
     outgoing = stacked[order].reshape(owners, per_owner, 2, page_size, width)
     outgoing_ids = page_table[order].reshape(owners, per_owner)
@@ -126,9 +127,11 @@
     query = rotate(projected[0].reshape(tok_group, local_heads, HD), position).astype(jnp.bfloat16)
     keys = rotate(projected[1].reshape(tok_group, local_heads, HD), position).astype(jnp.bfloat16)
     values = projected[2].reshape(tok_group, local_heads, HD).astype(jnp.bfloat16)
+    kv_cache = write_cache(keys, values, page_table)
     context = attend(query, keys, values, segment)
     attn_part = jnp.einsum("tr,dr->td", context, attn_w[3], preferred_element_type=jnp.float32)
-    attn_mine = sum_rows(attn_part.astype(jnp.bfloat16), "tensor")
+    attn_part, kv_cache = lax.optimization_barrier((attn_part.astype(jnp.bfloat16), kv_cache))
+    attn_mine = sum_rows(attn_part, "tensor")
     mid = (stream.astype(jnp.float32) + attn_mine).astype(jnp.bfloat16)
     normed2_mine = layer_norm(mid).astype(jnp.bfloat16)
     pieces = 2
@@ -142,7 +145,6 @@
         mlp_pieces.append(sum_rows(mlp_part.astype(jnp.bfloat16), "tensor"))
     mlp_mine = jnp.concatenate(mlp_pieces, axis=0)
     layer_out = (mid.astype(jnp.float32) + mlp_mine).astype(jnp.bfloat16)
-    kv_cache = write_cache(keys, values, page_table)
     return (layer_out, kv_cache)
 
 

time: 380 us -> 379 us (level)
  blocking collectives: 35.4 us -> 88.6 us
  waiting for transfers between devices: 177 us -> 132 us
  starting transfers between devices: 37.3 us -> 30.6 us
    all_to_all x0 -> x1, blocking collectives: none -> 57.7 us  [sum_rows(): lax.all_to_all(terms.reshape(count, terms.shape[0] // count, terms.shape[...]
    all_to_all x3 -> x2, waiting for transfers between devices: 84.5 us -> 43.1 us  [sum_rows(): lax.all_to_all(terms.reshape(count, terms.shape[0] // count, terms.shape[...]
    scatter x1, local copies, waits for them, and re-layouts: 9.1 us -> 2.5 us  [write_cache(): return empty.at[local].set(arrived.reshape(pages, 2, page_size, width))]
    all_to_all x3 -> x2, starting transfers between devices: 14.9 us -> 9.16 us  [sum_rows(): lax.all_to_all(terms.reshape(count, terms.shape[0] // count, terms.shape[...]
    all_to_all x1, blocking collectives: 35.4 us -> 30.8 us  [gather_rows(): gathered = lax.all_to_all(copies, axis_name, 0, 0, tiled=True)]
    unnamed x32 -> x40, local copies, waits for them, and re-layouts: 13.4 us -> 14.4 us
  transfers between devices with their start and end apart: 9 -> 8, of which waited for: 8 -> 6; matrix products, arithmetic and copies ran while one was open for 28% -> 27% of each run, Pallas kernels for 0% -> 0%
where the time goes in v6:
time: 379 us; the launch traced here: 378 us
  waiting for transfers between devices  132 us (35%)
  blocking collectives  88.6 us (23%)
  matrix products  49.8 us (13%)
  local copies, waits for them, and re-layouts  32.2 us (8%)
  starting transfers between devices  30.6 us (8%)
  other arithmetic  30.2 us (8%)
  between operations  14.5 us (4%)
    all_to_all x2, waiting for transfers between devices, gather_rows(): gathered = lax.all_to_all(copies, axis_name, 0, 0, tiled=True)  65.6 us
    all_to_all x1, blocking collectives, sum_rows(): lax.all_to_all(terms.reshape(count, terms.shape[0] // count, terms.shape[...  57.7 us
    all_to_all x2, waiting for transfers between devices, sum_rows(): lax.all_to_all(terms.reshape(count, terms.shape[0] // count, terms.shape[...  43.1 us
    all_to_all x1, blocking collectives, gather_rows(): gathered = lax.all_to_all(copies, axis_name, 0, 0, tiled=True)  30.8 us
    dot_general x2, matrix products, body(): jnp.einsum('td,cdf->ctf', rows, mlp_w[:2], preferred_element_type=jnp.flo...  15.3 us
    unnamed x40, local copies, waits for them, and re-layouts  14.4 us
    all_to_all x1, waiting for transfers between devices, write_cache(): lax.all_to_all(outgoing, 'dp', split_axis=0, concat_axis=0, tiled=True)  13.8 us
    dot_general x2, matrix products, body(): jnp.einsum('tf,df->td', hidden, mlp_w[2], preferred_element_type=jnp.floa...  12.3 us
  transfers between devices with their start and end apart: 8, of which 6 were waited for; matrix products, arithmetic and copies ran while one was open for 27% of the time, Pallas kernels for 0%

profile of v6, /device:TPU:1, one launch (start us, length us, event | category | flops | bytes accessed | tf_op | source)
XLA Modules:
  0.0 377.7 jit_solution(7025221537672854619)
XLA Ops:
  7.2 1.1 copy.29
  8.4 1.6 pad_maximum_fusion.3
  10.0 1.3 copy.40
  11.3 2.0 pad_maximum_fusion
  13.3 2.5 broadcast_in_dim.43
  15.8 8.3 %all-to-all-start = ((bf16[8,128,2048]{2,1,0:T(8,128)(2,1)}), bf16[8,128,2048]{2,1,0:T(8,128)(2,1)}, u32[]{:S(2)}, u32[]{:S(2)}) async-start(bf16[8,128,2048]{2,1,0:T(8,128)(2,1)} %broadcast_in_dim.43), calls=%async_computation | async-start | bytes 8388608 | tf_op jit(solution)/shard_map/all_to_all | solution.py:101
  24.5 1.4 fusion.23
  25.9 1.9 multiply_cosine_fusion
  27.8 51.2 %all-to-all-done = bf16[8,128,2048]{2,1,0:T(8,128)(2,1)} async-done(((bf16[8,128,2048]{2,1,0:T(8,128)(2,1)}), bf16[8,128,2048]{2,1,0:T(8,128)(2,1)}, u32[]{:S(2)}, u32[]{:S(2)}) %all-to-all-start) | async-done | bytes 4194336 | tf_op jit(solution)/shard_map/all_to_all | solution.py:101
  79.0 2.8 convert_reduce_fusion.1
  81.8 3.4 multiply_reduce_fusion
  85.2 4.2 %fusion.3 = bf16[1024,2048]{1,0:T(8,128)(2,1)} fusion(bf16[8,128,2048]{2,1,0:T(8,128)(2,1)} %all-to-all-done, f32[1024]{0:T(1024)S(1)} %rsqrt_bitcast_fusion, f32[1024]{0:T(1024)S(1)} %get-tuple-element.30), kind=kLoop, calls=%fused_computation.7 | loop fusion | flops 8388608 | bytes 8396800 | tf_op jit(solution)/shard_map/convert_element_type | solution.py:124
  89.4 9.2 %all-gather.3.cloned.1.call-done = bf16[4,2048,256]{1,2,0:T(8,128)(2,1)} async-done(((bf16[4,128,256]{1,2,0:T(8,128)(2,1)}), bf16[4,2048,256]{1,2,0:T(8,128)(2,1)}) %all-gather.3.cloned.1.call-update) | async-done | bytes 4194320 | tf_op jit(solution)/shard_map/all_gather | solution.py:117
  98.7 6.2 %fusion.26 = f32[3,1024,256]{1,2,0:T(8,128)S(1)} fusion(bf16[4,2048,256]{1,2,0:T(8,128)(2,1)} %all-gather.3.cloned.1.call-done, bf16[1024,2048]{1,0:T(8,128)(2,1)} %fusion.3), kind=kOutput, calls=%fused_computation.42 | convolution fusion | flops 3221225472 | bytes 11534336 | tf_op jit(solution)/shard_map/td,cdf->ctf/dot_general | solution.py:126
  104.9 0.9 slice.171
  106.0 1.0 fusion.78
  107.0 1.4 copy.44
  108.4 2.4 copy.45
  110.8 1.5 multiply_subtract_fusion
  112.3 0.3 maximum_convert_fusion
  112.6 1.3 copy.35
  113.9 2.2 convert_element_type.111
  116.1 1.0 copy.36
  117.1 1.3 maximum_bitcast_fusion
  118.4 2.0 sort.17
  120.5 0.8 gather_fusion
  121.3 0.7 all_to_all.28
  122.0 3.6 all-to-all-start.1
  125.6 1.0 fusion.79
  126.6 1.4 copy.42
  128.0 2.5 copy.43
  130.5 1.6 subtract_convert_fusion
  132.1 0.8 copy-done.11
  133.1 0.5 fusion.56
  133.6 1.3 copy-done.10
  134.9 1.1 fusion.83
  136.3 5.1 %fusion.82 = (f32[2,512]{1,0:T(2,128)S(1)}, bf16[2,512,1024]{2,1,0:T(8,128)(2,1)}) fusion(pred[512,1024]{1,0:T(8,128)(4,1)} %fusion.23, bf16[1024,2,128]{2,0,1:T(8,128)(2,1)S(1)} %copy-done.6, bf16[1024,2,64]{2,0,1:T(8,128)(2,1)S(1)} %copy-done.14, bf16[1024,2,64]{2,0,1:T(8,128)(2,1)S(1)} %copy-done.12), kind=kOutput, calls=%fused_computation.115 | convolution fusion | flops 545260544 | bytes 3674112 | tf_op jit(solution)/shard_map/sub | solution.py:53
  141.4 2.4 fusion.39
  143.9 1.6 gather_fusion.1
  145.5 5.6 %all-to-all-start.2 = ((bf16[16,4,2,16,256]{4,3,2,1,0:T(8,128)(2,1)}), bf16[16,4,2,16,256]{4,3,2,1,0:T(8,128)(2,1)S(1)}, u32[]{:S(2)}, u32[]{:S(2)}) async-start(bf16[16,4,2,16,256]{4,3,2,1,0:T(8,128)(2,1)} %bitcast.23), calls=%async_computation.2 | async-start | bytes 2097152 | tf_op jit(solution)/shard_map/all_to_all | solution.py:79
  151.1 3.3 fusion.38
  154.5 4.6 %convolution_convert_fusion = bf16[1024,2048]{1,0:T(8,128)(2,1)} fusion(bf16[1024,256]{0,1:T(8,128)(2,1)S(1)} %bitcast.99, bf16[4,2048,256]{1,2,0:T(8,128)(2,1)} %all-gather.3.cloned.1.call-done), kind=kOutput, calls=%fused_computation.19 | convolution fusion | flops 1075838976 | bytes 5767168 | tf_op jit(solution)/shard_map/tr,dr->td/dot_general | solution.py:132
  159.2 13.8 %all-to-all-done.2 = bf16[16,4,2,16,256]{4,3,2,1,0:T(8,128)(2,1)S(1)} async-done(((bf16[16,4,2,16,256]{4,3,2,1,0:T(8,128)(2,1)}), bf16[16,4,2,16,256]{4,3,2,1,0:T(8,128)(2,1)S(1)}, u32[]{:S(2)}, u32[]{:S(2)}) %all-to-all-start.2) | async-done | bytes 1048608 | tf_op jit(solution)/shard_map/all_to_all | solution.py:79
  173.1 2.5 scatter_fusion
  175.7 57.7 %all_to_all.44 = bf16[8,128,2048]{2,1,0:T(8,128)(2,1)S(1)} all-to-all(bf16[8,128,2048]{2,1,0:T(8,128)(2,1)} %bitcast.94), channel_id=1, replica_groups=mesh['dp'=16,'tensor'=8] {'tensor'}, dimensions={0} | all-to-all | bytes 8388608 | tf_op jit(solution)/shard_map/all_to_all | solution.py:107
  233.4 0.7 convert_reduce_fusion
  234.1 0.3 copy-done.8
  235.0 0.3 fusion.43
  235.6 30.8 %all_to_all.45 = bf16[8,64,2048]{2,1,0:T(8,128)(2,1)} all-to-all(bf16[8,64,2048]{2,1,0:T(8,128)(2,1)S(1)} %broadcast_in_dim.55), channel_id=1, replica_groups=mesh['dp'=16,'tensor'=8] {'tensor'}, dimensions={0} | all-to-all | bytes 4194304 | tf_op jit(solution)/shard_map/all_to_all | solution.py:101
  266.4 1.6 broadcast_in_dim.56
  268.0 3.8 %all-to-all-start.6 = ((bf16[8,64,2048]{2,1,0:T(8,128)(2,1)}), bf16[8,64,2048]{2,1,0:T(8,128)(2,1)S(1)}, u32[]{:S(2)}, u32[]{:S(2)}) async-start(bf16[8,64,2048]{2,1,0:T(8,128)(2,1)} %broadcast_in_dim.56), calls=%async_computation.6 | async-start | bytes 4194304 | tf_op jit(solution)/shard_map/all_to_all | solution.py:101
  271.9 7.6 %convolution_bitcast_fusion.1 = f32[2,512,1024]{1,2,0:T(8,128)S(1)} fusion(bf16[3,2048,1024]{1,2,0:T(8,128)(2,1)} %all-gather.5.cloned.1.call-done, bf16[512,2048,1]{1,0,2:T(8,128)(2,1)} %bitcast.102), kind=kOutput, calls=%fused_computation.26 | convolution fusion | flops 4294967296 | bytes 18874368 | tf_op jit(solution)/shard_map/td,cdf->ctf/dot_general | solution.py:142
  279.5 6.2 %fusion.12 = bf16[512,2048]{1,0:T(8,128)(2,1)} fusion(bf16[3,2048,1024]{1,2,0:T(8,128)(2,1)} %all-gather.5.cloned.1.call-done, f32[2,512,1024]{1,2,0:T(8,128)S(1)} %convolution_bitcast_fusion.1), kind=kOutput, calls=%fused_computation.23 | convolution fusion | flops 2151677952 | bytes 10485760 | tf_op jit(solution)/shard_map/tf,df->td/dot_general | solution.py:144
  285.7 14.5 %all-to-all-done.6 = bf16[8,64,2048]{2,1,0:T(8,128)(2,1)S(1)} async-done(((bf16[8,64,2048]{2,1,0:T(8,128)(2,1)}), bf16[8,64,2048]{2,1,0:T(8,128)(2,1)S(1)}, u32[]{:S(2)}, u32[]{:S(2)}) %all-to-all-start.6) | async-done | bytes 2097184 | tf_op jit(solution)/shard_map/all_to_all | solution.py:101
  300.2 1.3 copy-done.9
  301.5 3.6 all-to-all-start.5
  305.1 7.6 %convolution_bitcast_fusion = f32[2,512,1024]{1,2,0:T(8,128)S(1)} fusion(bf16[3,2048,1024]{1,2,0:T(8,128)(2,1)} %all-gather.5.cloned.1.call-done, bf16[512,2048,1]{1,0,2:T(8,128)(2,1)} %bitcast.100), kind=kOutput, calls=%fused_computation.25 | convolution fusion | flops 4294967296 | bytes 18874368 | tf_op jit(solution)/shard_map/td,cdf->ctf/dot_general | solution.py:142
  312.7 6.2 %fusion.13 = bf16[512,2048]{1,0:T(8,128)(2,1)} fusion(bf16[3,2048,1024]{1,2,0:T(8,128)(2,1)} %all-gather.5.cloned.1.call-done, f32[2,512,1024]{1,2,0:T(8,128)S(1)} %convolution_bitcast_fusion), kind=kOutput, calls=%fused_computation.24 | convolution fusion | flops 2151677952 | bytes 10485760 | tf_op jit(solution)/shard_map/tf,df->td/dot_general | solution.py:144
  318.9 14.7 %all-to-all-done.5 = bf16[8,64,2048]{2,1,0:T(8,128)(2,1)S(1)} async-done(((bf16[8,64,2048]{2,1,0:T(8,128)(2,1)}), bf16[8,64,2048]{2,1,0:T(8,128)(2,1)S(1)}, u32[]{:S(2)}, u32[]{:S(2)}) %all-to-all-start.5) | async-done | bytes 2097184 | tf_op jit(solution)/shard_map/all_to_all | solution.py:107
  333.6 5.6 %all-to-all-start.7 = ((bf16[8,64,2048]{2,1,0:T(8,128)(2,1)}), bf16[8,64,2048]{2,1,0:T(8,128)(2,1)}, u32[]{:S(2)}, u32[]{:S(2)}) async-start(bf16[8,64,2048]{2,1,0:T(8,128)(2,1)} %bitcast.103), calls=%async_computation.7 | async-start | bytes 4194304 | tf_op jit(solution)/shard_map/all_to_all | solution.py:107
  339.2 0.3 convert_reduce_fusion.3
  339.6 28.4 %all-to-all-done.7 = bf16[8,64,2048]{2,1,0:T(8,128)(2,1)} async-done(((bf16[8,64,2048]{2,1,0:T(8,128)(2,1)}), bf16[8,64,2048]{2,1,0:T(8,128)(2,1)}, u32[]{:S(2)}, u32[]{:S(2)}) %all-to-all-start.7) | async-done | bytes 2097184 | tf_op jit(solution)/shard_map/all_to_all | solution.py:107
  367.9 2.0 convert_reduce_fusion.2
  369.9 0.9 fusion.44
  (63 shorter events, 2.3 us)
Async XLA Ops:
  7.2 6.1 %copy-start.7 = (bf16[128,2048]{1,0:T(8,128)(2,1)S(1)}, bf16[128,2048]{1,0:T(8,128)(2,1)}, u32[]{:S(2)}) copy-start(bf16[128,2048]{1,0:T(8,128)(2,1)} %param.8) | copy-start | bytes 1572868
  7.2 91.5 %all-gather.3.cloned.1.call-start = ((), (), s32[]{:S(2)}) async-start(), calls=%async_computation.8 | async-start | bytes 4456448 | tf_op jit(solution)/shard_map/all_gather | solution.py:117
  10.0 261.9 %all-gather.5.cloned.1.call-start = ((), (), s32[]{:S(2)}) async-start(), calls=%async_computation.9 | async-start | bytes 13369344 | tf_op jit(solution)/shard_map/all_gather | solution.py:120
  15.8 8.3 %copy-start.16 = (s32[1024]{0:T(1024)S(1)}, s32[1024]{0:T(1024)}, u32[]{:S(2)}) copy-start(s32[1024]{0:T(1024)} %param.10) | copy-start | bytes 12292
  15.8 8.4 %copy-start.15 = (s32[1024]{0:T(1024)S(1)}, s32[1024]{0:T(1024)}, u32[]{:S(2)}) copy-start(s32[1024]{0:T(1024)} %param.9) | copy-start | bytes 12292
  15.8 63.1 %all-to-all-start = ((bf16[8,128,2048]{2,1,0:T(8,128)(2,1)}), bf16[8,128,2048]{2,1,0:T(8,128)(2,1)}, u32[]{:S(2)}, u32[]{:S(2)}) async-start(bf16[8,128,2048]{2,1,0:T(8,128)(2,1)} %broadcast_in_dim.43), calls=%async_computation | async-start | bytes 8388608 | tf_op jit(solution)/shard_map/all_to_all | solution.py:101
  112.3 3.8 %copy-start.2 = (bf16[1,1024,256]{1,2,0:T(8,128)(2,1)S(1)}, bf16[1,1024,256]{1,2,0:T(8,128)(2,1)}, u32[]{:S(2)}) copy-start(bf16[1,1024,256]{1,2,0:T(8,128)(2,1)} %slice.171) | copy-start | bytes 1572868
  112.3 6.1 %copy-start = (s32[64]{0:T(128)S(1)}, s32[64]{0:T(128)}, u32[]{:S(2)}) copy-start(s32[64]{0:T(128)} %param.15) | copy-start | bytes 772
  112.6 4.5 %copy-start.4 = (bf16[1024,2,128]{2,0,1:T(8,128)(2,1)}, bf16[1024,2,128]{2,0,1:T(8,128)(2,1)S(1)}, u32[]{:S(2)}) copy-start(bf16[1024,2,128]{2,0,1:T(8,128)(2,1)S(1)} %maximum_convert_fusion) | copy-start | bytes 1572868
  122.0 23.5 %all-to-all-start.1 = ((s32[16,1,4]{2,1,0:T(1,128)}), s32[16,1,4]{2,1,0:T(1,128)S(1)}, u32[]{:S(2)}, u32[]{:S(2)}) async-start(s32[16,1,4]{2,1,0:T(1,128)} %bitcast.21), calls=%async_computation.1 | async-start | bytes 16384 | tf_op jit(solution)/shard_map/all_to_all | solution.py:80
  130.5 2.6 copy-start.5
  132.1 0.8 copy-start.11
  132.1 1.0 copy-start.13
  133.6 1.4 copy-start.10
  134.9 1.1 copy-start.6
  134.9 1.2 copy-start.12
  134.9 1.4 copy-start.14
  136.3 5.1 %copy-start.3 = (bf16[1,1024,256]{1,2,0:T(8,128)(2,1)S(1)}, bf16[1,1024,256]{1,2,0:T(8,128)(2,1)}, u32[]{:S(2)}) copy-start(bf16[1,1024,256]{1,2,0:T(8,128)(2,1)} %slice.171) | copy-start | bytes 1572868
  145.5 27.5 %all-to-all-start.2 = ((bf16[16,4,2,16,256]{4,3,2,1,0:T(8,128)(2,1)}), bf16[16,4,2,16,256]{4,3,2,1,0:T(8,128)(2,1)S(1)}, u32[]{:S(2)}, u32[]{:S(2)}) async-start(bf16[16,4,2,16,256]{4,3,2,1,0:T(8,128)(2,1)} %bitcast.23), calls=%async_computation.2 | async-start | bytes 2097152 | tf_op jit(solution)/shard_map/all_to_all | solution.py:79
  175.6 57.8 %copy-start.1 = (bf16[64,2,16,256]{3,2,1,0:T(8,128)(2,1)}, bf16[64,2,16,256]{3,2,1,0:T(8,128)(2,1)S(1)}, u32[]{:S(2)}) copy-start(bf16[64,2,16,256]{3,2,1,0:T(8,128)(2,1)S(1)} %scatter_fusion) | copy-start | bytes 3145732
  233.4 1.0 copy-start.8
  268.0 32.2 %all-to-all-start.6 = ((bf16[8,64,2048]{2,1,0:T(8,128)(2,1)}), bf16[8,64,2048]{2,1,0:T(8,128)(2,1)S(1)}, u32[]{:S(2)}, u32[]{:S(2)}) async-start(bf16[8,64,2048]{2,1,0:T(8,128)(2,1)} %broadcast_in_dim.56), calls=%async_computation.6 | async-start | bytes 4194304 | tf_op jit(solution)/shard_map/all_to_all | solution.py:101
  300.2 1.3 copy-start.9
  301.5 32.2 %all-to-all-start.5 = ((bf16[8,64,2048]{2,1,0:T(8,128)(2,1)}), bf16[8,64,2048]{2,1,0:T(8,128)(2,1)S(1)}, u32[]{:S(2)}, u32[]{:S(2)}) async-start(bf16[8,64,2048]{2,1,0:T(8,128)(2,1)} %bitcast.101), calls=%async_computation.5 | async-start | bytes 4194304 | tf_op jit(solution)/shard_map/all_to_all | solution.py:107
  333.6 34.3 %all-to-all-start.7 = ((bf16[8,64,2048]{2,1,0:T(8,128)(2,1)}), bf16[8,64,2048]{2,1,0:T(8,128)(2,1)}, u32[]{:S(2)}, u32[]{:S(2)}) async-start(bf16[8,64,2048]{2,1,0:T(8,128)(2,1)} %bitcast.103), calls=%async_computation.7 | async-start | bytes 4194304 | tf_op jit(solution)/shard_map/all_to_all | solution.py:107
Sparse Core Ops, SparseCore 0:
  10.2 88.4 all-gather.2
  100.3 86.8 all-gather.4

commit v7 on v5

--- a/solution.py
+++ b/solution.py
@@ -71,16 +71,19 @@
     page_size = tokens // pages
     owners = lax.axis_size("dp")
     per_owner = pages // owners
+    me = lax.axis_index("dp")
     stacked = jnp.stack([keys.reshape(tokens, width), values.reshape(tokens, width)], axis=0)
     stacked = stacked.reshape(2, pages, page_size, width).transpose(1, 0, 2, 3)
     order = jnp.argsort(page_table // pages, stable=True)
     outgoing = stacked[order].reshape(owners, per_owner, 2, page_size, width)
-    outgoing_ids = page_table[order].reshape(owners, per_owner)
-    arrived, arrived_ids = (
-        lax.all_to_all(outgoing, "dp", split_axis=0, concat_axis=0, tiled=True),
-        lax.all_to_all(outgoing_ids, "dp", split_axis=0, concat_axis=0, tiled=True),
-    )
-    local = (arrived_ids - lax.axis_index("dp") * pages).reshape(-1)
+    arrived = lax.all_to_all(outgoing, "dp", split_axis=0, concat_axis=0, tiled=True)
+    every_table = lax.all_gather(page_table, "dp", axis=0, tiled=False)
+    every_order = jnp.argsort(every_table // pages, axis=1, stable=True)
+    every_sorted = jnp.take_along_axis(every_table, every_order, axis=1)
+    arrived_ids = lax.dynamic_index_in_dim(
+        every_sorted.reshape(owners, owners, per_owner), me, 1, keepdims=False
+    )
+    local = (arrived_ids - me * pages).reshape(-1)
     empty = jnp.zeros((pages, 2, page_size, width), jnp.bfloat16)
     return empty.at[local].set(arrived.reshape(pages, 2, page_size, width))
 

time: 390 us -> 392 us (level)
  waiting for transfers between devices: 155 us -> 101 us
  blocking collectives: 41.6 us -> 89.2 us
  local copies, waits for them, and re-layouts: 34.3 us -> 41.9 us
    unnamed x0 -> x1, blocking collectives: none -> 59.1 us
    all_to_all x3, waiting for transfers between devices: 84 us -> 34.2 us  [gather_rows(): gathered = lax.all_to_all(copies, axis_name, 0, 0, tiled=True)]
    all_to_all x1 -> x0, blocking collectives: 12.8 us -> none  [write_cache(): lax.all_to_all(outgoing_ids, 'dp', split_axis=0, concat_axis=0, tiled=True)]
    gather x1 -> x3, local copies, waits for them, and re-layouts: 0.78 us -> 7.21 us  [write_cache(): every_sorted = jnp.take_along_axis(every_table, every_order, axis=1)]
    unnamed x58 -> x63, local copies, waits for them, and re-layouts: 13.6 us -> 14.4 us
  transfers between devices with their start and end apart: 9 -> 9, of which waited for: 7 -> 6; matrix products, arithmetic and copies ran while one was open for 32% -> 34% of each run, Pallas kernels for 0% -> 0%
where the time goes in v7:
time: 392 us; the launch traced here: 389 us
  waiting for transfers between devices  101 us (26%)
  blocking collectives  89.2 us (23%)
  matrix products  58.6 us (15%)
  starting transfers between devices  42 us (11%)
  local copies, waits for them, and re-layouts  41.9 us (11%)
  other arithmetic  41.2 us (11%)
  between operations  15.4 us (4%)
    all_to_all x3, waiting for transfers between devices, sum_rows(): lax.all_to_all(terms.reshape(count, terms.shape[0] // count, terms.shape[...  65.5 us
    unnamed x1, blocking collectives  59.1 us
    all_to_all x3, waiting for transfers between devices, gather_rows(): gathered = lax.all_to_all(copies, axis_name, 0, 0, tiled=True)  34.2 us
    all_to_all x1, blocking collectives, sum_rows(): lax.all_to_all(terms.reshape(count, terms.shape[0] // count, terms.shape[...  30.1 us
    all_to_all x3, starting transfers between devices, gather_rows(): gathered = lax.all_to_all(copies, axis_name, 0, 0, tiled=True)  17.7 us
    all_to_all x3, starting transfers between devices, sum_rows(): lax.all_to_all(terms.reshape(count, terms.shape[0] // count, terms.shape[...  17.6 us
    dot_general x2, matrix products, mlp_of(): jnp.einsum('td,cdf->ctf', rows, mlp_w[:2], preferred_element_type=jnp.flo...  15.3 us
    unnamed x63, local copies, waits for them, and re-layouts  14.4 us
  transfers between devices with their start and end apart: 9, of which 6 were waited for; matrix products, arithmetic and copies ran while one was open for 34% of the time, Pallas kernels for 0%

profile of v7, /device:TPU:1, one launch (start us, length us, event | category | flops | bytes accessed | tf_op | source)
XLA Modules:
  0.0 389.4 jit_solution(15022380428198457462)
XLA Ops:
  7.2 1.1 copy.25
  8.4 1.6 pad_maximum_fusion.2
  10.0 1.3 copy.40
  11.3 2.0 pad_maximum_fusion
  13.3 2.5 broadcast_in_dim.210
  15.9 8.3 %all-to-all-start = ((bf16[8,128,2048]{2,1,0:T(8,128)(2,1)}), bf16[8,128,2048]{2,1,0:T(8,128)(2,1)}, u32[]{:S(2)}, u32[]{:S(2)}) async-start(bf16[8,128,2048]{2,1,0:T(8,128)(2,1)} %broadcast_in_dim.210), calls=%async_computation | async-start | bytes 8388608 | tf_op jit(solution)/shard_map/all_to_all | solution.py:105
  26.4 59.1 %all-reduce = s32[1024]{0:T(1024)S(1)} all-reduce(s32[1024]{0:T(1024)S(1)} %dynamic-update-slice), channel_id=2, replica_groups=mesh['dp'=16,'tensor'=8] {'dp'}, use_global_device_ids=true, to_apply=%add | all-reduce | flops 1024 | bytes 8192
  87.0 7.1 %gather_fusion.1 = s32[1024]{0:T(1024)S(1)} fusion(s32[16,64]{1,0:T(8,128)S(1)} %reshape.672, s32[1024]{0:T(1024)S(1)} %reshape.658), kind=kCustom, calls=%fused_computation.1 | custom fusion | bytes 16384 | tf_op jit(solution)/shard_map/jit(take_along_axis)/gather | solution.py:82
  94.4 2.0 sort.35
  99.1 1.1 fusion.95
  100.2 1.9 multiply_cosine_fusion
  102.1 2.8 convert_reduce_fusion
  104.9 3.4 multiply_reduce_fusion
  108.3 4.2 %fusion.9 = bf16[1024,2048]{1,0:T(8,128)(2,1)} fusion(bf16[8,128,2048]{2,1,0:T(8,128)(2,1)} %all-to-all-done, f32[1024]{0:T(1024)S(1)} %rsqrt_bitcast_fusion, f32[1024]{0:T(1024)S(1)} %get-tuple-element.54), kind=kLoop, calls=%fused_computation.13 | loop fusion | flops 8388608 | bytes 8396800 | tf_op jit(solution)/shard_map/convert_element_type | solution.py:147
  112.5 6.2 %fusion.20 = f32[3,1024,256]{1,2,0:T(8,128)S(1)} fusion(bf16[4,2048,256]{1,2,0:T(8,128)(2,1)} %all-gather.4.cloned.1.call-done, bf16[1024,2048]{1,0:T(8,128)(2,1)} %fusion.9), kind=kOutput, calls=%fused_computation.37 | convolution fusion | flops 3221225472 | bytes 11534336 | tf_op jit(solution)/shard_map/td,cdf->ctf/dot_general | solution.py:149
  118.8 1.7 copy-done.1
  122.2 2.7 fusion.224
  125.8 1.4 copy.43
  127.2 1.4 copy.44
  128.5 2.1 fusion.226
  130.7 2.4 copy.41
  133.0 1.3 copy.42
  134.3 1.5 multiply_subtract_fusion
  136.7 1.1 convert_element_type.174
  137.8 1.5 maximum_bitcast_fusion
  139.3 1.6 gather_fusion
  140.9 6.6 %all-to-all-start.1 = ((bf16[16,4,2,16,256]{4,3,2,1,0:T(8,128)(2,1)}), bf16[16,4,2,16,256]{4,3,2,1,0:T(8,128)(2,1)S(1)}, u32[]{:S(2)}, u32[]{:S(2)}) async-start(bf16[16,4,2,16,256]{4,3,2,1,0:T(8,128)(2,1)} %bitcast.40), calls=%async_computation.1 | async-start | bytes 2097152 | tf_op jit(solution)/shard_map/all_to_all | solution.py:79
  147.5 1.9 subtract_convert_fusion
  152.0 1.8 fusion.70
  156.0 1.3 fusion.232
  157.3 1.4 fusion.231
  158.7 2.6 fusion.72
  161.3 2.1 fusion.68
  163.4 3.6 convolution_convert_fusion.1
  167.0 1.5 all-to-all-done.1
  168.6 2.5 scatter_fusion
  172.1 8.5 %all-to-all-start.2 = ((bf16[8,64,2048]{2,1,0:T(8,128)(2,1)}), bf16[8,64,2048]{2,1,0:T(8,128)(2,1)S(1)}, u32[]{:S(2)}, u32[]{:S(2)}) async-start(bf16[8,64,2048]{2,1,0:T(8,128)(2,1)} %bitcast.182), calls=%async_computation.2 | async-start | bytes 4194304 | tf_op jit(solution)/shard_map/all_to_all | solution.py:111
  180.5 1.1 convolution_multiply_fusion.2
  181.7 1.5 fusion.228
  183.1 1.7 convolution_multiply_fusion.6
  184.9 1.9 convolution_multiply_fusion.4
  186.7 22.4 %all-to-all-done.2 = bf16[8,64,2048]{2,1,0:T(8,128)(2,1)S(1)} async-done(((bf16[8,64,2048]{2,1,0:T(8,128)(2,1)}), bf16[8,64,2048]{2,1,0:T(8,128)(2,1)S(1)}, u32[]{:S(2)}, u32[]{:S(2)}) %all-to-all-start.2) | async-done | bytes 2097184 | tf_op jit(solution)/shard_map/all_to_all | solution.py:111
  209.6 1.2 convert_reduce_fusion.6
  211.2 1.6 broadcast_in_dim.227
  212.8 5.6 %all-to-all-start.3 = ((bf16[8,64,2048]{2,1,0:T(8,128)(2,1)}), bf16[8,64,2048]{2,1,0:T(8,128)(2,1)}, u32[]{:S(2)}, u32[]{:S(2)}) async-start(bf16[8,64,2048]{2,1,0:T(8,128)(2,1)} %broadcast_in_dim.227), calls=%async_computation.3 | async-start | bytes 4194304 | tf_op jit(solution)/shard_map/all_to_all | solution.py:105
  219.6 1.4 fusion.69
  221.0 2.0 fusion.73
  222.9 1.9 fusion.74
  225.3 2.0 convolution_convert_fusion
  227.3 19.8 %all-to-all-done.3 = bf16[8,64,2048]{2,1,0:T(8,128)(2,1)} async-done(((bf16[8,64,2048]{2,1,0:T(8,128)(2,1)}), bf16[8,64,2048]{2,1,0:T(8,128)(2,1)}, u32[]{:S(2)}, u32[]{:S(2)}) %all-to-all-start.3) | async-done | bytes 2097184 | tf_op jit(solution)/shard_map/all_to_all | solution.py:105
  247.1 30.1 %all_to_all.40 = bf16[8,64,2048]{2,1,0:T(8,128)(2,1)S(1)} all-to-all(bf16[8,64,2048]{2,1,0:T(8,128)(2,1)S(1)} %bitcast.186), channel_id=1, replica_groups=mesh['dp'=16,'tensor'=8] {'tensor'}, dimensions={0} | all-to-all | bytes 4194304 | tf_op jit(solution)/shard_map/all_to_all | solution.py:111
  278.1 1.6 broadcast_in_dim.228
  279.7 3.8 all-to-all-start.5
  283.6 7.6 %convolution_bitcast_fusion.1 = f32[2,512,1024]{1,2,0:T(8,128)S(1)} fusion(bf16[3,2048,1024]{1,2,0:T(8,128)(2,1)} %all-gather.6.cloned.1.call-done, bf16[512,2048]{1,0:T(8,128)(2,1)} %bitcast.61), kind=kOutput, calls=%fused_computation.30 | convolution fusion | flops 4294967296 | bytes 18874368 | tf_op jit(solution)/shard_map/td,cdf->ctf/dot_general | solution.py:188
  291.2 6.2 %fusion.14 = bf16[512,2048]{1,0:T(8,128)(2,1)} fusion(bf16[3,2048,1024]{1,2,0:T(8,128)(2,1)} %all-gather.6.cloned.1.call-done, f32[2,512,1024]{1,2,0:T(8,128)S(1)} %convolution_bitcast_fusion.1), kind=kOutput, calls=%fused_computation.25 | convolution fusion | flops 2151677952 | bytes 10485760 | tf_op jit(solution)/shard_map/tf,df->td/dot_general | solution.py:190
  297.4 14.5 %all-to-all-done.5 = bf16[8,64,2048]{2,1,0:T(8,128)(2,1)S(1)} async-done(((bf16[8,64,2048]{2,1,0:T(8,128)(2,1)}), bf16[8,64,2048]{2,1,0:T(8,128)(2,1)S(1)}, u32[]{:S(2)}, u32[]{:S(2)}) %all-to-all-start.5) | async-done | bytes 2097184 | tf_op jit(solution)/shard_map/all_to_all | solution.py:105
  311.9 1.3 copy-done.2
  313.2 3.6 all-to-all-start.6
  316.8 7.6 %convolution_bitcast_fusion = f32[2,512,1024]{1,2,0:T(8,128)S(1)} fusion(bf16[3,2048,1024]{1,2,0:T(8,128)(2,1)} %all-gather.6.cloned.1.call-done, bf16[512,2048]{1,0:T(8,128)(2,1)} %bitcast.183), kind=kOutput, calls=%fused_computation.29 | convolution fusion | flops 4294967296 | bytes 18874368 | tf_op jit(solution)/shard_map/td,cdf->ctf/dot_general | solution.py:188
  324.5 6.2 %fusion.15 = bf16[512,2048]{1,0:T(8,128)(2,1)} fusion(bf16[3,2048,1024]{1,2,0:T(8,128)(2,1)} %all-gather.6.cloned.1.call-done, f32[2,512,1024]{1,2,0:T(8,128)S(1)} %convolution_bitcast_fusion), kind=kOutput, calls=%fused_computation.26 | convolution fusion | flops 2151677952 | bytes 10485760 | tf_op jit(solution)/shard_map/tf,df->td/dot_general | solution.py:190
  330.6 14.7 %all-to-all-done.6 = bf16[8,64,2048]{2,1,0:T(8,128)(2,1)S(1)} async-done(((bf16[8,64,2048]{2,1,0:T(8,128)(2,1)}), bf16[8,64,2048]{2,1,0:T(8,128)(2,1)S(1)}, u32[]{:S(2)}, u32[]{:S(2)}) %all-to-all-start.6) | async-done | bytes 2097184 | tf_op jit(solution)/shard_map/all_to_all | solution.py:111
  345.4 5.6 %all-to-all-start.7 = ((bf16[8,64,2048]{2,1,0:T(8,128)(2,1)}), bf16[8,64,2048]{2,1,0:T(8,128)(2,1)}, u32[]{:S(2)}, u32[]{:S(2)}) async-start(bf16[8,64,2048]{2,1,0:T(8,128)(2,1)} %bitcast.184), calls=%async_computation.7 | async-start | bytes 4194304 | tf_op jit(solution)/shard_map/all_to_all | solution.py:111
  351.3 28.3 %all-to-all-done.7 = bf16[8,64,2048]{2,1,0:T(8,128)(2,1)} async-done(((bf16[8,64,2048]{2,1,0:T(8,128)(2,1)}), bf16[8,64,2048]{2,1,0:T(8,128)(2,1)}, u32[]{:S(2)}, u32[]{:S(2)}) %all-to-all-start.7) | async-done | bytes 2097184 | tf_op jit(solution)/shard_map/all_to_all | solution.py:111
  379.6 2.0 convert_reduce_fusion.1
  (139 shorter events, 20.1 us)
Async XLA Ops:
  7.2 6.1 %copy-start.3 = (bf16[128,2048]{1,0:T(8,128)(2,1)S(1)}, bf16[128,2048]{1,0:T(8,128)(2,1)}, u32[]{:S(2)}) copy-start(bf16[128,2048]{1,0:T(8,128)(2,1)} %param.16) | copy-start | bytes 1572868
  7.2 105.4 %all-gather.4.cloned.1.call-start = ((), (), s32[]{:S(2)}) async-start(), calls=%async_computation.8 | async-start | bytes 4456448 | tf_op jit(solution)/shard_map/all_gather | solution.py:140
  10.0 273.6 %all-gather.6.cloned.1.call-start = ((), (), s32[]{:S(2)}) async-start(), calls=%async_computation.9 | async-start | bytes 13369344 | tf_op jit(solution)/shard_map/all_gather | solution.py:143
  15.8 8.3 %copy-start.13 = (s32[1024]{0:T(1024)S(1)}, s32[1024]{0:T(1024)}, u32[]{:S(2)}) copy-start(s32[1024]{0:T(1024)} %param.17) | copy-start | bytes 12292
  15.8 8.4 %copy-start.15 = (s32[1024]{0:T(1024)S(1)}, s32[1024]{0:T(1024)}, u32[]{:S(2)}) copy-start(s32[1024]{0:T(1024)} %param.18) | copy-start | bytes 12292
  15.8 9.1 %copy-start.26 = (u32[128]{0:T(128)S(1)}, u32[128]{0:T(128)}, u32[]{:S(2)}) copy-start(u32[128]{0:T(128)} %constant.127) | copy-start | bytes 1540
  15.8 10.3 %copy-start.24 = (s32[64]{0:T(128)S(1)}, s32[64]{0:T(128)}, u32[]{:S(2)}) copy-start(s32[64]{0:T(128)} %param.23) | copy-start | bytes 772
  15.9 86.2 %all-to-all-start = ((bf16[8,128,2048]{2,1,0:T(8,128)(2,1)}), bf16[8,128,2048]{2,1,0:T(8,128)(2,1)}, u32[]{:S(2)}, u32[]{:S(2)}) async-start(bf16[8,128,2048]{2,1,0:T(8,128)(2,1)} %broadcast_in_dim.210), calls=%async_computation | async-start | bytes 8388608 | tf_op jit(solution)/shard_map/all_to_all | solution.py:105
  86.9 9.6 %slice-start = ((s32[1024]{0:T(1024)}), s32[256]{0:T(256)S(1)}, s32[]{:S(2)}) async-start(s32[1024]{0:T(1024)} %param.17), calls=%async_computation.10 | async-start | bytes 2048 | tf_op jit(solution)/shard_map/slice | solution.py:172
  86.9 9.6 %copy-start.22 = (s32[128]{0:T(128)S(1)}, s32[128]{0:T(128)}, u32[]{:S(2)}) copy-start(s32[128]{0:T(128)} %constant.104.clone) | copy-start | bytes 1540
  86.9 9.6 %copy-start.23 = (s32[128]{0:T(128)S(1)}, s32[128]{0:T(128)}, u32[]{:S(2)}) copy-start(s32[128]{0:T(128)} %constant.108.clone) | copy-start | bytes 1540
  86.9 10.4 %slice-start.1 = ((s32[1024]{0:T(1024)}), s32[512]{0:T(512)S(1)}, s32[]{:S(2)}) async-start(s32[1024]{0:T(1024)} %param.17), calls=%async_computation.11 | async-start | bytes 4096 | tf_op jit(solution)/shard_map/slice | solution.py:172
  86.9 10.4 %copy-start.20 = (s32[128]{0:T(128)S(1)}, s32[128]{0:T(128)}, u32[]{:S(2)}) copy-start(s32[128]{0:T(128)} %constant.105.clone) | copy-start | bytes 1540
  86.9 10.4 %copy-start.21 = (s32[128]{0:T(128)S(1)}, s32[128]{0:T(128)}, u32[]{:S(2)}) copy-start(s32[128]{0:T(128)} %constant.109.clone) | copy-start | bytes 1540
  86.9 11.2 %copy-start.18 = (s32[128]{0:T(128)S(1)}, s32[128]{0:T(128)}, u32[]{:S(2)}) copy-start(s32[128]{0:T(128)} %constant.106.clone) | copy-start | bytes 1540
  87.0 11.1 %copy-start.19 = (s32[128]{0:T(128)S(1)}, s32[128]{0:T(128)}, u32[]{:S(2)}) copy-start(s32[128]{0:T(128)} %constant.110.clone) | copy-start | bytes 1540
  87.0 12.1 %copy-start.16 = (s32[128]{0:T(128)S(1)}, s32[128]{0:T(128)}, u32[]{:S(2)}) copy-start(s32[128]{0:T(128)} %constant.107.clone) | copy-start | bytes 1540
  87.0 12.1 %copy-start.17 = (s32[128]{0:T(128)S(1)}, s32[128]{0:T(128)}, u32[]{:S(2)}) copy-start(s32[128]{0:T(128)} %constant.111.clone) | copy-start | bytes 1540
  118.8 1.7 copy-start.1
  121.2 32.7 %copy-start.10 = (bf16[1,512,256]{1,2,0:T(8,128)(2,1)}, bf16[1,512,256]{1,2,0:T(8,128)(2,1)S(1)}, u32[]{:S(2)}) copy-start(bf16[1,512,256]{1,2,0:T(8,128)(2,1)S(1)} %slice.208) | copy-start | bytes 786436
  140.9 27.6 %all-to-all-start.1 = ((bf16[16,4,2,16,256]{4,3,2,1,0:T(8,128)(2,1)}), bf16[16,4,2,16,256]{4,3,2,1,0:T(8,128)(2,1)S(1)}, u32[]{:S(2)}, u32[]{:S(2)}) async-start(bf16[16,4,2,16,256]{4,3,2,1,0:T(8,128)(2,1)} %bitcast.40), calls=%async_computation.1 | async-start | bytes 2097152 | tf_op jit(solution)/shard_map/all_to_all | solution.py:79
  155.1 0.9 copy-start.6
  171.1 1.0 copy-start
  172.1 37.1 %all-to-all-start.2 = ((bf16[8,64,2048]{2,1,0:T(8,128)(2,1)}), bf16[8,64,2048]{2,1,0:T(8,128)(2,1)S(1)}, u32[]{:S(2)}, u32[]{:S(2)}) async-start(bf16[8,64,2048]{2,1,0:T(8,128)(2,1)} %bitcast.182), calls=%async_computation.2 | async-start | bytes 4194304 | tf_op jit(solution)/shard_map/all_to_all | solution.py:111
  181.7 3.2 copy-start.5
  209.5 8.8 %copy-start.7 = (f32[2,128,512]{2,1,0:T(8,128)S(1)}, f32[2,128,512]{2,1,0:T(8,128)}, u32[]{:S(2)}) copy-start(f32[2,128,512]{2,1,0:T(8,128)} %convolution_multiply_fusion.4) | copy-start | bytes 1572868
  209.6 8.8 %copy-start.12 = (pred[128,512]{1,0:T(8,128)(4,1)S(1)}, pred[128,512]{1,0:T(8,128)(4,1)}, u32[]{:S(2)}) copy-start(pred[128,512]{1,0:T(8,128)(4,1)} %get-tuple-element.57) | copy-start | bytes 196612
  210.8 7.9 %copy-start.9 = (f32[2,128,256]{2,1,0:T(8,128)S(1)}, f32[2,128,256]{2,1,0:T(8,128)}, u32[]{:S(2)}) copy-start(f32[2,128,256]{2,1,0:T(8,128)} %convolution_multiply_fusion.6) | copy-start | bytes 786436
  210.8 7.9 %copy-start.14 = (pred[128,256]{1,0:T(8,128)(4,1)S(1)}, pred[128,256]{1,0:T(8,128)(4,1)}, u32[]{:S(2)}) copy-start(pred[128,256]{1,0:T(8,128)(4,1)} %get-tuple-element.59) | copy-start | bytes 98308
  211.2 7.7 %copy-start.8 = (bf16[2,1,64,2,128]{4,2,1,0,3:T(8,128)(2,1)S(1)}, bf16[2,1,64,2,128]{4,2,1,0,3:T(8,128)(2,1)}, u32[]{:S(2)}) copy-start(bf16[2,1,64,2,128]{4,2,1,0,3:T(8,128)(2,1)} %get-tuple-element.42) | copy-start | bytes 196612
  212.8 6.4 %copy-start.11 = (pred[128,1024]{1,0:T(8,128)(4,1)S(1)}, pred[128,1024]{1,0:T(8,128)(4,1)}, u32[]{:S(2)}) copy-start(pred[128,1024]{1,0:T(8,128)(4,1)} %get-tuple-element.53) | copy-start | bytes 393220
  212.8 34.3 %all-to-all-start.3 = ((bf16[8,64,2048]{2,1,0:T(8,128)(2,1)}), bf16[8,64,2048]{2,1,0:T(8,128)(2,1)}, u32[]{:S(2)}, u32[]{:S(2)}) async-start(bf16[8,64,2048]{2,1,0:T(8,128)(2,1)} %broadcast_in_dim.227), calls=%async_computation.3 | async-start | bytes 4194304 | tf_op jit(solution)/shard_map/all_to_all | solution.py:105
  222.9 2.4 copy-start.25
  227.3 50.2 %copy-start.4 = (bf16[128,2048]{1,0:T(8,128)(2,1)S(1)}, bf16[128,2048]{1,0:T(8,128)(2,1)}, u32[]{:S(2)}) copy-start(bf16[128,2048]{1,0:T(8,128)(2,1)} %param.16) | copy-start | bytes 1572868
  279.7 32.2 %all-to-all-start.5 = ((bf16[8,64,2048]{2,1,0:T(8,128)(2,1)}), bf16[8,64,2048]{2,1,0:T(8,128)(2,1)S(1)}, u32[]{:S(2)}, u32[]{:S(2)}) async-start(bf16[8,64,2048]{2,1,0:T(8,128)(2,1)} %broadcast_in_dim.228), calls=%async_computation.5 | async-start | bytes 4194304 | tf_op jit(solution)/shard_map/all_to_all | solution.py:105
  311.9 1.3 copy-start.2
  313.2 32.2 %all-to-all-start.6 = ((bf16[8,64,2048]{2,1,0:T(8,128)(2,1)}), bf16[8,64,2048]{2,1,0:T(8,128)(2,1)S(1)}, u32[]{:S(2)}, u32[]{:S(2)}) async-start(bf16[8,64,2048]{2,1,0:T(8,128)(2,1)} %bitcast.185), calls=%async_computation.6 | async-start | bytes 4194304 | tf_op jit(solution)/shard_map/all_to_all | solution.py:111
  345.4 34.3 %all-to-all-start.7 = ((bf16[8,64,2048]{2,1,0:T(8,128)(2,1)}), bf16[8,64,2048]{2,1,0:T(8,128)(2,1)}, u32[]{:S(2)}, u32[]{:S(2)}) async-start(bf16[8,64,2048]{2,1,0:T(8,128)(2,1)} %bitcast.184), calls=%async_computation.7 | async-start | bytes 4194304 | tf_op jit(solution)/shard_map/all_to_all | solution.py:111
Sparse Core Ops, SparseCore 0:
  10.2 89.7 all-gather.3
  101.6 88.8 all-gather.5

commit v8 on v5

--- a/solution.py
+++ b/solution.py
@@ -71,18 +71,24 @@
     page_size = tokens // pages
     owners = lax.axis_size("dp")
     per_owner = pages // owners
+    me = lax.axis_index("dp")
+    base = 128
     stacked = jnp.stack([keys.reshape(tokens, width), values.reshape(tokens, width)], axis=0)
     stacked = stacked.reshape(2, pages, page_size, width).transpose(1, 0, 2, 3)
     order = jnp.argsort(page_table // pages, stable=True)
-    outgoing = stacked[order].reshape(owners, per_owner, 2, page_size, width)
-    outgoing_ids = page_table[order].reshape(owners, per_owner)
-    arrived, arrived_ids = (
-        lax.all_to_all(outgoing, "dp", split_axis=0, concat_axis=0, tiled=True),
-        lax.all_to_all(outgoing_ids, "dp", split_axis=0, concat_axis=0, tiled=True),
-    )
-    local = (arrived_ids - lax.axis_index("dp") * pages).reshape(-1)
+    sorted_ids = page_table[order].reshape(owners, per_owner)
+    code = jnp.stack([sorted_ids // base, sorted_ids % base], axis=-1).astype(jnp.bfloat16)
+    slab = jnp.zeros((owners, 1, 2, page_size, width), jnp.bfloat16)
+    slab = slab.at[:, 0, 0, 0, : 2 * per_owner].set(code.reshape(owners, 2 * per_owner))
+    outgoing = jnp.concatenate(
+        [stacked[order].reshape(owners, per_owner, 2, page_size, width), slab], axis=1
+    )
+    arrived = lax.all_to_all(outgoing, "dp", split_axis=0, concat_axis=0, tiled=True)
+    codes = arrived[:, per_owner, 0, 0, : 2 * per_owner].astype(jnp.int32)
+    codes = codes.reshape(owners, per_owner, 2)
+    local = (codes[..., 0] * base + codes[..., 1] - me * pages).reshape(-1)
     empty = jnp.zeros((pages, 2, page_size, width), jnp.bfloat16)
-    return empty.at[local].set(arrived.reshape(pages, 2, page_size, width))
+    return empty.at[local].set(arrived[:, :per_owner].reshape(pages, 2, page_size, width))
 
 
 def gather_packed(pieces, axis_name):

time: 390 us -> 384 us (0.985)
  blocking collectives: 41.6 us -> 29.6 us
  waiting for transfers between devices: 155 us -> 165 us
    all_to_all x1 -> x0, blocking collectives: 12.8 us -> none  [write_cache(): lax.all_to_all(outgoing_ids, 'dp', split_axis=0, concat_axis=0, tiled=True)]
    all_gather x1, waiting for transfers between devices: 0.01 us -> 9.47 us  [body(): lax.all_gather(jnp.concatenate([w_qkv, jnp.transpose(w_out)[None]], axis=...]
    all_to_all x3, waiting for transfers between devices: 84 us -> 79.1 us  [gather_rows(): gathered = lax.all_to_all(copies, axis_name, 0, 0, tiled=True)]
    all_to_all x3, starting transfers between devices: 20.5 us -> 16.1 us  [sum_rows(): lax.all_to_all(terms.reshape(count, terms.shape[0] // count, terms.shape[...]
    sub x8, other arithmetic: 6.31 us -> 2.36 us  [attend_block(): weights = jnp.exp(jnp.where(allowed[None], scores - top, -1e+30))]
    unnamed x58 -> x80, local copies, waits for them, and re-layouts: 13.6 us -> 13.3 us
  transfers between devices with their start and end apart: 9 -> 9, of which waited for: 7 -> 8; matrix products, arithmetic and copies ran while one was open for 32% -> 32% of each run, Pallas kernels for 0% -> 0%
where the time goes in v8:
time: 384 us; the launch traced here: 378 us
  waiting for transfers between devices  165 us (43%)
  matrix products  55.3 us (14%)
  starting transfers between devices  38.3 us (10%)
  other arithmetic  38.3 us (10%)
  local copies, waits for them, and re-layouts  36.7 us (10%)
  blocking collectives  29.6 us (8%)
  between operations  14.8 us (4%)
    all_to_all x3, waiting for transfers between devices, gather_rows(): gathered = lax.all_to_all(copies, axis_name, 0, 0, tiled=True)  79.1 us
    all_to_all x3, waiting for transfers between devices, sum_rows(): lax.all_to_all(terms.reshape(count, terms.shape[0] // count, terms.shape[...  71.7 us
    all_to_all x1, blocking collectives, sum_rows(): lax.all_to_all(terms.reshape(count, terms.shape[0] // count, terms.shape[...  29.6 us
    all_to_all x3, starting transfers between devices, gather_rows(): gathered = lax.all_to_all(copies, axis_name, 0, 0, tiled=True)  17.6 us
    all_to_all x3, starting transfers between devices, sum_rows(): lax.all_to_all(terms.reshape(count, terms.shape[0] // count, terms.shape[...  16.1 us
    dot_general x2, matrix products, mlp_of(): jnp.einsum('td,cdf->ctf', rows, mlp_w[:2], preferred_element_type=jnp.flo...  15.3 us
    unnamed x80, local copies, waits for them, and re-layouts  13.3 us
    dot_general x8, matrix products, attend_block(): jnp.einsum('hqk,khd->qhd', weights.astype(jnp.bfloat16), values, preferre...  12.8 us
  transfers between devices with their start and end apart: 9, of which 8 were waited for; matrix products, arithmetic and copies ran while one was open for 32% of the time, Pallas kernels for 0%

profile of v8, /device:TPU:1, one launch (start us, length us, event | category | flops | bytes accessed | tf_op | source)
XLA Modules:
  0.0 377.8 jit_solution(4181732406730476259)
XLA Ops:
  7.2 1.1 copy.89
  8.4 1.6 pad_maximum_fusion.2
  10.0 1.3 copy.103
  11.3 2.0 pad_maximum_fusion
  13.3 2.5 broadcast_in_dim.119
  16.0 8.3 %all-to-all-start = ((bf16[8,128,2048]{2,1,0:T(8,128)(2,1)}), bf16[8,128,2048]{2,1,0:T(8,128)(2,1)}, u32[]{:S(2)}, u32[]{:S(2)}) async-start(bf16[8,128,2048]{2,1,0:T(8,128)(2,1)} %broadcast_in_dim.119), calls=%async_computation | async-start | bytes 8388608 | tf_op jit(solution)/shard_map/all_to_all | solution.py:108
  24.4 2.0 sort.17
  29.8 1.0 fusion.105
  30.8 1.1 fusion.97
  31.9 1.9 multiply_cosine_fusion
  33.8 44.9 %all-to-all-done = bf16[8,128,2048]{2,1,0:T(8,128)(2,1)} async-done(((bf16[8,128,2048]{2,1,0:T(8,128)(2,1)}), bf16[8,128,2048]{2,1,0:T(8,128)(2,1)}, u32[]{:S(2)}, u32[]{:S(2)}) %all-to-all-start) | async-done | bytes 4194336 | tf_op jit(solution)/shard_map/all_to_all | solution.py:108
  78.7 2.8 convert_reduce_fusion
  81.5 3.4 multiply_reduce_fusion
  85.0 4.2 %fusion.9 = bf16[1024,2048]{1,0:T(8,128)(2,1)} fusion(bf16[8,128,2048]{2,1,0:T(8,128)(2,1)} %all-to-all-done, f32[1024]{0:T(1024)S(1)} %rsqrt_bitcast_fusion, f32[1024]{0:T(1024)S(1)} %get-tuple-element.68), kind=kLoop, calls=%fused_computation.13 | loop fusion | flops 8388608 | bytes 8396800 | tf_op jit(solution)/shard_map/convert_element_type | solution.py:150
  89.2 9.5 %all-gather.3.cloned.1.call-done = bf16[4,2048,256]{1,2,0:T(8,128)(2,1)} async-done(((bf16[4,128,256]{1,2,0:T(8,128)(2,1)}), bf16[4,2048,256]{1,2,0:T(8,128)(2,1)}) %all-gather.3.cloned.1.call-update) | async-done | bytes 4194320 | tf_op jit(solution)/shard_map/all_gather | solution.py:143
  98.7 6.2 %fusion.21 = f32[3,1024,256]{1,2,0:T(8,128)S(1)} fusion(bf16[4,2048,256]{1,2,0:T(8,128)(2,1)} %all-gather.3.cloned.1.call-done, bf16[1024,2048]{1,0:T(8,128)(2,1)} %fusion.9), kind=kOutput, calls=%fused_computation.39 | convolution fusion | flops 3221225472 | bytes 11534336 | tf_op jit(solution)/shard_map/td,cdf->ctf/dot_general | solution.py:152
  104.9 1.7 copy-done.3
  106.6 1.0 copy.95
  109.8 2.7 fusion.228
  113.4 1.4 copy.106
  114.8 1.3 copy.107
  116.1 1.5 multiply_subtract_fusion
  118.5 1.1 convert_element_type.193
  119.6 1.3 maximum_bitcast_fusion
  120.9 1.6 gather_fusion
  122.5 2.5 fusion.40
  125.1 4.5 %all-to-all-start.1 = ((bf16[16,5,2,16,256]{4,3,2,1,0:T(8,128)(2,1)}), bf16[16,5,2,16,256]{4,3,2,1,0:T(8,128)(2,1)}, u32[]{:S(2)}, u32[]{:S(2)}) async-start(bf16[16,5,2,16,256]{4,3,2,1,0:T(8,128)(2,1)} %fusion.40), calls=%async_computation.1 | async-start | bytes 2621440 | tf_op jit(solution)/shard_map/all_to_all | solution.py:86
  129.5 1.0 fusion.230
  130.6 1.4 copy.104
  132.0 2.4 copy.105
  134.3 1.5 subtract_convert_fusion
  139.1 2.0 fusion.72
  141.1 2.0 fusion.73
  143.1 1.5 fusion.74
  144.7 1.5 fusion.70
  146.2 3.3 convolution_convert_fusion.1
  149.5 4.6 %all-to-all-done.1 = bf16[16,5,2,16,256]{4,3,2,1,0:T(8,128)(2,1)} async-done(((bf16[16,5,2,16,256]{4,3,2,1,0:T(8,128)(2,1)}), bf16[16,5,2,16,256]{4,3,2,1,0:T(8,128)(2,1)}, u32[]{:S(2)}, u32[]{:S(2)}) %all-to-all-start.1) | async-done | bytes 1310752 | tf_op jit(solution)/shard_map/all_to_all | solution.py:86
  155.2 1.3 slice.274
  156.7 2.5 scatter_fusion
  160.2 7.0 %all-to-all-start.2 = ((bf16[8,64,2048]{2,1,0:T(8,128)(2,1)}), bf16[8,64,2048]{2,1,0:T(8,128)(2,1)S(1)}, u32[]{:S(2)}, u32[]{:S(2)}) async-start(bf16[8,64,2048]{2,1,0:T(8,128)(2,1)} %bitcast.180), calls=%async_computation.2 | async-start | bytes 4194304 | tf_op jit(solution)/shard_map/all_to_all | solution.py:114
  168.6 1.0 convolution_multiply_fusion.4
  169.7 28.6 %all-to-all-done.2 = bf16[8,64,2048]{2,1,0:T(8,128)(2,1)S(1)} async-done(((bf16[8,64,2048]{2,1,0:T(8,128)(2,1)}), bf16[8,64,2048]{2,1,0:T(8,128)(2,1)S(1)}, u32[]{:S(2)}, u32[]{:S(2)}) %all-to-all-start.2) | async-done | bytes 2097184 | tf_op jit(solution)/shard_map/all_to_all | solution.py:114
  198.7 1.2 convert_reduce_fusion.6
  200.3 1.6 broadcast_in_dim.224
  201.9 5.5 %all-to-all-start.3 = ((bf16[8,64,2048]{2,1,0:T(8,128)(2,1)}), bf16[8,64,2048]{2,1,0:T(8,128)(2,1)}, u32[]{:S(2)}, u32[]{:S(2)}) async-start(bf16[8,64,2048]{2,1,0:T(8,128)(2,1)} %broadcast_in_dim.224), calls=%async_computation.3 | async-start | bytes 4194304 | tf_op jit(solution)/shard_map/all_to_all | solution.py:108
  208.6 1.4 fusion.71
  209.9 2.0 fusion.75
  211.9 1.9 fusion.76
  214.3 2.0 convolution_convert_fusion
  216.3 19.7 %all-to-all-done.3 = bf16[8,64,2048]{2,1,0:T(8,128)(2,1)} async-done(((bf16[8,64,2048]{2,1,0:T(8,128)(2,1)}), bf16[8,64,2048]{2,1,0:T(8,128)(2,1)}, u32[]{:S(2)}, u32[]{:S(2)}) %all-to-all-start.3) | async-done | bytes 2097184 | tf_op jit(solution)/shard_map/all_to_all | solution.py:108
  236.0 29.6 %all_to_all.40 = bf16[8,64,2048]{2,1,0:T(8,128)(2,1)S(1)} all-to-all(bf16[8,64,2048]{2,1,0:T(8,128)(2,1)S(1)} %bitcast.184), channel_id=1, replica_groups=mesh['dp'=16,'tensor'=8] {'tensor'}, dimensions={0} | all-to-all | bytes 4194304 | tf_op jit(solution)/shard_map/all_to_all | solution.py:114
  266.6 1.6 broadcast_in_dim.225
  268.2 3.8 %all-to-all-start.5 = ((bf16[8,64,2048]{2,1,0:T(8,128)(2,1)}), bf16[8,64,2048]{2,1,0:T(8,128)(2,1)S(1)}, u32[]{:S(2)}, u32[]{:S(2)}) async-start(bf16[8,64,2048]{2,1,0:T(8,128)(2,1)} %broadcast_in_dim.225), calls=%async_computation.5 | async-start | bytes 4194304 | tf_op jit(solution)/shard_map/all_to_all | solution.py:108
  272.0 7.6 %convolution_bitcast_fusion.1 = f32[2,512,1024]{1,2,0:T(8,128)S(1)} fusion(bf16[3,2048,1024]{1,2,0:T(8,128)(2,1)} %all-gather.5.cloned.1.call-done, bf16[512,2048]{1,0:T(8,128)(2,1)} %bitcast.61), kind=kOutput, calls=%fused_computation.32 | convolution fusion | flops 4294967296 | bytes 18874368 | tf_op jit(solution)/shard_map/td,cdf->ctf/dot_general | solution.py:191
  279.7 6.2 %fusion.14 = bf16[512,2048]{1,0:T(8,128)(2,1)} fusion(bf16[3,2048,1024]{1,2,0:T(8,128)(2,1)} %all-gather.5.cloned.1.call-done, f32[2,512,1024]{1,2,0:T(8,128)S(1)} %convolution_bitcast_fusion.1), kind=kOutput, calls=%fused_computation.25 | convolution fusion | flops 2151677952 | bytes 10485760 | tf_op jit(solution)/shard_map/tf,df->td/dot_general | solution.py:193
  285.9 14.5 %all-to-all-done.5 = bf16[8,64,2048]{2,1,0:T(8,128)(2,1)S(1)} async-done(((bf16[8,64,2048]{2,1,0:T(8,128)(2,1)}), bf16[8,64,2048]{2,1,0:T(8,128)(2,1)S(1)}, u32[]{:S(2)}, u32[]{:S(2)}) %all-to-all-start.5) | async-done | bytes 2097184 | tf_op jit(solution)/shard_map/all_to_all | solution.py:108
  300.3 1.3 copy-done.4
  301.7 3.6 all-to-all-start.6
  305.3 7.6 %convolution_bitcast_fusion = f32[2,512,1024]{1,2,0:T(8,128)S(1)} fusion(bf16[3,2048,1024]{1,2,0:T(8,128)(2,1)} %all-gather.5.cloned.1.call-done, bf16[512,2048]{1,0:T(8,128)(2,1)} %bitcast.181), kind=kOutput, calls=%fused_computation.31 | convolution fusion | flops 4294967296 | bytes 18874368 | tf_op jit(solution)/shard_map/td,cdf->ctf/dot_general | solution.py:191
  312.9 6.1 %fusion.15 = bf16[512,2048]{1,0:T(8,128)(2,1)} fusion(bf16[3,2048,1024]{1,2,0:T(8,128)(2,1)} %all-gather.5.cloned.1.call-done, f32[2,512,1024]{1,2,0:T(8,128)S(1)} %convolution_bitcast_fusion), kind=kOutput, calls=%fused_computation.26 | convolution fusion | flops 2151677952 | bytes 10485760 | tf_op jit(solution)/shard_map/tf,df->td/dot_general | solution.py:193
  319.1 14.8 %all-to-all-done.6 = bf16[8,64,2048]{2,1,0:T(8,128)(2,1)S(1)} async-done(((bf16[8,64,2048]{2,1,0:T(8,128)(2,1)}), bf16[8,64,2048]{2,1,0:T(8,128)(2,1)S(1)}, u32[]{:S(2)}, u32[]{:S(2)}) %all-to-all-start.6) | async-done | bytes 2097184 | tf_op jit(solution)/shard_map/all_to_all | solution.py:114
  333.8 5.6 %all-to-all-start.7 = ((bf16[8,64,2048]{2,1,0:T(8,128)(2,1)}), bf16[8,64,2048]{2,1,0:T(8,128)(2,1)}, u32[]{:S(2)}, u32[]{:S(2)}) async-start(bf16[8,64,2048]{2,1,0:T(8,128)(2,1)} %bitcast.182), calls=%async_computation.7 | async-start | bytes 4194304 | tf_op jit(solution)/shard_map/all_to_all | solution.py:114
  339.8 28.3 %all-to-all-done.7 = bf16[8,64,2048]{2,1,0:T(8,128)(2,1)} async-done(((bf16[8,64,2048]{2,1,0:T(8,128)(2,1)}), bf16[8,64,2048]{2,1,0:T(8,128)(2,1)}, u32[]{:S(2)}, u32[]{:S(2)}) %all-to-all-start.7) | async-done | bytes 2097184 | tf_op jit(solution)/shard_map/all_to_all | solution.py:114
  368.1 2.0 convert_reduce_fusion.1
  (152 shorter events, 19.1 us)
Async XLA Ops:
  7.2 6.1 %copy-start.5 = (bf16[128,2048]{1,0:T(8,128)(2,1)S(1)}, bf16[128,2048]{1,0:T(8,128)(2,1)}, u32[]{:S(2)}) copy-start(bf16[128,2048]{1,0:T(8,128)(2,1)} %param.18) | copy-start | bytes 1572868
  7.2 91.5 %all-gather.3.cloned.1.call-start = ((), (), s32[]{:S(2)}) async-start(), calls=%async_computation.8 | async-start | bytes 4456448 | tf_op jit(solution)/shard_map/all_gather | solution.py:143
  10.0 262.1 %all-gather.5.cloned.1.call-start = ((), (), s32[]{:S(2)}) async-start(), calls=%async_computation.9 | async-start | bytes 13369344 | tf_op jit(solution)/shard_map/all_gather | solution.py:146
  15.8 8.4 %copy-start.20 = (s32[1024]{0:T(1024)S(1)}, s32[1024]{0:T(1024)}, u32[]{:S(2)}) copy-start(s32[1024]{0:T(1024)} %param.19) | copy-start | bytes 12292
  15.8 8.5 %copy-start.23 = (s32[1024]{0:T(1024)S(1)}, s32[1024]{0:T(1024)}, u32[]{:S(2)}) copy-start(s32[1024]{0:T(1024)} %param.20) | copy-start | bytes 12292
  15.8 8.5 %copy-start = (s32[64]{0:T(128)S(1)}, s32[64]{0:T(128)}, u32[]{:S(2)}) copy-start(s32[64]{0:T(128)} %param.25) | copy-start | bytes 772
  15.8 12.4 %slice-start = ((s32[1024]{0:T(1024)}), s32[256]{0:T(256)S(1)}, s32[]{:S(2)}) async-start(s32[1024]{0:T(1024)} %param.19), calls=%async_computation.10 | async-start | bytes 2048 | tf_op jit(solution)/shard_map/slice | solution.py:175
  15.9 12.4 %copy-start.30 = (s32[128]{0:T(128)S(1)}, s32[128]{0:T(128)}, u32[]{:S(2)}) copy-start(s32[128]{0:T(128)} %constant.134.clone) | copy-start | bytes 1540
  15.9 12.4 %copy-start.31 = (s32[128]{0:T(128)S(1)}, s32[128]{0:T(128)}, u32[]{:S(2)}) copy-start(s32[128]{0:T(128)} %constant.138.clone) | copy-start | bytes 1540
  15.9 13.1 %slice-start.1 = ((s32[1024]{0:T(1024)}), s32[512]{0:T(512)S(1)}, s32[]{:S(2)}) async-start(s32[1024]{0:T(1024)} %param.19), calls=%async_computation.11 | async-start | bytes 4096 | tf_op jit(solution)/shard_map/slice | solution.py:175
  15.9 13.1 %copy-start.28 = (s32[128]{0:T(128)S(1)}, s32[128]{0:T(128)}, u32[]{:S(2)}) copy-start(s32[128]{0:T(128)} %constant.135.clone) | copy-start | bytes 1540
  15.9 13.1 %copy-start.29 = (s32[128]{0:T(128)S(1)}, s32[128]{0:T(128)}, u32[]{:S(2)}) copy-start(s32[128]{0:T(128)} %constant.139.clone) | copy-start | bytes 1540
  15.9 13.9 %copy-start.26 = (s32[128]{0:T(128)S(1)}, s32[128]{0:T(128)}, u32[]{:S(2)}) copy-start(s32[128]{0:T(128)} %constant.136.clone) | copy-start | bytes 1540
  15.9 13.9 %copy-start.27 = (s32[128]{0:T(128)S(1)}, s32[128]{0:T(128)}, u32[]{:S(2)}) copy-start(s32[128]{0:T(128)} %constant.140.clone) | copy-start | bytes 1540
  15.9 14.9 %copy-start.24 = (s32[128]{0:T(128)S(1)}, s32[128]{0:T(128)}, u32[]{:S(2)}) copy-start(s32[128]{0:T(128)} %constant.137.clone) | copy-start | bytes 1540
  16.0 14.8 %copy-start.25 = (s32[128]{0:T(128)S(1)}, s32[128]{0:T(128)}, u32[]{:S(2)}) copy-start(s32[128]{0:T(128)} %constant.141.clone) | copy-start | bytes 1540
  16.0 62.7 %all-to-all-start = ((bf16[8,128,2048]{2,1,0:T(8,128)(2,1)}), bf16[8,128,2048]{2,1,0:T(8,128)(2,1)}, u32[]{:S(2)}, u32[]{:S(2)}) async-start(bf16[8,128,2048]{2,1,0:T(8,128)(2,1)} %broadcast_in_dim.119), calls=%async_computation | async-start | bytes 8388608 | tf_op jit(solution)/shard_map/all_to_all | solution.py:108
  29.0 108.0 %copy-start.22 = (pred[128,256]{1,0:T(8,128)(4,1)}, pred[128,256]{1,0:T(8,128)(4,1)S(1)}, u32[]{:S(2)}) copy-start(pred[128,256]{1,0:T(8,128)(4,1)S(1)} %get-tuple-element.72) | copy-start | bytes 98308
  104.9 1.7 copy-start.3
  122.5 7.0 %copy-start.2 = (f32[1,1024,256]{1,2,0:T(8,128)S(1)}, f32[1,1024,256]{1,2,0:T(8,128)}, u32[]{:S(2)}) copy-start(f32[1,1024,256]{1,2,0:T(8,128)} %get-tuple-element.43) | copy-start | bytes 3145732
  125.1 29.0 %all-to-all-start.1 = ((bf16[16,5,2,16,256]{4,3,2,1,0:T(8,128)(2,1)}), bf16[16,5,2,16,256]{4,3,2,1,0:T(8,128)(2,1)}, u32[]{:S(2)}, u32[]{:S(2)}) async-start(bf16[16,5,2,16,256]{4,3,2,1,0:T(8,128)(2,1)} %fusion.40), calls=%async_computation.1 | async-start | bytes 2621440 | tf_op jit(solution)/shard_map/all_to_all | solution.py:86
  134.3 3.1 copy-start.19
  134.3 3.7 copy-start.17
  135.9 2.8 copy-start.15
  137.0 1.3 copy-start.12
  143.1 3.0 copy-start.33
  143.1 3.0 copy-start.34
  156.5 10.6 %copy-start.10 = (bf16[2,1,64,2,128]{4,2,1,0,3:T(8,128)(2,1)S(1)}, bf16[2,1,64,2,128]{4,2,1,0,3:T(8,128)(2,1)}, u32[]{:S(2)}) copy-start(bf16[2,1,64,2,128]{4,2,1,0,3:T(8,128)(2,1)} %get-tuple-element.53) | copy-start | bytes 196612
  156.7 10.8 %copy-start.16 = (pred[128,768]{1,0:T(8,128)(4,1)S(1)}, pred[128,768]{1,0:T(8,128)(4,1)}, u32[]{:S(2)}) copy-start(pred[128,768]{1,0:T(8,128)(4,1)} %get-tuple-element.65) | copy-start | bytes 294916
  159.2 1.0 copy-start.1
  159.2 9.4 %copy-start.13 = (bf16[2,1,64,2,128]{4,2,1,0,3:T(8,128)(2,1)S(1)}, bf16[2,1,64,2,128]{4,2,1,0,3:T(8,128)(2,1)}, u32[]{:S(2)}) copy-start(bf16[2,1,64,2,128]{4,2,1,0,3:T(8,128)(2,1)} %get-tuple-element.51) | copy-start | bytes 196612
  160.2 38.1 %all-to-all-start.2 = ((bf16[8,64,2048]{2,1,0:T(8,128)(2,1)}), bf16[8,64,2048]{2,1,0:T(8,128)(2,1)S(1)}, u32[]{:S(2)}, u32[]{:S(2)}) async-start(bf16[8,64,2048]{2,1,0:T(8,128)(2,1)} %bitcast.180), calls=%async_computation.2 | async-start | bytes 4194304 | tf_op jit(solution)/shard_map/all_to_all | solution.py:114
  167.4 1.2 copy-start.7
  198.7 8.7 %copy-start.8 = (f32[2,128,512]{2,1,0:T(8,128)S(1)}, f32[2,128,512]{2,1,0:T(8,128)}, u32[]{:S(2)}) copy-start(f32[2,128,512]{2,1,0:T(8,128)} %convolution_multiply_fusion.4) | copy-start | bytes 1572868
  198.7 8.7 %copy-start.18 = (pred[128,512]{1,0:T(8,128)(4,1)S(1)}, pred[128,512]{1,0:T(8,128)(4,1)}, u32[]{:S(2)}) copy-start(pred[128,512]{1,0:T(8,128)(4,1)} %get-tuple-element.71) | copy-start | bytes 196612
  199.9 7.7 %copy-start.11 = (f32[2,128,256]{2,1,0:T(8,128)S(1)}, f32[2,128,256]{2,1,0:T(8,128)}, u32[]{:S(2)}) copy-start(f32[2,128,256]{2,1,0:T(8,128)} %convolution_multiply_fusion.6) | copy-start | bytes 786436
  199.9 7.7 %copy-start.21 = (pred[128,256]{1,0:T(8,128)(4,1)S(1)}, pred[128,256]{1,0:T(8,128)(4,1)}, u32[]{:S(2)}) copy-start(pred[128,256]{1,0:T(8,128)(4,1)} %get-tuple-element.73) | copy-start | bytes 98308
  201.9 6.3 %copy-start.14 = (pred[128,1024]{1,0:T(8,128)(4,1)S(1)}, pred[128,1024]{1,0:T(8,128)(4,1)}, u32[]{:S(2)}) copy-start(pred[128,1024]{1,0:T(8,128)(4,1)} %get-tuple-element.67) | copy-start | bytes 393220
  201.9 34.2 %all-to-all-start.3 = ((bf16[8,64,2048]{2,1,0:T(8,128)(2,1)}), bf16[8,64,2048]{2,1,0:T(8,128)(2,1)}, u32[]{:S(2)}, u32[]{:S(2)}) async-start(bf16[8,64,2048]{2,1,0:T(8,128)(2,1)} %broadcast_in_dim.224), calls=%async_computation.3 | async-start | bytes 4194304 | tf_op jit(solution)/shard_map/all_to_all | solution.py:108
  207.3 4.6 %copy-start.9 = (bf16[1,768,256]{1,2,0:T(8,128)(2,1)S(1)}, bf16[1,768,256]{1,2,0:T(8,128)(2,1)}, u32[]{:S(2)}) copy-start(bf16[1,768,256]{1,2,0:T(8,128)(2,1)} %slice.262) | copy-start | bytes 1179652
  211.9 2.4 copy-start.32
  216.3 49.7 %copy-start.6 = (bf16[128,2048]{1,0:T(8,128)(2,1)S(1)}, bf16[128,2048]{1,0:T(8,128)(2,1)}, u32[]{:S(2)}) copy-start(bf16[128,2048]{1,0:T(8,128)(2,1)} %param.18) | copy-start | bytes 1572868
  268.2 32.2 %all-to-all-start.5 = ((bf16[8,64,2048]{2,1,0:T(8,128)(2,1)}), bf16[8,64,2048]{2,1,0:T(8,128)(2,1)S(1)}, u32[]{:S(2)}, u32[]{:S(2)}) async-start(bf16[8,64,2048]{2,1,0:T(8,128)(2,1)} %broadcast_in_dim.225), calls=%async_computation.5 | async-start | bytes 4194304 | tf_op jit(solution)/shard_map/all_to_all | solution.py:108
  300.3 1.3 copy-start.4
  301.7 32.2 %all-to-all-start.6 = ((bf16[8,64,2048]{2,1,0:T(8,128)(2,1)}), bf16[8,64,2048]{2,1,0:T(8,128)(2,1)S(1)}, u32[]{:S(2)}, u32[]{:S(2)}) async-start(bf16[8,64,2048]{2,1,0:T(8,128)(2,1)} %bitcast.183), calls=%async_computation.6 | async-start | bytes 4194304 | tf_op jit(solution)/shard_map/all_to_all | solution.py:114
  333.8 34.3 %all-to-all-start.7 = ((bf16[8,64,2048]{2,1,0:T(8,128)(2,1)}), bf16[8,64,2048]{2,1,0:T(8,128)(2,1)}, u32[]{:S(2)}, u32[]{:S(2)}) async-start(bf16[8,64,2048]{2,1,0:T(8,128)(2,1)} %bitcast.182), calls=%async_computation.7 | async-start | bytes 4194304 | tf_op jit(solution)/shard_map/all_to_all | solution.py:114
Sparse Core Ops, SparseCore 0:
  10.2 88.4 all-gather.2
  100.3 110.9 all-gather.4

commit v9 on v8

--- a/solution.py
+++ b/solution.py
@@ -8,6 +8,7 @@
 from jax.sharding import PartitionSpec as P
 
 HD = 128
+DP = ("chips", "core")
 
 
 def layer_norm(values):
@@ -69,9 +70,9 @@
     width = keys.shape[1] * keys.shape[2]
     pages = page_table.shape[0]
     page_size = tokens // pages
-    owners = lax.axis_size("dp")
+    owners = lax.axis_size(DP)
     per_owner = pages // owners
-    me = lax.axis_index("dp")
+    me = lax.axis_index(DP)
     base = 128
     stacked = jnp.stack([keys.reshape(tokens, width), values.reshape(tokens, width)], axis=0)
     stacked = stacked.reshape(2, pages, page_size, width).transpose(1, 0, 2, 3)
@@ -83,12 +84,20 @@
     outgoing = jnp.concatenate(
         [stacked[order].reshape(owners, per_owner, 2, page_size, width), slab], axis=1
     )
-    arrived = lax.all_to_all(outgoing, "dp", split_axis=0, concat_axis=0, tiled=True)
+    arrived = lax.all_to_all(outgoing, DP, split_axis=0, concat_axis=0, tiled=True)
     codes = arrived[:, per_owner, 0, 0, : 2 * per_owner].astype(jnp.int32)
     codes = codes.reshape(owners, per_owner, 2)
     local = (codes[..., 0] * base + codes[..., 1] - me * pages).reshape(-1)
     empty = jnp.zeros((pages, 2, page_size, width), jnp.bfloat16)
     return empty.at[local].set(arrived[:, :per_owner].reshape(pages, 2, page_size, width))
+
+
+def gather_weights(piece):
+    mine = lax.all_gather(piece, "chips", axis=1, tiled=False)
+    other = lax.ppermute(mine, "core", [(0, 1), (1, 0)])
+    first = lax.axis_index("core") == 0
+    both = jnp.stack([jnp.where(first, mine, other), jnp.where(first, other, mine)], axis=2)
+    return both.reshape(piece.shape[0], -1, piece.shape[2])
 
 
 def gather_packed(pieces, axis_name):
@@ -140,12 +149,8 @@
     share_rows = stream.shape[0]
     shares = tok_group // share_rows
     local_cols = w_qkv.shape[2]
-    attn_w = lax.all_gather(
-        jnp.concatenate([w_qkv, jnp.transpose(w_out)[None]], axis=0), "dp", axis=1, tiled=True
-    )
-    mlp_w = lax.all_gather(
-        jnp.concatenate([w_gate_up, jnp.transpose(w_down)[None]], axis=0), "dp", axis=1, tiled=True
-    )
+    attn_w = gather_weights(jnp.concatenate([w_qkv, jnp.transpose(w_out)[None]], axis=0))
+    mlp_w = gather_weights(jnp.concatenate([w_gate_up, jnp.transpose(w_down)[None]], axis=0))
     full_stream = gather_rows(stream, "tensor")
     normed = layer_norm(full_stream).astype(jnp.bfloat16)
     local_heads = local_cols // HD
@@ -212,19 +217,23 @@
 
 
 def solution(mesh):
+    dp_size = mesh.shape["dp"]
+    split = jax.sharding.Mesh(
+        mesh.devices.reshape(dp_size // 2, 2, mesh.shape["tensor"]), ("chips", "core", "tensor")
+    )
     return jax.shard_map(
         body,
-        mesh=mesh,
+        mesh=split,
         in_specs=(
-            P(("dp", "tensor"), None),
-            P("dp"),
-            P("dp"),
-            P(None, "dp", "tensor"),
-            P("tensor", "dp"),
-            P(None, "dp", "tensor"),
-            P("tensor", "dp"),
-            P("dp"),
+            P(DP + ("tensor",), None),
+            P(DP),
+            P(DP),
+            P(None, DP, "tensor"),
+            P("tensor", DP),
+            P(None, DP, "tensor"),
+            P("tensor", DP),
+            P(DP),
         ),
-        out_specs=(P(("dp", "tensor"), None), P("dp", None, None, "tensor")),
+        out_specs=(P(DP + ("tensor",), None), P(DP, None, None, "tensor")),
         check_vma=False,
     )

time: 384 us -> 505 us (1.32)
  local copies, waits for them, and re-layouts: 36.7 us -> 103 us
  blocking collectives: 29.6 us -> 67.5 us
  other arithmetic: 38.3 us -> 56.3 us
  waiting for transfers between devices: 165 us -> 173 us
  matrix products: 55.3 us -> 49.6 us
    all_gather x2, waiting for transfers between devices: 9.49 us -> 77.8 us  [gather_weights(): mine = lax.all_gather(piece, 'chips', axis=1, tiled=False)]
    all_to_all x3, waiting for transfers between devices: 79.1 us -> 16.6 us  [gather_rows(): gathered = lax.all_to_all(copies, axis_name, 0, 0, tiled=True)]
    slice x0 -> x6, local copies, waits for them, and re-layouts: none -> 53.2 us  [the longest x2 35.9 us: mlp_of(): mlp_w[:2]]
    all_to_all x1 -> x2, blocking collectives: 29.6 us -> 67.5 us  [sum_rows(): lax.all_to_all(terms.reshape(count, terms.shape[0] // count, terms.shape[...]
    another operation x2 -> x8, other arithmetic: 1.56 us -> 16.4 us  [the longest x6 14.5 us: gather_weights(): jnp.stack([jnp.where(first, mine, other), jnp.where(first, other, mine)],...]
    all_to_all x3 -> x2, starting transfers between devices: 16.1 us -> 8.09 us  [sum_rows(): lax.all_to_all(terms.reshape(count, terms.shape[0] // count, terms.shape[...]
    scatter x1, local copies, waits for them, and re-layouts: 2.5 us -> 9.1 us  [write_cache(): empty.at[local]]
    all_to_all x1, waiting for transfers between devices: 4.6 us -> 10.8 us  [write_cache(): lax.all_to_all(outgoing, DP, split_axis=0, concat_axis=0, tiled=True)]
  transfers between devices with their start and end apart: 9 -> 10, of which waited for: 8 -> 5; matrix products, arithmetic and copies ran while one was open for 32% -> 38% of each run, Pallas kernels for 0% -> 0%
where the time goes in v9:
time: 505 us; the launch traced here: 499 us
  waiting for transfers between devices  173 us (34%)
  local copies, waits for them, and re-layouts  103 us (20%)
  blocking collectives  67.5 us (13%)
  other arithmetic  56.3 us (11%)
  matrix products  49.6 us (10%)
  starting transfers between devices  33.4 us (7%)
  between operations  15.2 us (3%)
    all_gather x2, waiting for transfers between devices, gather_weights(): mine = lax.all_gather(piece, 'chips', axis=1, tiled=False)  77.8 us
    all_to_all x2, waiting for transfers between devices, sum_rows(): lax.all_to_all(terms.reshape(count, terms.shape[0] // count, terms.shape[...  68.2 us
    all_to_all x2, blocking collectives, sum_rows(): lax.all_to_all(terms.reshape(count, terms.shape[0] // count, terms.shape[...  67.5 us
    slice x2, local copies, waits for them, and re-layouts, mlp_of(): mlp_w[:2]  35.9 us
    all_to_all x3, starting transfers between devices, gather_rows(): gathered = lax.all_to_all(copies, axis_name, 0, 0, tiled=True)  17.5 us
    all_to_all x3, waiting for transfers between devices, gather_rows(): gathered = lax.all_to_all(copies, axis_name, 0, 0, tiled=True)  16.6 us
    slice x2, local copies, waits for them, and re-layouts, body(): attn_w[:3]  14.9 us
    dot_general x2, matrix products, mlp_of(): jnp.einsum('td,cdf->ctf', rows, mlp_w[:2], preferred_element_type=jnp.flo...  14.9 us
  transfers between devices with their start and end apart: 10, of which 5 were waited for; matrix products, arithmetic and copies ran while one was open for 38% of the time, Pallas kernels for 0%

profile of v9, /device:TPU:1, one launch (start us, length us, event | category | flops | bytes accessed | tf_op | source)
XLA Modules:
  0.0 498.6 jit_solution(5509112683062877923)
XLA Ops:
  8.2 1.7 pad_maximum_fusion.4
  9.8 3.6 broadcast_in_dim.119
  13.5 8.3 %all-to-all-start = ((bf16[8,128,2048]{2,1,0:T(8,128)(2,1)}), bf16[8,128,2048]{2,1,0:T(8,128)(2,1)}, u32[]{:S(2)}, u32[]{:S(2)}) async-start(bf16[8,128,2048]{2,1,0:T(8,128)(2,1)} %broadcast_in_dim.119), calls=%async_computation | async-start | bytes 8388608 | tf_op jit(solution)/shard_map/all_to_all | solution.py:117
  23.9 2.0 sort.17
  30.6 77.8 %all-gather.5.cloned.1.call-done = bf16[4,1024,256]{2,1,0:T(8,128)(2,1)} async-done(((bf16[4,128,256]{2,1,0:T(8,128)(2,1)}), bf16[4,1024,256]{2,1,0:T(8,128)(2,1)}) %all-gather.5.cloned.1.call-update) | async-done | bytes 2097168 | tf_op jit(solution)/shard_map/all_gather | solution.py:96
  108.5 1.5 collective-permute-start
  110.0 2.9 multiply_cosine_fusion
  112.9 2.8 convert_reduce_fusion
  115.7 3.4 fusion.10
  119.2 4.5 fusion.11
  123.7 2.1 select_bitcast_fusion.3
  125.8 1.3 copy-done.1
  127.2 1.8 fusion.13
  129.0 8.7 %copy.131 = bf16[3,8,2,128,256]{3,2,1,4,0:T(2,128)(2,1)} copy(bf16[3,8,2,128,256]{4,3,1,0,2:T(8,128)(2,1)} %fusion.13) | data formatting | bytes 6291456 | tf_op jit(solution)/shard_map/slice | solution.py:157
  137.7 6.2 %slice.202 = bf16[3,2048,256]{1,2,0:T(8,128)(2,1)} reshape(bf16[3,8,2,128,256]{3,2,1,4,0:T(2,128)(2,1)} %copy.131) | data formatting | bytes 6291456 | tf_op jit(solution)/shard_map/slice | solution.py:157
  143.9 6.3 %convolution_bitcast_fusion.2 = f32[3,1024,256]{1,2,0:T(8,128)S(1)} fusion(bf16[3,2048,256]{1,2,0:T(8,128)(2,1)} %slice.202, bf16[1024,2048,1]{1,0,2:T(8,128)(2,1)} %bitcast.179), kind=kOutput, calls=%fused_computation.46 | convolution fusion | flops 3221225472 | bytes 10485760 | tf_op jit(solution)/shard_map/td,cdf->ctf/dot_general | solution.py:157
  150.2 1.7 copy-done.5
  158.5 1.4 copy.150
  161.1 2.2 fusion.223
  163.3 2.4 copy.152
  165.6 1.4 copy.151
  167.1 1.8 multiply_subtract_fusion
  169.2 1.3 copy.137
  170.5 2.2 convert_element_type.191
  172.7 2.3 maximum_bitcast_fusion
  175.0 2.9 gather_fusion
  177.9 2.5 fusion.35
  180.4 5.4 %all-to-all-start.1 = ((bf16[16,5,2,16,256]{4,3,2,1,0:T(8,128)(2,1)}), bf16[16,5,2,16,256]{4,3,2,1,0:T(8,128)(2,1)}, u32[]{:S(2)}, u32[]{:S(2)}) async-start(bf16[16,5,2,16,256]{4,3,2,1,0:T(8,128)(2,1)} %fusion.35), calls=%async_computation.1 | async-start | bytes 2621440 | tf_op jit(solution)/shard_map/all_to_all | solution.py:87
  185.8 1.9 subtract_convert_fusion
  192.3 2.0 fusion.67
  194.3 2.0 fusion.68
  196.3 1.5 fusion.69
  197.9 2.2 fusion.65
  200.1 2.1 convolution_convert_fusion.3
  202.2 10.8 %all-to-all-done.1 = bf16[16,5,2,16,256]{4,3,2,1,0:T(8,128)(2,1)} async-done(((bf16[16,5,2,16,256]{4,3,2,1,0:T(8,128)(2,1)}), bf16[16,5,2,16,256]{4,3,2,1,0:T(8,128)(2,1)}, u32[]{:S(2)}, u32[]{:S(2)}) %all-to-all-start.1) | async-done | bytes 1310752 | tf_op jit(solution)/shard_map/all_to_all | solution.py:87
  214.1 2.3 slice.285
  217.5 9.1 %scatter_fusion = bf16[64,2,16,256]{3,2,1,0:T(8,128)(2,1)} fusion(bf16[64,2,16,256]{3,2,1,0:T(8,128)(2,1)} %broadcast_in_dim.217, s32[64]{0:T(128)S(1)} %fusion.193, bf16[64,2,16,256]{3,2,1,0:T(8,128)(2,1)} %bitcast.183), kind=kCustom, calls=%fused_computation.2 | custom fusion | bytes 3145984 | tf_op jit(solution)/shard_map/scatter | solution.py:92
  226.6 4.5 all-to-all-start.2
  234.5 41.7 %all-to-all-done.2 = bf16[8,64,2048]{2,1,0:T(8,128)(2,1)} async-done(((bf16[8,64,2048]{2,1,0:T(8,128)(2,1)}), bf16[8,64,2048]{2,1,0:T(8,128)(2,1)}, u32[]{:S(2)}, u32[]{:S(2)}) %all-to-all-start.2) | async-done | bytes 2097184 | tf_op jit(solution)/shard_map/all_to_all | solution.py:123
  276.2 2.0 convert_reduce_fusion.4
  279.6 1.6 broadcast_in_dim.224
  281.3 5.3 %all-to-all-start.3 = ((bf16[8,64,2048]{2,1,0:T(8,128)(2,1)}), bf16[8,64,2048]{2,1,0:T(8,128)(2,1)}, u32[]{:S(2)}, u32[]{:S(2)}) async-start(bf16[8,64,2048]{2,1,0:T(8,128)(2,1)} %broadcast_in_dim.224), calls=%async_computation.3 | async-start | bytes 4194304 | tf_op jit(solution)/shard_map/all_to_all | solution.py:117
  289.8 1.4 fusion.66
  291.2 1.3 fusion.70
  292.5 2.0 fusion.71
  294.5 2.1 fusion.64
  296.7 2.1 convolution_convert_fusion.2
  298.8 16.6 %all-to-all-done.3 = bf16[8,64,2048]{2,1,0:T(8,128)(2,1)} async-done(((bf16[8,64,2048]{2,1,0:T(8,128)(2,1)}), bf16[8,64,2048]{2,1,0:T(8,128)(2,1)}, u32[]{:S(2)}, u32[]{:S(2)}) %all-to-all-start.3) | async-done | bytes 2097184 | tf_op jit(solution)/shard_map/all_to_all | solution.py:117
  315.3 35.0 %all_to_all.40 = bf16[8,64,2048]{2,1,0:T(8,128)(2,1)S(1)} all-to-all(bf16[8,64,2048]{2,1,0:T(8,128)(2,1)} %bitcast.174), channel_id=1, replica_groups=mesh['chips'=8,'core'=2,'tensor'=8] {'tensor'}, dimensions={0} | all-to-all | bytes 4194304 | tf_op jit(solution)/shard_map/all_to_all | solution.py:123
  351.3 1.6 broadcast_in_dim.225
  352.9 3.9 all-to-all-start.5
  356.8 5.2 %select_bitcast_fusion.1 = (bf16[3,8,1,128,1024]{4,3,1,0,2:T(8,128)(2,1)S(1)}, bf16[3,8,1,128,1024]{4,3,1,0,2:T(8,128)(2,1)S(1)}) fusion(bf16[3,8,128,1024]{3,2,1,0:T(8,128)(2,1)} %bitcast.178, bf16[3,8,128,1024]{3,2,1,0:T(8,128)(2,1)} %collective-permute-done.1, pred[]{:T(512)S(6)} %eq.150), kind=kLoop, calls=%fused_computation.21 | loop fusion | flops 6291456 | bytes 25165824 | tf_op jit(solution)/shard_map/stack | solution.py:99
  362.4 3.7 fusion.12
  366.1 2.4 copy.148
  368.4 21.4 %copy.147 = bf16[2,8,2,128,1024]{3,2,1,4,0:T(2,128)(2,1)} copy(bf16[2,8,2,128,1024]{4,3,1,0,2:T(8,128)(2,1)} %fusion.12) | data formatting | bytes 16777216 | tf_op jit(solution)/shard_map/slice | solution.py:196
  389.9 14.4 %slice.236 = bf16[2,2048,1024]{1,2,0:T(8,128)(2,1)} reshape(bf16[2,8,2,128,1024]{3,2,1,4,0:T(2,128)(2,1)} %copy.147) | data formatting | bytes 16777216 | tf_op jit(solution)/shard_map/slice | solution.py:196
  404.3 7.8 %convolution_bitcast_fusion.1 = f32[2,512,1024]{1,2,0:T(8,128)S(1)} fusion(bf16[2,2048,1024]{1,2,0:T(8,128)(2,1)} %slice.236, bf16[512,2048]{1,0:T(8,128)(2,1)} %bitcast.65), kind=kOutput, calls=%fused_computation.37 | convolution fusion | flops 4294967296 | bytes 14680064 | tf_op jit(solution)/shard_map/td,cdf->ctf/dot_general | solution.py:196
  412.1 3.8 convolution_convert_fusion.1
  415.9 7.1 %convolution_bitcast_fusion = f32[2,512,1024]{1,2,0:T(8,128)S(1)} fusion(bf16[2,2048,1024]{1,2,0:T(8,128)(2,1)} %slice.236, bf16[512,2048]{1,0:T(8,128)(2,1)S(1)} %bitcast.186), kind=kOutput, calls=%fused_computation.36 | convolution fusion | flops 4294967296 | bytes 14680064 | tf_op jit(solution)/shard_map/td,cdf->ctf/dot_general | solution.py:196
  423.0 2.5 convolution_convert_fusion
  425.6 32.4 %all_to_all.41 = bf16[8,64,2048]{2,1,0:T(8,128)(2,1)} all-to-all(bf16[8,64,2048]{2,1,0:T(8,128)(2,1)S(1)} %bitcast.188), channel_id=1, replica_groups=mesh['chips'=8,'core'=2,'tensor'=8] {'tensor'}, dimensions={0} | all-to-all | bytes 4194304 | tf_op jit(solution)/shard_map/all_to_all | solution.py:123
  458.0 3.6 all-to-all-start.6
  461.6 2.0 convert_reduce_fusion.1
  463.7 26.5 %all-to-all-done.6 = bf16[8,64,2048]{2,1,0:T(8,128)(2,1)S(1)} async-done(((bf16[8,64,2048]{2,1,0:T(8,128)(2,1)}), bf16[8,64,2048]{2,1,0:T(8,128)(2,1)S(1)}, u32[]{:S(2)}, u32[]{:S(2)}) %all-to-all-start.6) | async-done | bytes 2097184 | tf_op jit(solution)/shard_map/all_to_all | solution.py:123
  (171 shorter events, 33.2 us)
Async XLA Ops:
  7.2 101.3 %all-gather.5.cloned.1.call-start = ((), (), s32[]{:S(2)}) async-start(), calls=%async_computation.8 | async-start | bytes 2359296 | tf_op jit(solution)/shard_map/all_gather | solution.py:96
  13.5 8.5 %copy-start.16 = (bf16[1024,128]{1,0:T(8,128)(2,1)S(1)}, bf16[1024,128]{1,0:T(8,128)(2,1)}, u32[]{:S(2)}) copy-start(bf16[1024,128]{1,0:T(8,128)(2,1)} %param.24) | copy-start | bytes 786436
  13.5 8.6 %copy-start.12 = (bf16[2,128,1024]{2,1,0:T(8,128)(2,1)S(1)}, bf16[2,128,1024]{2,1,0:T(8,128)(2,1)}, u32[]{:S(2)}) copy-start(bf16[2,128,1024]{2,1,0:T(8,128)(2,1)} %param.23) | copy-start | bytes 1572868
  13.5 9.6 %copy-start.26 = (s32[1024]{0:T(1024)S(1)}, s32[1024]{0:T(1024)}, u32[]{:S(2)}) copy-start(s32[1024]{0:T(1024)} %param.19) | copy-start | bytes 12292
  13.5 9.7 %copy-start.28 = (s32[1024]{0:T(1024)S(1)}, s32[1024]{0:T(1024)}, u32[]{:S(2)}) copy-start(s32[1024]{0:T(1024)} %param.20) | copy-start | bytes 12292
  13.5 10.4 %copy-start = (s32[64]{0:T(128)S(1)}, s32[64]{0:T(128)}, u32[]{:S(2)}) copy-start(s32[64]{0:T(128)} %param.25) | copy-start | bytes 772
  13.5 99.4 %all-to-all-start = ((bf16[8,128,2048]{2,1,0:T(8,128)(2,1)}), bf16[8,128,2048]{2,1,0:T(8,128)(2,1)}, u32[]{:S(2)}, u32[]{:S(2)}) async-start(bf16[8,128,2048]{2,1,0:T(8,128)(2,1)} %broadcast_in_dim.119), calls=%async_computation | async-start | bytes 8388608 | tf_op jit(solution)/shard_map/all_to_all | solution.py:117
  21.8 5.3 %slice-start.1 = ((s32[1024]{0:T(1024)}), s32[256]{0:T(256)S(1)}, s32[]{:S(2)}) async-start(s32[1024]{0:T(1024)} %param.19), calls=%async_computation.11 | async-start | bytes 2048 | tf_op jit(solution)/shard_map/slice | solution.py:180
  21.8 5.3 %copy-start.35 = (s32[128]{0:T(128)S(1)}, s32[128]{0:T(128)}, u32[]{:S(2)}) copy-start(s32[128]{0:T(128)} %constant.142.clone) | copy-start | bytes 1540
  21.8 5.3 %copy-start.36 = (s32[128]{0:T(128)S(1)}, s32[128]{0:T(128)}, u32[]{:S(2)}) copy-start(s32[128]{0:T(128)} %constant.146.clone) | copy-start | bytes 1540
  21.8 6.0 %slice-start = ((s32[1024]{0:T(1024)}), s32[512]{0:T(512)S(1)}, s32[]{:S(2)}) async-start(s32[1024]{0:T(1024)} %param.19), calls=%async_computation.10 | async-start | bytes 4096 | tf_op jit(solution)/shard_map/slice | solution.py:180
  21.8 6.0 %copy-start.33 = (s32[128]{0:T(128)S(1)}, s32[128]{0:T(128)}, u32[]{:S(2)}) copy-start(s32[128]{0:T(128)} %constant.143.clone) | copy-start | bytes 1540
  21.9 6.0 %copy-start.34 = (s32[128]{0:T(128)S(1)}, s32[128]{0:T(128)}, u32[]{:S(2)}) copy-start(s32[128]{0:T(128)} %constant.147.clone) | copy-start | bytes 1540
  21.9 6.8 %copy-start.31 = (s32[128]{0:T(128)S(1)}, s32[128]{0:T(128)}, u32[]{:S(2)}) copy-start(s32[128]{0:T(128)} %constant.144.clone) | copy-start | bytes 1540
  21.9 6.8 %copy-start.32 = (s32[128]{0:T(128)S(1)}, s32[128]{0:T(128)}, u32[]{:S(2)}) copy-start(s32[128]{0:T(128)} %constant.148.clone) | copy-start | bytes 1540
  21.9 7.7 %copy-start.29 = (s32[128]{0:T(128)S(1)}, s32[128]{0:T(128)}, u32[]{:S(2)}) copy-start(s32[128]{0:T(128)} %constant.145.clone) | copy-start | bytes 1540
  21.9 7.7 %copy-start.30 = (s32[128]{0:T(128)S(1)}, s32[128]{0:T(128)}, u32[]{:S(2)}) copy-start(s32[128]{0:T(128)} %constant.149.clone) | copy-start | bytes 1540
  21.9 256.5 %all-gather.7.cloned.1.call-start = ((), (), s32[]{:S(2)}) async-start(), calls=%async_computation.9 | async-start | bytes 7077888 | tf_op jit(solution)/shard_map/all_gather | solution.py:96
  27.9 161.0 %copy-start.27 = (pred[128,256]{1,0:T(8,128)(4,1)}, pred[128,256]{1,0:T(8,128)(4,1)S(1)}, u32[]{:S(2)}) copy-start(pred[128,256]{1,0:T(8,128)(4,1)S(1)} %get-tuple-element.74) | copy-start | bytes 98308
  28.6 161.1 %copy-start.23 = (pred[128,512]{1,0:T(8,128)(4,1)}, pred[128,512]{1,0:T(8,128)(4,1)S(1)}, u32[]{:S(2)}) copy-start(pred[128,512]{1,0:T(8,128)(4,1)S(1)} %get-tuple-element.72) | copy-start | bytes 196612
  108.5 15.2 %collective-permute-start = (bf16[4,8,128,256]{3,2,1,0:T(8,128)(2,1)}, bf16[4,8,128,256]{3,2,1,0:T(8,128)(2,1)}, u32[]{:S(2)}, u32[]{:S(2)}) collective-permute-start(bf16[4,8,128,256]{3,2,1,0:T(8,128)(2,1)} %bitcast.191), channel_id=1, source_target_pairs={{0,8},{8,0},{1,9},{9,1},{2,10},{10,2},{3,11},{11,3},{4,12},{12,4},... | collective-permute-start | bytes 6291464 | tf_op jit(solution)/shard_map/ppermute | solution.py:97
  119.2 4.5 copy-start.8
  125.8 1.4 copy-start.1
  150.2 1.7 copy-start.5
  155.1 2.1 copy-start.6
  159.8 7.3 %copy-start.2 = (f32[1024,64]{1,0:T(8,128)S(1)}, f32[1024,64]{1,0:T(8,128)}, u32[]{:S(2)}) copy-start(f32[1024,64]{1,0:T(8,128)} %get-tuple-element.65) | copy-start | bytes 786436
  180.4 32.5 %all-to-all-start.1 = ((bf16[16,5,2,16,256]{4,3,2,1,0:T(8,128)(2,1)}), bf16[16,5,2,16,256]{4,3,2,1,0:T(8,128)(2,1)}, u32[]{:S(2)}, u32[]{:S(2)}) async-start(bf16[16,5,2,16,256]{4,3,2,1,0:T(8,128)(2,1)} %fusion.35), calls=%async_computation.1 | async-start | bytes 2621440 | tf_op jit(solution)/shard_map/all_to_all | solution.py:87
  187.7 2.6 copy-start.21
  188.8 0.7 copy-start.15
  189.5 2.4 copy-start.19
  191.0 1.0 copy-start.10
  196.3 3.7 copy-start.24
  196.3 3.7 copy-start.25
  217.5 13.6 %copy-start.14 = (bf16[2,1,64,2,128]{4,2,1,0,3:T(8,128)(2,1)S(1)}, bf16[2,1,64,2,128]{4,2,1,0,3:T(8,128)(2,1)}, u32[]{:S(2)}) copy-start(bf16[2,1,64,2,128]{4,2,1,0,3:T(8,128)(2,1)} %get-tuple-element.57) | copy-start | bytes 196612
  226.6 5.7 %copy-start.20 = (pred[128,768]{1,0:T(8,128)(4,1)S(1)}, pred[128,768]{1,0:T(8,128)(4,1)}, u32[]{:S(2)}) copy-start(pred[128,768]{1,0:T(8,128)(4,1)} %get-tuple-element.69) | copy-start | bytes 294916
  226.6 6.9 %copy-start.17 = (bf16[2,1,64,2,128]{4,2,1,0,3:T(8,128)(2,1)S(1)}, bf16[2,1,64,2,128]{4,2,1,0,3:T(8,128)(2,1)}, u32[]{:S(2)}) copy-start(bf16[2,1,64,2,128]{4,2,1,0,3:T(8,128)(2,1)} %get-tuple-element.55) | copy-start | bytes 196612
  226.6 49.6 %all-to-all-start.2 = ((bf16[8,64,2048]{2,1,0:T(8,128)(2,1)}), bf16[8,64,2048]{2,1,0:T(8,128)(2,1)}, u32[]{:S(2)}, u32[]{:S(2)}) async-start(bf16[8,64,2048]{2,1,0:T(8,128)(2,1)} %bitcast.173), calls=%async_computation.2 | async-start | bytes 4194304 | tf_op jit(solution)/shard_map/all_to_all | solution.py:123
  231.1 47.1 %copy-start.7 = (bf16[128,2048]{1,0:T(8,128)(2,1)S(1)}, bf16[128,2048]{1,0:T(8,128)(2,1)}, u32[]{:S(2)}) copy-start(bf16[128,2048]{1,0:T(8,128)(2,1)} %param.18) | copy-start | bytes 1572868
  231.4 0.9 copy-start.11
  278.4 78.4 %collective-permute-start.1 = (bf16[3,8,128,1024]{3,2,1,0:T(8,128)(2,1)}, bf16[3,8,128,1024]{3,2,1,0:T(8,128)(2,1)}, u32[]{:S(2)}, u32[]{:S(2)}) collective-permute-start(bf16[3,8,128,1024]{3,2,1,0:T(8,128)(2,1)} %bitcast.177), channel_id=1, source_target_pairs={{0,8},{8,0},{1,9},{9,1},{2,10},{10,2},{3,11},{11,3},{4,12},{12,4},... | collective-permute-start | bytes 18874376 | tf_op jit(solution)/shard_map/ppermute | solution.py:97
  279.6 7.0 %copy-start.22 = (pred[128,512]{1,0:T(8,128)(4,1)S(1)}, pred[128,512]{1,0:T(8,128)(4,1)}, u32[]{:S(2)}) copy-start(pred[128,512]{1,0:T(8,128)(4,1)} %get-tuple-element.73) | copy-start | bytes 196612
  281.3 5.3 %copy-start.13 = (f32[2,128,512]{2,1,0:T(8,128)S(1)}, f32[2,128,512]{2,1,0:T(8,128)}, u32[]{:S(2)}) copy-start(f32[2,128,512]{2,1,0:T(8,128)} %convolution_multiply_fusion.4) | copy-start | bytes 1572868
  281.3 34.0 %all-to-all-start.3 = ((bf16[8,64,2048]{2,1,0:T(8,128)(2,1)}), bf16[8,64,2048]{2,1,0:T(8,128)(2,1)}, u32[]{:S(2)}, u32[]{:S(2)}) async-start(bf16[8,64,2048]{2,1,0:T(8,128)(2,1)} %broadcast_in_dim.224), calls=%async_computation.3 | async-start | bytes 4194304 | tf_op jit(solution)/shard_map/all_to_all | solution.py:117
  286.6 2.8 copy-start.18
  288.5 1.0 copy-start.9
  352.9 63.0 %all-to-all-start.5 = ((bf16[8,64,2048]{2,1,0:T(8,128)(2,1)}), bf16[8,64,2048]{2,1,0:T(8,128)(2,1)S(1)}, u32[]{:S(2)}, u32[]{:S(2)}) async-start(bf16[8,64,2048]{2,1,0:T(8,128)(2,1)} %broadcast_in_dim.225), calls=%async_computation.5 | async-start | bytes 4194304 | tf_op jit(solution)/shard_map/all_to_all | solution.py:117
  404.3 7.8 %copy-start.3 = (bf16[1,8,2,128,1024]{4,3,2,1,0:T(8,128)(2,1)S(1)}, bf16[1,8,2,128,1024]{4,3,2,1,0:T(8,128)(2,1)}, u32[]{:S(2)}) copy-start(bf16[1,8,2,128,1024]{4,3,2,1,0:T(8,128)(2,1)} %copy.148) | copy-start | bytes 12582916
  415.9 7.1 %copy-start.4 = (bf16[1,8,2,128,1024]{4,3,2,1,0:T(8,128)(2,1)S(1)}, bf16[1,8,2,128,1024]{4,3,2,1,0:T(8,128)(2,1)}, u32[]{:S(2)}) copy-start(bf16[1,8,2,128,1024]{4,3,2,1,0:T(8,128)(2,1)} %copy.148) | copy-start | bytes 12582916
  458.0 32.2 %all-to-all-start.6 = ((bf16[8,64,2048]{2,1,0:T(8,128)(2,1)}), bf16[8,64,2048]{2,1,0:T(8,128)(2,1)S(1)}, u32[]{:S(2)}, u32[]{:S(2)}) async-start(bf16[8,64,2048]{2,1,0:T(8,128)(2,1)} %bitcast.187), calls=%async_computation.6 | async-start | bytes 4194304 | tf_op jit(solution)/shard_map/all_to_all | solution.py:123
Sparse Core Ops, SparseCore 0:
  10.2 98.2 all-gather.4
  110.1 167.1 all-gather.6

commit v10 on v6

--- a/solution.py
+++ b/solution.py
@@ -69,19 +69,25 @@
     page_size = tokens // pages
     owners = lax.axis_size("dp")
     per_owner = pages // owners
+    me = lax.axis_index("dp")
+    base = 128
     stacked = jnp.stack([keys.reshape(tokens, width), values.reshape(tokens, width)], axis=0)
     stacked = stacked.reshape(2, pages, page_size, width).transpose(1, 0, 2, 3)
     page_table, stacked = lax.optimization_barrier((page_table, stacked))
     order = jnp.argsort(page_table // pages, stable=True)
-    outgoing = stacked[order].reshape(owners, per_owner, 2, page_size, width)
-    outgoing_ids = page_table[order].reshape(owners, per_owner)
-    arrived, arrived_ids = (
-        lax.all_to_all(outgoing, "dp", split_axis=0, concat_axis=0, tiled=True),
-        lax.all_to_all(outgoing_ids, "dp", split_axis=0, concat_axis=0, tiled=True),
+    sorted_ids = page_table[order].reshape(owners, per_owner)
+    code = jnp.stack([sorted_ids // base, sorted_ids % base], axis=-1).astype(jnp.bfloat16)
+    slab = jnp.zeros((owners, 1, 2, page_size, width), jnp.bfloat16)
+    slab = slab.at[:, 0, 0, 0, : 2 * per_owner].set(code.reshape(owners, 2 * per_owner))
+    outgoing = jnp.concatenate(
+        [stacked[order].reshape(owners, per_owner, 2, page_size, width), slab], axis=1
     )
-    local = (arrived_ids - lax.axis_index("dp") * pages).reshape(-1)
+    arrived = lax.all_to_all(outgoing, "dp", split_axis=0, concat_axis=0, tiled=True)
+    codes = arrived[:, per_owner, 0, 0, : 2 * per_owner].astype(jnp.int32)
+    codes = codes.reshape(owners, per_owner, 2)
+    local = (codes[..., 0] * base + codes[..., 1] - me * pages).reshape(-1)
     empty = jnp.zeros((pages, 2, page_size, width), jnp.bfloat16)
-    return empty.at[local].set(arrived.reshape(pages, 2, page_size, width))
+    return empty.at[local].set(arrived[:, :per_owner].reshape(pages, 2, page_size, width))
 
 
 def gather_packed(pieces, axis_name):

time: 379 us -> 369 us (0.974)
  waiting for transfers between devices: 132 us -> 120 us
  blocking collectives: 88.6 us -> 98.6 us
  starting transfers between devices: 30.6 us -> 26.6 us
  local copies, waits for them, and re-layouts: 32.2 us -> 28.4 us
    all_to_all x1, waiting for transfers between devices: 13.8 us -> 1.1 us  [write_cache(): lax.all_to_all(outgoing, 'dp', split_axis=0, concat_axis=0, tiled=True)]
    all_to_all x1, blocking collectives: 57.7 us -> 65.2 us  [sum_rows(): lax.all_to_all(terms.reshape(count, terms.shape[0] // count, terms.shape[...]
    unnamed x40 -> x56, local copies, waits for them, and re-layouts: 14.4 us -> 12.7 us
  transfers between devices with their start and end apart: 8 -> 7, of which waited for: 6 -> 6; matrix products, arithmetic and copies ran while one was open for 27% -> 27% of each run, Pallas kernels for 0% -> 0%
where the time goes in v10:
time: 369 us; the launch traced here: 367 us
  waiting for transfers between devices  120 us (33%)
  blocking collectives  98.6 us (27%)
  matrix products  50.6 us (14%)
  other arithmetic  29 us (8%)
  local copies, waits for them, and re-layouts  28.4 us (8%)
  starting transfers between devices  26.6 us (7%)
  between operations  14.6 us (4%)
    all_to_all x2, waiting for transfers between devices, gather_rows(): gathered = lax.all_to_all(copies, axis_name, 0, 0, tiled=True)  66.8 us
    all_to_all x1, blocking collectives, sum_rows(): lax.all_to_all(terms.reshape(count, terms.shape[0] // count, terms.shape[...  65.2 us
    all_to_all x2, waiting for transfers between devices, sum_rows(): lax.all_to_all(terms.reshape(count, terms.shape[0] // count, terms.shape[...  43.1 us
    all_to_all x1, blocking collectives, gather_rows(): gathered = lax.all_to_all(copies, axis_name, 0, 0, tiled=True)  33.5 us
    dot_general x2, matrix products, body(): jnp.einsum('td,cdf->ctf', rows, mlp_w[:2], preferred_element_type=jnp.flo...  15.3 us
    all_to_all x2, starting transfers between devices, gather_rows(): gathered = lax.all_to_all(copies, axis_name, 0, 0, tiled=True)  13.5 us
    unnamed x56, local copies, waits for them, and re-layouts  12.7 us
    dot_general x2, matrix products, body(): jnp.einsum('tf,df->td', hidden, mlp_w[2], preferred_element_type=jnp.floa...  12.3 us
  transfers between devices with their start and end apart: 7, of which 6 were waited for; matrix products, arithmetic and copies ran while one was open for 27% of the time, Pallas kernels for 0%

profile of v10, /device:TPU:1, one launch (start us, length us, event | category | flops | bytes accessed | tf_op | source)
XLA Modules:
  0.0 367.4 jit_solution(17837561756394996634)
XLA Ops:
  7.2 1.1 copy.86
  8.4 1.6 pad_maximum_fusion.3
  10.1 1.3 copy.101
  11.4 1.0 pad_maximum_fusion
  12.4 2.5 broadcast_in_dim.43
  15.0 8.3 %all-to-all-start = ((bf16[8,128,2048]{2,1,0:T(8,128)(2,1)}), bf16[8,128,2048]{2,1,0:T(8,128)(2,1)}, u32[]{:S(2)}, u32[]{:S(2)}) async-start(bf16[8,128,2048]{2,1,0:T(8,128)(2,1)} %broadcast_in_dim.43), calls=%async_computation | async-start | bytes 8388608 | tf_op jit(solution)/shard_map/all_to_all | solution.py:107
  23.4 1.0 compare_and_fusion
  24.3 1.4 fusion.24
  25.7 1.9 multiply_cosine_fusion
  27.6 52.0 %all-to-all-done = bf16[8,128,2048]{2,1,0:T(8,128)(2,1)} async-done(((bf16[8,128,2048]{2,1,0:T(8,128)(2,1)}), bf16[8,128,2048]{2,1,0:T(8,128)(2,1)}, u32[]{:S(2)}, u32[]{:S(2)}) %all-to-all-start) | async-done | bytes 4194336 | tf_op jit(solution)/shard_map/all_to_all | solution.py:107
  79.6 2.9 convert_reduce_fusion.1
  82.5 3.4 multiply_reduce_fusion
  86.0 4.2 %fusion.3 = bf16[1024,2048]{1,0:T(8,128)(2,1)} fusion(bf16[8,128,2048]{2,1,0:T(8,128)(2,1)} %all-to-all-done, f32[1024]{0:T(1024)S(1)} %rsqrt_bitcast_fusion, f32[1024]{0:T(1024)S(1)} %get-tuple-element.46), kind=kLoop, calls=%fused_computation.7 | loop fusion | flops 8388608 | bytes 8396800 | tf_op jit(solution)/shard_map/convert_element_type | solution.py:130
  90.2 8.6 %all-gather.3.cloned.1.call-done = bf16[4,2048,256]{1,2,0:T(8,128)(2,1)} async-done(((bf16[4,128,256]{1,2,0:T(8,128)(2,1)}), bf16[4,2048,256]{1,2,0:T(8,128)(2,1)}) %all-gather.3.cloned.1.call-update) | async-done | bytes 4194320 | tf_op jit(solution)/shard_map/all_gather | solution.py:123
  98.8 6.2 %fusion.27 = f32[3,1024,256]{1,2,0:T(8,128)S(1)} fusion(bf16[4,2048,256]{1,2,0:T(8,128)(2,1)} %all-gather.3.cloned.1.call-done, bf16[1024,2048]{1,0:T(8,128)(2,1)} %fusion.3), kind=kOutput, calls=%fused_computation.44 | convolution fusion | flops 3221225472 | bytes 11534336 | tf_op jit(solution)/shard_map/td,cdf->ctf/dot_general | solution.py:132
  105.0 1.6 copy-done.8
  106.8 1.0 copy.93
  107.8 3.0 fusion.83
  110.7 0.9 fusion.84
  111.6 0.3 copy.105
  112.0 1.4 copy.106
  113.4 0.3 multiply_subtract_fusion
  113.6 0.3 maximum_convert_fusion
  114.0 0.5 copy.92
  114.5 0.3 convert_element_type.130
  115.0 2.0 sort.17
  117.0 0.8 gather_fusion.1
  118.1 0.6 gather_fusion
  118.8 1.3 fusion.30
  120.0 3.9 %all-to-all-start.1 = ((bf16[16,5,2,16,256]{4,3,2,1,0:T(8,128)(2,1)}), bf16[16,5,2,16,256]{4,3,2,1,0:T(8,128)(2,1)S(1)}, u32[]{:S(2)}, u32[]{:S(2)}) async-start(bf16[16,5,2,16,256]{4,3,2,1,0:T(8,128)(2,1)} %fusion.30), calls=%async_computation.1 | async-start | bytes 2621440 | tf_op jit(solution)/shard_map/all_to_all | solution.py:85
  124.0 1.0 fusion.85
  125.0 1.4 copy.103
  126.4 2.4 copy.104
  128.7 1.6 subtract_convert_fusion
  130.3 0.8 copy-done.14
  131.3 0.5 fusion.58
  131.8 1.1 fusion.90
  133.2 4.2 %fusion.40 = bf16[512,2,128]{0,2,1:T(8,128)(2,1)} fusion(bf16[512,2,128]{0,2,1:T(8,128)(2,1)S(1)} %bitcast.104, f32[512,2]{0,1:T(2,128)S(1)} %bitcast.117, f32[2,512,512]{1,2,0:T(8,128)} %copy-done.12, pred[512,512]{0,1:T(8,128)(4,1)S(1)} %copy-done.18), kind=kOutput, calls=%fused_computation.55 | convolution fusion | flops 137627136 | bytes 2887680 | tf_op jit(solution)/shard_map/hqk,khd->qhd/dot_general | solution.py:55
  137.4 5.1 %fusion.89 = (f32[2,512]{1,0:T(2,128)S(1)}, bf16[2,512,1024]{2,1,0:T(8,128)(2,1)}) fusion(pred[512,1024]{1,0:T(8,128)(4,1)} %fusion.24, bf16[1024,2,128]{2,0,1:T(8,128)(2,1)S(1)} %copy-done.7, bf16[1024,2,64]{2,0,1:T(8,128)(2,1)S(1)} %copy-done.17, bf16[1024,2,64]{2,0,1:T(8,128)(2,1)S(1)} %copy-done.15), kind=kOutput, calls=%fused_computation.130 | convolution fusion | flops 545260544 | bytes 3674112 | tf_op jit(solution)/shard_map/sub | solution.py:53
  142.6 2.5 fusion.41
  145.1 4.5 %convolution_convert_fusion = bf16[1024,2048]{1,0:T(8,128)(2,1)} fusion(bf16[1024,256]{0,1:T(8,128)(2,1)S(1)} %bitcast.105, bf16[4,2048,256]{1,2,0:T(8,128)(2,1)} %all-gather.3.cloned.1.call-done), kind=kOutput, calls=%fused_computation.19 | convolution fusion | flops 1075838976 | bytes 5767168 | tf_op jit(solution)/shard_map/tr,dr->td/dot_general | solution.py:138
  149.6 1.1 all-to-all-done.1
  151.3 2.5 scatter_fusion
  153.8 65.2 %all_to_all.35 = bf16[8,128,2048]{2,1,0:T(8,128)(2,1)S(1)} all-to-all(bf16[8,128,2048]{2,1,0:T(8,128)(2,1)} %bitcast.98), channel_id=1, replica_groups=mesh['dp'=16,'tensor'=8] {'tensor'}, dimensions={0} | all-to-all | bytes 8388608 | tf_op jit(solution)/shard_map/all_to_all | solution.py:113
  219.0 0.7 convert_reduce_fusion
  219.7 0.3 copy-done.10
  220.3 0.3 fusion.44
  220.6 0.3 fusion.45
  221.2 33.5 %all_to_all.36 = bf16[8,64,2048]{2,1,0:T(8,128)(2,1)} all-to-all(bf16[8,64,2048]{2,1,0:T(8,128)(2,1)S(1)} %broadcast_in_dim.55), channel_id=1, replica_groups=mesh['dp'=16,'tensor'=8] {'tensor'}, dimensions={0} | all-to-all | bytes 4194304 | tf_op jit(solution)/shard_map/all_to_all | solution.py:107
  254.7 1.6 broadcast_in_dim.56
  256.2 5.2 %all-to-all-start.5 = ((bf16[8,64,2048]{2,1,0:T(8,128)(2,1)}), bf16[8,64,2048]{2,1,0:T(8,128)(2,1)S(1)}, u32[]{:S(2)}, u32[]{:S(2)}) async-start(bf16[8,64,2048]{2,1,0:T(8,128)(2,1)} %broadcast_in_dim.56), calls=%async_computation.5 | async-start | bytes 4194304 | tf_op jit(solution)/shard_map/all_to_all | solution.py:107
  261.5 7.6 %convolution_bitcast_fusion.1 = f32[2,512,1024]{1,2,0:T(8,128)S(1)} fusion(bf16[3,2048,1024]{1,2,0:T(8,128)(2,1)} %all-gather.5.cloned.1.call-done, bf16[512,2048,1]{1,0,2:T(8,128)(2,1)} %bitcast.108), kind=kOutput, calls=%fused_computation.28 | convolution fusion | flops 4294967296 | bytes 18874368 | tf_op jit(solution)/shard_map/td,cdf->ctf/dot_general | solution.py:148
  269.1 6.1 %fusion.12 = bf16[512,2048]{1,0:T(8,128)(2,1)} fusion(bf16[3,2048,1024]{1,2,0:T(8,128)(2,1)} %all-gather.5.cloned.1.call-done, f32[2,512,1024]{1,2,0:T(8,128)S(1)} %convolution_bitcast_fusion.1), kind=kOutput, calls=%fused_computation.23 | convolution fusion | flops 2151677952 | bytes 10485760 | tf_op jit(solution)/shard_map/tf,df->td/dot_general | solution.py:150
  275.3 14.8 %all-to-all-done.5 = bf16[8,64,2048]{2,1,0:T(8,128)(2,1)S(1)} async-done(((bf16[8,64,2048]{2,1,0:T(8,128)(2,1)}), bf16[8,64,2048]{2,1,0:T(8,128)(2,1)S(1)}, u32[]{:S(2)}, u32[]{:S(2)}) %all-to-all-start.5) | async-done | bytes 2097184 | tf_op jit(solution)/shard_map/all_to_all | solution.py:107
  290.1 1.3 copy-done.11
  291.4 4.7 %all-to-all-start.4 = ((bf16[8,64,2048]{2,1,0:T(8,128)(2,1)}), bf16[8,64,2048]{2,1,0:T(8,128)(2,1)S(1)}, u32[]{:S(2)}, u32[]{:S(2)}) async-start(bf16[8,64,2048]{2,1,0:T(8,128)(2,1)} %bitcast.107), calls=%async_computation.4 | async-start | bytes 4194304 | tf_op jit(solution)/shard_map/all_to_all | solution.py:113
  296.1 7.6 %convolution_bitcast_fusion = f32[2,512,1024]{1,2,0:T(8,128)S(1)} fusion(bf16[3,2048,1024]{1,2,0:T(8,128)(2,1)} %all-gather.5.cloned.1.call-done, bf16[512,2048,1]{1,0,2:T(8,128)(2,1)} %bitcast.106), kind=kOutput, calls=%fused_computation.27 | convolution fusion | flops 4294967296 | bytes 18874368 | tf_op jit(solution)/shard_map/td,cdf->ctf/dot_general | solution.py:148
  303.7 6.1 %fusion.13 = bf16[512,2048]{1,0:T(8,128)(2,1)} fusion(bf16[3,2048,1024]{1,2,0:T(8,128)(2,1)} %all-gather.5.cloned.1.call-done, f32[2,512,1024]{1,2,0:T(8,128)S(1)} %convolution_bitcast_fusion), kind=kOutput, calls=%fused_computation.24 | convolution fusion | flops 2151677952 | bytes 10485760 | tf_op jit(solution)/shard_map/tf,df->td/dot_general | solution.py:150
  309.8 14.8 %all-to-all-done.4 = bf16[8,64,2048]{2,1,0:T(8,128)(2,1)S(1)} async-done(((bf16[8,64,2048]{2,1,0:T(8,128)(2,1)}), bf16[8,64,2048]{2,1,0:T(8,128)(2,1)S(1)}, u32[]{:S(2)}, u32[]{:S(2)}) %all-to-all-start.4) | async-done | bytes 2097184 | tf_op jit(solution)/shard_map/all_to_all | solution.py:113
  324.7 4.3 %all-to-all-start.6 = ((bf16[8,64,2048]{2,1,0:T(8,128)(2,1)}), bf16[8,64,2048]{2,1,0:T(8,128)(2,1)}, u32[]{:S(2)}, u32[]{:S(2)}) async-start(bf16[8,64,2048]{2,1,0:T(8,128)(2,1)} %bitcast.109), calls=%async_computation.6 | async-start | bytes 4194304 | tf_op jit(solution)/shard_map/all_to_all | solution.py:113
  329.0 0.3 convert_reduce_fusion.3
  329.4 28.3 %all-to-all-done.6 = bf16[8,64,2048]{2,1,0:T(8,128)(2,1)} async-done(((bf16[8,64,2048]{2,1,0:T(8,128)(2,1)}), bf16[8,64,2048]{2,1,0:T(8,128)(2,1)}, u32[]{:S(2)}, u32[]{:S(2)}) %all-to-all-start.6) | async-done | bytes 2097184 | tf_op jit(solution)/shard_map/all_to_all | solution.py:113
  357.6 2.0 convert_reduce_fusion.2
  359.6 0.9 fusion.46
  (86 shorter events, 2.3 us)
Async XLA Ops:
  7.2 4.2 %copy-start.19 = (bf16[1024,128]{1,0:T(8,128)(2,1)S(1)}, bf16[1024,128]{1,0:T(8,128)(2,1)}, u32[]{:S(2)}) copy-start(bf16[1024,128]{1,0:T(8,128)(2,1)} %param.16) | copy-start | bytes 786436
  7.2 91.7 %all-gather.3.cloned.1.call-start = ((), (), s32[]{:S(2)}) async-start(), calls=%async_computation.7 | async-start | bytes 4456448 | tf_op jit(solution)/shard_map/all_gather | solution.py:123
  8.3 4.1 %copy-start.9 = (bf16[128,2048]{1,0:T(8,128)(2,1)S(1)}, bf16[128,2048]{1,0:T(8,128)(2,1)}, u32[]{:S(2)}) copy-start(bf16[128,2048]{1,0:T(8,128)(2,1)} %param.10) | copy-start | bytes 1572868
  10.0 251.5 %all-gather.5.cloned.1.call-start = ((), (), s32[]{:S(2)}) async-start(), calls=%async_computation.8 | async-start | bytes 13369344 | tf_op jit(solution)/shard_map/all_gather | solution.py:126
  15.0 8.3 %copy-start.22 = (s32[1024]{0:T(1024)S(1)}, s32[1024]{0:T(1024)}, u32[]{:S(2)}) copy-start(s32[1024]{0:T(1024)} %param.12) | copy-start | bytes 12292
  15.0 8.4 %copy-start.21 = (s32[1024]{0:T(1024)S(1)}, s32[1024]{0:T(1024)}, u32[]{:S(2)}) copy-start(s32[1024]{0:T(1024)} %param.11) | copy-start | bytes 12292
  15.0 64.6 %all-to-all-start = ((bf16[8,128,2048]{2,1,0:T(8,128)(2,1)}), bf16[8,128,2048]{2,1,0:T(8,128)(2,1)}, u32[]{:S(2)}, u32[]{:S(2)}) async-start(bf16[8,128,2048]{2,1,0:T(8,128)(2,1)} %broadcast_in_dim.43), calls=%async_computation | async-start | bytes 8388608 | tf_op jit(solution)/shard_map/all_to_all | solution.py:107
  105.0 1.6 copy-start.8
  106.7 4.0 %copy-start.3 = (bf16[1,1024,256]{1,2,0:T(8,128)(2,1)}, bf16[1,1024,256]{1,2,0:T(8,128)(2,1)S(1)}, u32[]{:S(2)}) copy-start(bf16[1,1024,256]{1,2,0:T(8,128)(2,1)S(1)} %slice.224) | copy-start | bytes 1572868
  113.6 1.2 copy-start.13
  113.9 0.9 copy-start.5
  114.0 1.0 copy-start
  120.0 4.0 %copy-start.2 = (f32[1,1024,256]{1,2,0:T(8,128)S(1)}, f32[1,1024,256]{1,2,0:T(8,128)}, u32[]{:S(2)}) copy-start(f32[1,1024,256]{1,2,0:T(8,128)} %get-tuple-element.29) | copy-start | bytes 3145732
  120.0 30.7 %all-to-all-start.1 = ((bf16[16,5,2,16,256]{4,3,2,1,0:T(8,128)(2,1)}), bf16[16,5,2,16,256]{4,3,2,1,0:T(8,128)(2,1)S(1)}, u32[]{:S(2)}, u32[]{:S(2)}) async-start(bf16[16,5,2,16,256]{4,3,2,1,0:T(8,128)(2,1)} %fusion.30), calls=%async_computation.1 | async-start | bytes 2621440 | tf_op jit(solution)/shard_map/all_to_all | solution.py:85
  128.7 2.5 copy-start.6
  130.3 0.8 copy-start.14
  130.3 1.0 copy-start.16
  130.3 1.5 copy-start.18
  131.8 1.3 copy-start.12
  131.8 1.3 slice-start
  133.1 4.3 %copy-start.7 = (bf16[1024,2,128]{2,0,1:T(8,128)(2,1)S(1)}, bf16[1024,2,128]{2,0,1:T(8,128)(2,1)}, u32[]{:S(2)}) copy-start(bf16[1024,2,128]{2,0,1:T(8,128)(2,1)} %copy-done.5) | copy-start | bytes 1572868
  133.1 4.3 %copy-start.15 = (bf16[1024,2,64]{2,0,1:T(8,128)(2,1)S(1)}, bf16[1024,2,64]{2,0,1:T(8,128)(2,1)}, u32[]{:S(2)}) copy-start(bf16[1024,2,64]{2,0,1:T(8,128)(2,1)} %copy-done.14) | copy-start | bytes 786436
  133.2 4.3 %copy-start.17 = (bf16[1024,2,64]{2,0,1:T(8,128)(2,1)S(1)}, bf16[1024,2,64]{2,0,1:T(8,128)(2,1)}, u32[]{:S(2)}) copy-start(bf16[1024,2,64]{2,0,1:T(8,128)(2,1)} %copy-done.16) | copy-start | bytes 786436
  137.4 5.2 %copy-start.4 = (bf16[1,1024,256]{1,2,0:T(8,128)(2,1)S(1)}, bf16[1,1024,256]{1,2,0:T(8,128)(2,1)}, u32[]{:S(2)}) copy-start(bf16[1,1024,256]{1,2,0:T(8,128)(2,1)} %copy-done.3) | copy-start | bytes 1572868
  142.6 2.5 copy-start.20
  153.8 65.2 %copy-start.1 = (bf16[64,2,16,256]{3,2,1,0:T(8,128)(2,1)}, bf16[64,2,16,256]{3,2,1,0:T(8,128)(2,1)S(1)}, u32[]{:S(2)}) copy-start(bf16[64,2,16,256]{3,2,1,0:T(8,128)(2,1)S(1)} %scatter_fusion) | copy-start | bytes 3145732
  219.0 1.0 copy-start.10
  256.2 33.9 %all-to-all-start.5 = ((bf16[8,64,2048]{2,1,0:T(8,128)(2,1)}), bf16[8,64,2048]{2,1,0:T(8,128)(2,1)S(1)}, u32[]{:S(2)}, u32[]{:S(2)}) async-start(bf16[8,64,2048]{2,1,0:T(8,128)(2,1)} %broadcast_in_dim.56), calls=%async_computation.5 | async-start | bytes 4194304 | tf_op jit(solution)/shard_map/all_to_all | solution.py:107
  290.1 1.3 copy-start.11
  291.4 33.3 %all-to-all-start.4 = ((bf16[8,64,2048]{2,1,0:T(8,128)(2,1)}), bf16[8,64,2048]{2,1,0:T(8,128)(2,1)S(1)}, u32[]{:S(2)}, u32[]{:S(2)}) async-start(bf16[8,64,2048]{2,1,0:T(8,128)(2,1)} %bitcast.107), calls=%async_computation.4 | async-start | bytes 4194304 | tf_op jit(solution)/shard_map/all_to_all | solution.py:113
  324.7 33.0 %all-to-all-start.6 = ((bf16[8,64,2048]{2,1,0:T(8,128)(2,1)}), bf16[8,64,2048]{2,1,0:T(8,128)(2,1)}, u32[]{:S(2)}, u32[]{:S(2)}) async-start(bf16[8,64,2048]{2,1,0:T(8,128)(2,1)} %bitcast.109), calls=%async_computation.6 | async-start | bytes 4194304 | tf_op jit(solution)/shard_map/all_to_all | solution.py:113
Sparse Core Ops, SparseCore 0:
  10.2 88.6 all-gather.2
  100.4 146.1 all-gather.4

commit v11 on v10

--- a/solution.py
+++ b/solution.py
@@ -73,7 +73,6 @@
     base = 128
     stacked = jnp.stack([keys.reshape(tokens, width), values.reshape(tokens, width)], axis=0)
     stacked = stacked.reshape(2, pages, page_size, width).transpose(1, 0, 2, 3)
-    page_table, stacked = lax.optimization_barrier((page_table, stacked))
     order = jnp.argsort(page_table // pages, stable=True)
     sorted_ids = page_table[order].reshape(owners, per_owner)
     code = jnp.stack([sorted_ids // base, sorted_ids % base], axis=-1).astype(jnp.bfloat16)
@@ -126,8 +125,7 @@
     mlp_w = lax.all_gather(
         jnp.concatenate([w_gate_up, jnp.transpose(w_down)[None]], axis=0), "dp", axis=1, tiled=True
     )
-    full_stream = gather_rows(stream, "tensor")
-    normed = layer_norm(full_stream).astype(jnp.bfloat16)
+    normed = gather_rows(layer_norm(stream).astype(jnp.bfloat16), "tensor")
     local_heads = local_cols // HD
     projected = jnp.einsum("td,cdf->ctf", normed, attn_w[:3], preferred_element_type=jnp.float32)
     query = rotate(projected[0].reshape(tok_group, local_heads, HD), position).astype(jnp.bfloat16)

time: 369 us -> 374 us (1.014)
  waiting for transfers between devices: 120 us -> 129 us
  other arithmetic: 29 us -> 23.1 us
    all_gather x1, waiting for transfers between devices: 8.61 us -> 19.3 us  [body(): lax.all_gather(jnp.concatenate([w_qkv, jnp.transpose(w_out)[None]], axis=...]
    all_to_all x2, waiting for transfers between devices: 66.8 us -> 62.3 us  [gather_rows(): gathered = lax.all_to_all(copies, axis_name, 0, 0, tiled=True)]
    convert_element_type x1, other arithmetic: 4.23 us -> 0.32 us  [body(): normed = gather_rows(layer_norm(stream).astype(jnp.bfloat16), 'tensor')]
    unnamed x56 -> x42, local copies, waits for them, and re-layouts: 12.7 us -> 13.4 us
  transfers between devices with their start and end apart: 7 -> 7, of which waited for: 6 -> 6; matrix products, arithmetic and copies ran while one was open for 27% -> 26% of each run, Pallas kernels for 0% -> 0%
where the time goes in v11:
time: 374 us; the launch traced here: 372 us
  waiting for transfers between devices  129 us (34%)
  blocking collectives  97.7 us (26%)
  matrix products  50.8 us (14%)
  local copies, waits for them, and re-layouts  31.7 us (8%)
  starting transfers between devices  25.2 us (7%)
  other arithmetic  23.1 us (6%)
  between operations  14.5 us (4%)
    all_to_all x1, blocking collectives, sum_rows(): lax.all_to_all(terms.reshape(count, terms.shape[0] // count, terms.shape[...  65.3 us
    all_to_all x2, waiting for transfers between devices, gather_rows(): gathered = lax.all_to_all(copies, axis_name, 0, 0, tiled=True)  62.3 us
    all_to_all x2, waiting for transfers between devices, sum_rows(): lax.all_to_all(terms.reshape(count, terms.shape[0] // count, terms.shape[...  43.1 us
    all_to_all x1, blocking collectives, gather_rows(): gathered = lax.all_to_all(copies, axis_name, 0, 0, tiled=True)  32.4 us
    all_gather x1, waiting for transfers between devices, body(): lax.all_gather(jnp.concatenate([w_qkv, jnp.transpose(w_out)[None]], axis=...  19.3 us
    dot_general x2, matrix products, body(): jnp.einsum('td,cdf->ctf', rows, mlp_w[:2], preferred_element_type=jnp.flo...  15.3 us
    unnamed x42, local copies, waits for them, and re-layouts  13.4 us
    dot_general x2, matrix products, body(): jnp.einsum('tf,df->td', hidden, mlp_w[2], preferred_element_type=jnp.floa...  12.3 us
  transfers between devices with their start and end apart: 7, of which 6 were waited for; matrix products, arithmetic and copies ran while one was open for 26% of the time, Pallas kernels for 0%

profile of v11, /device:TPU:1, one launch (start us, length us, event | category | flops | bytes accessed | tf_op | source)
XLA Modules:
  0.0 372.2 jit_solution(2468420375434121068)
XLA Ops:
  7.2 1.1 copy.86
  8.4 1.6 pad_maximum_fusion.3
  10.1 1.3 copy.101
  11.4 1.0 pad_maximum_fusion
  12.6 0.3 fusion.41
  12.9 0.3 fusion.42
  13.2 2.5 broadcast_in_dim.43
  15.7 8.3 %all-to-all-start = ((bf16[8,128,2048]{2,1,0:T(8,128)(2,1)}), bf16[8,128,2048]{2,1,0:T(8,128)(2,1)}, u32[]{:S(2)}, u32[]{:S(2)}) async-start(bf16[8,128,2048]{2,1,0:T(8,128)(2,1)} %broadcast_in_dim.43), calls=%async_computation | async-start | bytes 8388608 | tf_op jit(solution)/shard_map/all_to_all | solution.py:106
  24.1 2.0 sort.17
  26.1 0.8 gather_fusion.1
  27.3 1.0 compare_and_fusion
  28.3 1.4 fusion.20
  29.7 1.9 multiply_cosine_fusion
  31.5 47.8 %all-to-all-done = bf16[8,128,2048]{2,1,0:T(8,128)(2,1)} async-done(((bf16[8,128,2048]{2,1,0:T(8,128)(2,1)}), bf16[8,128,2048]{2,1,0:T(8,128)(2,1)}, u32[]{:S(2)}, u32[]{:S(2)}) %all-to-all-start) | async-done | bytes 4194336 | tf_op jit(solution)/shard_map/all_to_all | solution.py:106
  79.3 19.3 %all-gather.3.cloned.1.call-done = bf16[4,2048,256]{1,2,0:T(8,128)(2,1)} async-done(((bf16[4,128,256]{1,2,0:T(8,128)(2,1)}), bf16[4,2048,256]{1,2,0:T(8,128)(2,1)}) %all-gather.3.cloned.1.call-update) | async-done | bytes 4194320 | tf_op jit(solution)/shard_map/all_gather | solution.py:122
  98.7 6.2 %convolution_bitcast_fusion.2 = f32[3,1024,256]{1,2,0:T(8,128)S(1)} fusion(bf16[4,2048,256]{1,2,0:T(8,128)(2,1)} %all-gather.3.cloned.1.call-done, bf16[1024,2048,1]{1,0,2:T(8,128)(2,1)} %bitcast.3), kind=kOutput, calls=%fused_computation.37 | convolution fusion | flops 3221225472 | bytes 11534336 | tf_op jit(solution)/shard_map/td,cdf->ctf/dot_general | solution.py:130
  104.9 1.7 copy-done.5
  106.6 1.0 copy.93
  107.6 2.8 fusion.81
  110.4 0.9 fusion.82
  111.3 1.4 copy.105
  112.7 1.4 copy.106
  114.0 2.1 fusion.83
  116.1 2.4 copy.103
  118.5 1.3 copy.104
  119.8 1.5 multiply_subtract_fusion
  121.3 0.3 maximum_convert_fusion
  121.6 0.5 copy.92
  122.2 1.1 convert_element_type.118
  123.3 1.3 maximum_bitcast_fusion
  124.6 1.6 gather_fusion
  126.3 2.5 fusion.23
  128.7 3.9 %all-to-all-start.1 = ((bf16[16,5,2,16,256]{4,3,2,1,0:T(8,128)(2,1)}), bf16[16,5,2,16,256]{4,3,2,1,0:T(8,128)(2,1)S(1)}, u32[]{:S(2)}, u32[]{:S(2)}) async-start(bf16[16,5,2,16,256]{4,3,2,1,0:T(8,128)(2,1)} %fusion.23), calls=%async_computation.1 | async-start | bytes 2621440 | tf_op jit(solution)/shard_map/all_to_all | solution.py:84
  132.6 1.8 subtract_convert_fusion
  134.4 0.8 copy-done.8
  135.4 0.5 fusion.56
  135.9 1.1 fusion.88
  137.2 4.1 %fusion.35 = bf16[512,2,128]{0,2,1:T(8,128)(2,1)} fusion(bf16[512,2,128]{0,2,1:T(8,128)(2,1)S(1)} %bitcast.93, f32[512,2]{0,1:T(2,128)S(1)} %bitcast.106, f32[2,512,512]{1,2,0:T(8,128)} %copy-done.7, pred[512,512]{0,1:T(8,128)(4,1)S(1)} %copy-done.11), kind=kOutput, calls=%fused_computation.53 | convolution fusion | flops 137627136 | bytes 2887680 | tf_op jit(solution)/shard_map/hqk,khd->qhd/dot_general | solution.py:55
  141.4 5.4 %fusion.87 = (f32[2,512]{1,0:T(2,128)S(1)}, bf16[2,512,1024]{2,1,0:T(8,128)(2,1)}) fusion(pred[512,1024]{1,0:T(8,128)(4,1)} %fusion.20, bf16[1024,2,128]{2,0,1:T(8,128)(2,1)S(1)} %maximum_convert_fusion, bf16[1024,2,64]{2,0,1:T(8,128)(2,1)} %copy-done.10, bf16[1024,2,64]{2,0,1:T(8,128)(2,1)S(1)} %copy-done.9), kind=kOutput, calls=%fused_computation.129 | convolution fusion | flops 545260544 | bytes 3674112 | tf_op jit(solution)/shard_map/sub | solution.py:53
  146.8 2.5 fusion.36
  149.3 4.5 %convolution_convert_fusion = bf16[1024,2048]{1,0:T(8,128)(2,1)} fusion(bf16[1024,256]{0,1:T(8,128)(2,1)S(1)} %bitcast.94, bf16[4,2048,256]{1,2,0:T(8,128)(2,1)} %all-gather.3.cloned.1.call-done), kind=kOutput, calls=%fused_computation.12 | convolution fusion | flops 1075838976 | bytes 5767168 | tf_op jit(solution)/shard_map/tr,dr->td/dot_general | solution.py:136
  153.8 4.5 %all-to-all-done.1 = bf16[16,5,2,16,256]{4,3,2,1,0:T(8,128)(2,1)S(1)} async-done(((bf16[16,5,2,16,256]{4,3,2,1,0:T(8,128)(2,1)}), bf16[16,5,2,16,256]{4,3,2,1,0:T(8,128)(2,1)S(1)}, u32[]{:S(2)}, u32[]{:S(2)}) %all-to-all-start.1) | async-done | bytes 1310752 | tf_op jit(solution)/shard_map/all_to_all | solution.py:84
  158.9 2.5 scatter_fusion
  161.4 65.3 %all_to_all.35 = bf16[8,128,2048]{2,1,0:T(8,128)(2,1)S(1)} all-to-all(bf16[8,128,2048]{2,1,0:T(8,128)(2,1)} %bitcast.87), channel_id=1, replica_groups=mesh['dp'=16,'tensor'=8] {'tensor'}, dimensions={0} | all-to-all | bytes 8388608 | tf_op jit(solution)/shard_map/all_to_all | solution.py:112
  226.7 0.7 convert_reduce_fusion
  227.6 0.3 fusion.39
  227.9 0.3 fusion.40
  228.3 0.2 broadcast_in_dim.55
  228.6 32.4 %all_to_all.36 = bf16[8,64,2048]{2,1,0:T(8,128)(2,1)} all-to-all(bf16[8,64,2048]{2,1,0:T(8,128)(2,1)S(1)} %broadcast_in_dim.55), channel_id=1, replica_groups=mesh['dp'=16,'tensor'=8] {'tensor'}, dimensions={0} | all-to-all | bytes 4194304 | tf_op jit(solution)/shard_map/all_to_all | solution.py:106
  261.0 1.6 broadcast_in_dim.56
  262.5 3.8 %all-to-all-start.5 = ((bf16[8,64,2048]{2,1,0:T(8,128)(2,1)}), bf16[8,64,2048]{2,1,0:T(8,128)(2,1)S(1)}, u32[]{:S(2)}, u32[]{:S(2)}) async-start(bf16[8,64,2048]{2,1,0:T(8,128)(2,1)} %broadcast_in_dim.56), calls=%async_computation.5 | async-start | bytes 4194304 | tf_op jit(solution)/shard_map/all_to_all | solution.py:106
  266.4 7.6 %convolution_bitcast_fusion.1 = f32[2,512,1024]{1,2,0:T(8,128)S(1)} fusion(bf16[3,2048,1024]{1,2,0:T(8,128)(2,1)} %all-gather.5.cloned.1.call-done, bf16[512,2048,1]{1,0,2:T(8,128)(2,1)} %bitcast.97), kind=kOutput, calls=%fused_computation.21 | convolution fusion | flops 4294967296 | bytes 18874368 | tf_op jit(solution)/shard_map/td,cdf->ctf/dot_general | solution.py:146
  274.1 6.2 %fusion.8 = bf16[512,2048]{1,0:T(8,128)(2,1)} fusion(bf16[3,2048,1024]{1,2,0:T(8,128)(2,1)} %all-gather.5.cloned.1.call-done, f32[2,512,1024]{1,2,0:T(8,128)S(1)} %convolution_bitcast_fusion.1), kind=kOutput, calls=%fused_computation.16 | convolution fusion | flops 2151677952 | bytes 10485760 | tf_op jit(solution)/shard_map/tf,df->td/dot_general | solution.py:148
  280.2 14.5 %all-to-all-done.5 = bf16[8,64,2048]{2,1,0:T(8,128)(2,1)S(1)} async-done(((bf16[8,64,2048]{2,1,0:T(8,128)(2,1)}), bf16[8,64,2048]{2,1,0:T(8,128)(2,1)S(1)}, u32[]{:S(2)}, u32[]{:S(2)}) %all-to-all-start.5) | async-done | bytes 2097184 | tf_op jit(solution)/shard_map/all_to_all | solution.py:106
  294.7 1.3 copy-done.6
  296.0 3.6 all-to-all-start.4
  299.6 7.6 %convolution_bitcast_fusion = f32[2,512,1024]{1,2,0:T(8,128)S(1)} fusion(bf16[3,2048,1024]{1,2,0:T(8,128)(2,1)} %all-gather.5.cloned.1.call-done, bf16[512,2048,1]{1,0,2:T(8,128)(2,1)} %bitcast.95), kind=kOutput, calls=%fused_computation.20 | convolution fusion | flops 4294967296 | bytes 18874368 | tf_op jit(solution)/shard_map/td,cdf->ctf/dot_general | solution.py:146
  307.3 6.2 %fusion.9 = bf16[512,2048]{1,0:T(8,128)(2,1)} fusion(bf16[3,2048,1024]{1,2,0:T(8,128)(2,1)} %all-gather.5.cloned.1.call-done, f32[2,512,1024]{1,2,0:T(8,128)S(1)} %convolution_bitcast_fusion), kind=kOutput, calls=%fused_computation.17 | convolution fusion | flops 2151677952 | bytes 10485760 | tf_op jit(solution)/shard_map/tf,df->td/dot_general | solution.py:148
  313.4 14.7 %all-to-all-done.4 = bf16[8,64,2048]{2,1,0:T(8,128)(2,1)S(1)} async-done(((bf16[8,64,2048]{2,1,0:T(8,128)(2,1)}), bf16[8,64,2048]{2,1,0:T(8,128)(2,1)S(1)}, u32[]{:S(2)}, u32[]{:S(2)}) %all-to-all-start.4) | async-done | bytes 2097184 | tf_op jit(solution)/shard_map/all_to_all | solution.py:112
  328.2 5.6 %all-to-all-start.6 = ((bf16[8,64,2048]{2,1,0:T(8,128)(2,1)}), bf16[8,64,2048]{2,1,0:T(8,128)(2,1)}, u32[]{:S(2)}, u32[]{:S(2)}) async-start(bf16[8,64,2048]{2,1,0:T(8,128)(2,1)} %bitcast.98), calls=%async_computation.6 | async-start | bytes 4194304 | tf_op jit(solution)/shard_map/all_to_all | solution.py:112
  333.7 0.3 convert_reduce_fusion.2
  334.1 28.4 %all-to-all-done.6 = bf16[8,64,2048]{2,1,0:T(8,128)(2,1)} async-done(((bf16[8,64,2048]{2,1,0:T(8,128)(2,1)}), bf16[8,64,2048]{2,1,0:T(8,128)(2,1)}, u32[]{:S(2)}, u32[]{:S(2)}) %all-to-all-start.6) | async-done | bytes 2097184 | tf_op jit(solution)/shard_map/all_to_all | solution.py:112
  362.5 2.0 convert_reduce_fusion.1
  364.5 0.9 fusion.44
  (72 shorter events, 2.1 us)
Async XLA Ops:
  7.2 4.2 %copy-start.12 = (bf16[1024,128]{1,0:T(8,128)(2,1)S(1)}, bf16[1024,128]{1,0:T(8,128)(2,1)}, u32[]{:S(2)}) copy-start(bf16[1024,128]{1,0:T(8,128)(2,1)} %param.16) | copy-start | bytes 786436
  7.2 91.5 %all-gather.3.cloned.1.call-start = ((), (), s32[]{:S(2)}) async-start(), calls=%async_computation.7 | async-start | bytes 4456448 | tf_op jit(solution)/shard_map/all_gather | solution.py:122
  8.3 4.1 %copy-start.1 = (bf16[128,2048]{1,0:T(8,128)(2,1)S(1)}, bf16[128,2048]{1,0:T(8,128)(2,1)}, u32[]{:S(2)}) copy-start(bf16[128,2048]{1,0:T(8,128)(2,1)} %param.10) | copy-start | bytes 1572868
  10.0 256.4 %all-gather.5.cloned.1.call-start = ((), (), s32[]{:S(2)}) async-start(), calls=%async_computation.8 | async-start | bytes 13369344 | tf_op jit(solution)/shard_map/all_gather | solution.py:125
  15.7 8.3 %copy-start.15 = (s32[1024]{0:T(1024)S(1)}, s32[1024]{0:T(1024)}, u32[]{:S(2)}) copy-start(s32[1024]{0:T(1024)} %param.12) | copy-start | bytes 12292
  15.7 8.3 %copy-start = (s32[64]{0:T(128)S(1)}, s32[64]{0:T(128)}, u32[]{:S(2)}) copy-start(s32[64]{0:T(128)} %param.17) | copy-start | bytes 772
  15.7 11.5 %copy-start.14 = (s32[1024]{0:T(1024)S(1)}, s32[1024]{0:T(1024)}, u32[]{:S(2)}) copy-start(s32[1024]{0:T(1024)} %param.11) | copy-start | bytes 12292
  15.7 63.6 %all-to-all-start = ((bf16[8,128,2048]{2,1,0:T(8,128)(2,1)}), bf16[8,128,2048]{2,1,0:T(8,128)(2,1)}, u32[]{:S(2)}, u32[]{:S(2)}) async-start(bf16[8,128,2048]{2,1,0:T(8,128)(2,1)} %broadcast_in_dim.43), calls=%async_computation | async-start | bytes 8388608 | tf_op jit(solution)/shard_map/all_to_all | solution.py:106
  104.9 1.7 copy-start.5
  106.6 3.8 %copy-start.3 = (bf16[1,1024,256]{1,2,0:T(8,128)(2,1)}, bf16[1,1024,256]{1,2,0:T(8,128)(2,1)S(1)}, u32[]{:S(2)}) copy-start(bf16[1,1024,256]{1,2,0:T(8,128)(2,1)S(1)} %slice.224) | copy-start | bytes 1572868
  128.7 29.6 %all-to-all-start.1 = ((bf16[16,5,2,16,256]{4,3,2,1,0:T(8,128)(2,1)}), bf16[16,5,2,16,256]{4,3,2,1,0:T(8,128)(2,1)S(1)}, u32[]{:S(2)}, u32[]{:S(2)}) async-start(bf16[16,5,2,16,256]{4,3,2,1,0:T(8,128)(2,1)} %fusion.23), calls=%async_computation.1 | async-start | bytes 2621440 | tf_op jit(solution)/shard_map/all_to_all | solution.py:84
  134.4 0.8 copy-start.8
  134.4 1.0 copy-start.10
  134.4 1.5 copy-start.11
  135.9 1.3 copy-start.7
  135.9 1.3 slice-start
  137.2 4.1 %copy-start.9 = (bf16[1024,2,64]{2,0,1:T(8,128)(2,1)S(1)}, bf16[1024,2,64]{2,0,1:T(8,128)(2,1)}, u32[]{:S(2)}) copy-start(bf16[1024,2,64]{2,0,1:T(8,128)(2,1)} %copy-done.8) | copy-start | bytes 786436
  141.4 5.4 %copy-start.4 = (bf16[1,1024,256]{1,2,0:T(8,128)(2,1)S(1)}, bf16[1,1024,256]{1,2,0:T(8,128)(2,1)}, u32[]{:S(2)}) copy-start(bf16[1,1024,256]{1,2,0:T(8,128)(2,1)} %copy-done.3) | copy-start | bytes 1572868
  146.8 2.5 copy-start.13
  161.4 65.3 %copy-start.2 = (bf16[64,2,16,256]{3,2,1,0:T(8,128)(2,1)}, bf16[64,2,16,256]{3,2,1,0:T(8,128)(2,1)S(1)}, u32[]{:S(2)}) copy-start(bf16[64,2,16,256]{3,2,1,0:T(8,128)(2,1)S(1)} %scatter_fusion) | copy-start | bytes 3145732
  262.5 32.2 %all-to-all-start.5 = ((bf16[8,64,2048]{2,1,0:T(8,128)(2,1)}), bf16[8,64,2048]{2,1,0:T(8,128)(2,1)S(1)}, u32[]{:S(2)}, u32[]{:S(2)}) async-start(bf16[8,64,2048]{2,1,0:T(8,128)(2,1)} %broadcast_in_dim.56), calls=%async_computation.5 | async-start | bytes 4194304 | tf_op jit(solution)/shard_map/all_to_all | solution.py:106
  294.7 1.3 copy-start.6
  296.0 32.2 %all-to-all-start.4 = ((bf16[8,64,2048]{2,1,0:T(8,128)(2,1)}), bf16[8,64,2048]{2,1,0:T(8,128)(2,1)S(1)}, u32[]{:S(2)}, u32[]{:S(2)}) async-start(bf16[8,64,2048]{2,1,0:T(8,128)(2,1)} %bitcast.96), calls=%async_computation.4 | async-start | bytes 4194304 | tf_op jit(solution)/shard_map/all_to_all | solution.py:112
  328.2 34.3 %all-to-all-start.6 = ((bf16[8,64,2048]{2,1,0:T(8,128)(2,1)}), bf16[8,64,2048]{2,1,0:T(8,128)(2,1)}, u32[]{:S(2)}, u32[]{:S(2)}) async-start(bf16[8,64,2048]{2,1,0:T(8,128)(2,1)} %bitcast.98), calls=%async_computation.6 | async-start | bytes 4194304 | tf_op jit(solution)/shard_map/all_to_all | solution.py:112
Sparse Core Ops, SparseCore 0:
  10.2 88.4 all-gather.2
  100.3 134.4 all-gather.4

commit v12 on v10

--- a/solution.py
+++ b/solution.py
@@ -120,22 +120,27 @@
     tok_group = segment.shape[0]
     share_rows = stream.shape[0]
     local_cols = w_qkv.shape[2]
-    attn_w = lax.all_gather(
-        jnp.concatenate([w_qkv, jnp.transpose(w_out)[None]], axis=0), "dp", axis=1, tiled=True
+    attn_local = jnp.concatenate([w_qkv, jnp.transpose(w_out)[None]], axis=0)
+    owners = lax.axis_size("dp")
+    attn_w = lax.all_to_all(
+        jnp.broadcast_to(attn_local[None], (owners,) + attn_local.shape), "dp", 0, 0, tiled=True
     )
     mlp_w = lax.all_gather(
         jnp.concatenate([w_gate_up, jnp.transpose(w_down)[None]], axis=0), "dp", axis=1, tiled=True
     )
-    full_stream = gather_rows(stream, "tensor")
+    full_stream = lax.all_gather(stream, "tensor", axis=0, tiled=True)
     normed = layer_norm(full_stream).astype(jnp.bfloat16)
+    normed = normed.reshape(tok_group, owners, normed.shape[1] // owners)
     local_heads = local_cols // HD
-    projected = jnp.einsum("td,cdf->ctf", normed, attn_w[:3], preferred_element_type=jnp.float32)
+    projected = jnp.einsum("tgd,gcdf->ctf", normed, attn_w[:, :3], preferred_element_type=jnp.float32)
     query = rotate(projected[0].reshape(tok_group, local_heads, HD), position).astype(jnp.bfloat16)
     keys = rotate(projected[1].reshape(tok_group, local_heads, HD), position).astype(jnp.bfloat16)
     values = projected[2].reshape(tok_group, local_heads, HD).astype(jnp.bfloat16)
     kv_cache = write_cache(keys, values, page_table)
     context = attend(query, keys, values, segment)
-    attn_part = jnp.einsum("tr,dr->td", context, attn_w[3], preferred_element_type=jnp.float32)
+    attn_part = jnp.einsum(
+        "tr,gdr->tgd", context, attn_w[:, 3], preferred_element_type=jnp.float32
+    ).reshape(tok_group, -1)
     attn_part, kv_cache = lax.optimization_barrier((attn_part.astype(jnp.bfloat16), kv_cache))
     attn_mine = sum_rows(attn_part, "tensor")
     mid = (stream.astype(jnp.float32) + attn_mine).astype(jnp.bfloat16)

time: 369 us -> 403 us (1.092)
  waiting for transfers between devices: 120 us -> 152 us
  local copies, waits for them, and re-layouts: 28.4 us -> 36.4 us
    all_to_all x2 -> x1, waiting for transfers between devices: 66.8 us -> 14.5 us  [gather_rows(): gathered = lax.all_to_all(copies, axis_name, 0, 0, tiled=True)]
    all_to_all x0 -> x1, waiting for transfers between devices: none -> 48.9 us  [body(): lax.all_to_all(jnp.broadcast_to(attn_local[None], (owners,) + attn_local....]
    all_gather x1, waiting for transfers between devices: 8.61 us -> 45.2 us  [body(): full_stream = lax.all_gather(stream, 'tensor', axis=0, tiled=True)]
    all_to_all x2 -> x1, starting transfers between devices: 13.5 us -> 3.82 us  [gather_rows(): gathered = lax.all_to_all(copies, axis_name, 0, 0, tiled=True)]
    all_to_all x0 -> x1, starting transfers between devices: none -> 7.46 us  [body(): lax.all_to_all(jnp.broadcast_to(attn_local[None], (owners,) + attn_local....]
    convert_element_type x1 -> x0, other arithmetic: 4.23 us -> none  [body(): normed = layer_norm(full_stream).astype(jnp.bfloat16)]
    unnamed x56 -> x50, local copies, waits for them, and re-layouts: 12.7 us -> 15.7 us
  transfers between devices with their start and end apart: 7 -> 7, of which waited for: 6 -> 5; matrix products, arithmetic and copies ran while one was open for 27% -> 26% of each run, Pallas kernels for 0% -> 0%
where the time goes in v12:
time: 403 us; the launch traced here: 400 us
  waiting for transfers between devices  152 us (38%)
  blocking collectives  94.7 us (23%)
  matrix products  49.2 us (12%)
  local copies, waits for them, and re-layouts  36.4 us (9%)
  starting transfers between devices  26.2 us (7%)
  other arithmetic  26.2 us (7%)
  between operations  14.6 us (4%)
    all_to_all x1, blocking collectives, sum_rows(): lax.all_to_all(terms.reshape(count, terms.shape[0] // count, terms.shape[...  62.2 us
    all_to_all x1, waiting for transfers between devices, body(): lax.all_to_all(jnp.broadcast_to(attn_local[None], (owners,) + attn_local....  48.9 us
    all_gather x1, waiting for transfers between devices, body(): full_stream = lax.all_gather(stream, 'tensor', axis=0, tiled=True)  45.2 us
    all_to_all x2, waiting for transfers between devices, sum_rows(): lax.all_to_all(terms.reshape(count, terms.shape[0] // count, terms.shape[...  43.1 us
    all_to_all x1, blocking collectives, gather_rows(): gathered = lax.all_to_all(copies, axis_name, 0, 0, tiled=True)  32.4 us
    unnamed x50, local copies, waits for them, and re-layouts  15.7 us
    dot_general x2, matrix products, body(): jnp.einsum('td,cdf->ctf', rows, mlp_w[:2], preferred_element_type=jnp.flo...  15.3 us
    all_to_all x1, waiting for transfers between devices, gather_rows(): gathered = lax.all_to_all(copies, axis_name, 0, 0, tiled=True)  14.5 us
  transfers between devices with their start and end apart: 7, of which 5 were waited for; matrix products, arithmetic and copies ran while one was open for 26% of the time, Pallas kernels for 0%

profile of v12, /device:TPU:1, one launch (start us, length us, event | category | flops | bytes accessed | tf_op | source)
XLA Modules:
  0.0 399.7 jit_solution(7340330005967639938)
XLA Ops:
  7.2 0.7 all-gather.3.cloned.1.call-update
  8.0 1.3 copy.122
  9.3 2.0 pad_maximum_fusion
  11.6 3.0 broadcast_in_dim.43
  14.6 7.5 %all-to-all-start = ((bf16[16,4,128,256]{2,3,1,0:T(8,128)(2,1)}), bf16[16,4,128,256]{2,3,1,0:T(8,128)(2,1)}, u32[]{:S(2)}, u32[]{:S(2)}) async-start(bf16[16,4,128,256]{2,3,1,0:T(8,128)(2,1)} %broadcast_in_dim.43), calls=%async_computation | async-start | bytes 8388608 | tf_op jit(solution)/shard_map/all_to_all | solution.py:125
  22.2 1.0 compare_and_fusion
  23.1 1.4 fusion.27
  24.5 1.9 multiply_cosine_fusion
  26.4 48.9 %all-to-all-done = bf16[16,4,128,256]{2,3,1,0:T(8,128)(2,1)} async-done(((bf16[16,4,128,256]{2,3,1,0:T(8,128)(2,1)}), bf16[16,4,128,256]{2,3,1,0:T(8,128)(2,1)}, u32[]{:S(2)}, u32[]{:S(2)}) %all-to-all-start) | async-done | bytes 4194336 | tf_op jit(solution)/shard_map/all_to_all | solution.py:125
  75.3 1.3 slice.172
  76.6 0.5 copy.130
  77.2 45.2 %all-gather.3.cloned.1.call-done = bf16[1024,2048]{1,0:T(8,128)(2,1)} async-done(((bf16[128,2048]{1,0:T(8,128)(2,1)}), bf16[1024,2048]{1,0:T(8,128)(2,1)}) %all-gather.3.cloned.1.call-update) | async-done | bytes 4194320 | tf_op jit(solution)/shard_map/all_gather | solution.py:131
  122.4 3.0 convert_reduce_fusion
  125.4 0.5 copy-done.1
  125.8 1.2 fusion.4
  127.1 5.6 %fusion.30 = f32[3,1024,256]{1,2,0:T(8,128)S(1)} fusion(bf16[16,4,128,256]{2,3,1,0:T(8,128)(2,1)} %all-to-all-done, bf16[1024,2048]{1,0:T(8,128)(2,1)S(1)} %copy-done.1, f32[1024]{0:T(1024)S(1)} %add_rsqrt_fusion, f32[1024]{0:T(1024)S(1)} %broadcast_multiply_fusion), kind=kOutput, calls=%fused_computation.47 | convolution fusion | flops 3229614080 | bytes 11542528 | tf_op jit(solution)/shard_map/tgd,gcdf->ctf/dot_general | solution.py:135
  132.7 1.6 copy-done.8
  134.4 1.0 copy.114
  135.4 2.7 fusion.83
  138.1 1.1 fusion.84
  139.2 1.4 copy.128
  140.5 2.4 copy.129
  143.0 1.5 multiply_subtract_fusion
  144.5 0.3 maximum_convert_fusion
  144.8 0.5 copy.113
  145.4 1.1 convert_element_type.121
  146.5 1.3 maximum_bitcast_fusion
  147.8 2.0 sort.17
  149.9 0.8 gather_fusion.1
  151.0 1.6 gather_fusion
  152.6 2.7 fusion.31
  155.4 5.7 %all-to-all-start.1 = ((bf16[16,5,2,16,256]{4,3,2,1,0:T(8,128)(2,1)}), bf16[16,5,2,16,256]{4,3,2,1,0:T(8,128)(2,1)S(1)}, u32[]{:S(2)}, u32[]{:S(2)}) async-start(bf16[16,5,2,16,256]{4,3,2,1,0:T(8,128)(2,1)} %fusion.31), calls=%async_computation.1 | async-start | bytes 2621440 | tf_op jit(solution)/shard_map/all_to_all | solution.py:85
  161.0 2.3 fusion.85
  163.3 2.4 copy.126
  165.7 2.4 copy.127
  168.1 1.9 subtract_convert_fusion
  170.0 0.8 copy-done.12
  170.9 0.5 fusion.59
  171.5 1.1 fusion.90
  172.8 4.1 %fusion.41 = bf16[512,2,128]{0,2,1:T(8,128)(2,1)} fusion(bf16[512,2,128]{0,2,1:T(8,128)(2,1)S(1)} %bitcast.111, f32[512,2]{0,1:T(2,128)S(1)} %bitcast.123, f32[2,512,512]{1,2,0:T(8,128)} %copy-done.11, pred[512,512]{0,1:T(8,128)(4,1)S(1)} %copy-done.14), kind=kOutput, calls=%fused_computation.58 | convolution fusion | flops 137627136 | bytes 2887680 | tf_op jit(solution)/shard_map/hqk,khd->qhd/dot_general | solution.py:55
  176.9 5.5 %fusion.89 = (f32[2,512]{1,0:T(2,128)S(1)}, bf16[2,512,1024]{2,1,0:T(8,128)(2,1)}) fusion(pred[512,1024]{1,0:T(8,128)(4,1)} %fusion.27, bf16[1024,2,128]{2,0,1:T(8,128)(2,1)S(1)} %copy-done.7, bf16[1024,2,64]{2,0,1:T(8,128)(2,1)} %copy-done.13, bf16[1024,2,64]{2,0,1:T(8,128)(2,1)} %copy-done.12), kind=kOutput, calls=%fused_computation.131 | convolution fusion | flops 545260544 | bytes 3674112 | tf_op jit(solution)/shard_map/sub | solution.py:53
  182.4 2.8 fusion.42
  185.2 3.3 convolution_convert_fusion
  189.1 2.5 scatter_fusion
  191.6 62.2 %all_to_all.35 = bf16[8,128,2048]{2,1,0:T(8,128)(2,1)S(1)} all-to-all(bf16[8,128,2048]{2,1,0:T(8,128)(2,1)} %bitcast.103), channel_id=1, replica_groups=mesh['dp'=16,'tensor'=8] {'tensor'}, dimensions={0} | all-to-all | bytes 8388608 | tf_op jit(solution)/shard_map/all_to_all | solution.py:113
  253.9 0.7 convert_reduce_fusion.1
  254.6 0.3 copy-done.9
  255.4 0.3 fusion.46
  256.0 32.4 %all_to_all.36 = bf16[8,64,2048]{2,1,0:T(8,128)(2,1)} all-to-all(bf16[8,64,2048]{2,1,0:T(8,128)(2,1)S(1)} %broadcast_in_dim.55), channel_id=1, replica_groups=mesh['dp'=16,'tensor'=8] {'tensor'}, dimensions={0} | all-to-all | bytes 4194304 | tf_op jit(solution)/shard_map/all_to_all | solution.py:107
  288.5 1.6 broadcast_in_dim.56
  290.0 3.8 all-to-all-start.5
  293.9 7.6 %convolution_bitcast_fusion.1 = f32[2,512,1024]{1,2,0:T(8,128)S(1)} fusion(bf16[3,2048,1024]{1,2,0:T(8,128)(2,1)} %all-gather.5.cloned.1.call-done, bf16[512,2048,1]{1,0,2:T(8,128)(2,1)} %bitcast.114), kind=kOutput, calls=%fused_computation.31 | convolution fusion | flops 4294967296 | bytes 18874368 | tf_op jit(solution)/shard_map/td,cdf->ctf/dot_general | solution.py:153
  301.6 6.2 %fusion.15 = bf16[512,2048]{1,0:T(8,128)(2,1)} fusion(bf16[3,2048,1024]{1,2,0:T(8,128)(2,1)} %all-gather.5.cloned.1.call-done, f32[2,512,1024]{1,2,0:T(8,128)S(1)} %convolution_bitcast_fusion.1), kind=kOutput, calls=%fused_computation.26 | convolution fusion | flops 2151677952 | bytes 10485760 | tf_op jit(solution)/shard_map/tf,df->td/dot_general | solution.py:155
  307.7 14.5 %all-to-all-done.5 = bf16[8,64,2048]{2,1,0:T(8,128)(2,1)S(1)} async-done(((bf16[8,64,2048]{2,1,0:T(8,128)(2,1)}), bf16[8,64,2048]{2,1,0:T(8,128)(2,1)S(1)}, u32[]{:S(2)}, u32[]{:S(2)}) %all-to-all-start.5) | async-done | bytes 2097184 | tf_op jit(solution)/shard_map/all_to_all | solution.py:107
  322.2 1.3 copy-done.10
  323.5 3.6 all-to-all-start.4
  327.1 7.6 %convolution_bitcast_fusion = f32[2,512,1024]{1,2,0:T(8,128)S(1)} fusion(bf16[3,2048,1024]{1,2,0:T(8,128)(2,1)} %all-gather.5.cloned.1.call-done, bf16[512,2048,1]{1,0,2:T(8,128)(2,1)} %bitcast.112), kind=kOutput, calls=%fused_computation.30 | convolution fusion | flops 4294967296 | bytes 18874368 | tf_op jit(solution)/shard_map/td,cdf->ctf/dot_general | solution.py:153
  334.8 6.1 %fusion.16 = bf16[512,2048]{1,0:T(8,128)(2,1)} fusion(bf16[3,2048,1024]{1,2,0:T(8,128)(2,1)} %all-gather.5.cloned.1.call-done, f32[2,512,1024]{1,2,0:T(8,128)S(1)} %convolution_bitcast_fusion), kind=kOutput, calls=%fused_computation.27 | convolution fusion | flops 2151677952 | bytes 10485760 | tf_op jit(solution)/shard_map/tf,df->td/dot_general | solution.py:155
  340.9 14.8 %all-to-all-done.4 = bf16[8,64,2048]{2,1,0:T(8,128)(2,1)S(1)} async-done(((bf16[8,64,2048]{2,1,0:T(8,128)(2,1)}), bf16[8,64,2048]{2,1,0:T(8,128)(2,1)S(1)}, u32[]{:S(2)}, u32[]{:S(2)}) %all-to-all-start.4) | async-done | bytes 2097184 | tf_op jit(solution)/shard_map/all_to_all | solution.py:113
  355.7 5.6 %all-to-all-start.6 = ((bf16[8,64,2048]{2,1,0:T(8,128)(2,1)}), bf16[8,64,2048]{2,1,0:T(8,128)(2,1)}, u32[]{:S(2)}, u32[]{:S(2)}) async-start(bf16[8,64,2048]{2,1,0:T(8,128)(2,1)} %bitcast.115), calls=%async_computation.6 | async-start | bytes 4194304 | tf_op jit(solution)/shard_map/all_to_all | solution.py:113
  361.2 0.3 convert_reduce_fusion.3
  361.6 28.4 %all-to-all-done.6 = bf16[8,64,2048]{2,1,0:T(8,128)(2,1)} async-done(((bf16[8,64,2048]{2,1,0:T(8,128)(2,1)}), bf16[8,64,2048]{2,1,0:T(8,128)(2,1)}, u32[]{:S(2)}, u32[]{:S(2)}) %all-to-all-start.6) | async-done | bytes 2097184 | tf_op jit(solution)/shard_map/all_to_all | solution.py:113
  389.9 2.0 convert_reduce_fusion.2
  391.9 0.9 fusion.47
  (82 shorter events, 2.8 us)
Async XLA Ops:
  7.2 4.1 %copy-start.17 = (bf16[256,128]{1,0:T(8,128)(2,1)S(1)}, bf16[256,128]{1,0:T(8,128)(2,1)}, u32[]{:S(2)}) copy-start(bf16[256,128]{1,0:T(8,128)(2,1)} %param.14) | copy-start | bytes 196612
  7.2 4.2 %copy-start.16 = (bf16[3,128,256]{2,1,0:T(8,128)(2,1)S(1)}, bf16[3,128,256]{2,1,0:T(8,128)(2,1)}, u32[]{:S(2)}) copy-start(bf16[3,128,256]{2,1,0:T(8,128)(2,1)} %param.13) | copy-start | bytes 589828
  7.2 115.2 %all-gather.3.cloned.1.call-start = ((), (), s32[]{:S(2)}) async-start(), calls=%async_computation.7 | async-start | bytes 4718592 | tf_op jit(solution)/shard_map/all_gather | solution.py:131
  7.9 286.0 %all-gather.5.cloned.1.call-start = ((), (), s32[]{:S(2)}) async-start(), calls=%async_computation.8 | async-start | bytes 13369344 | tf_op jit(solution)/shard_map/all_gather | solution.py:128
  14.6 7.5 %copy-start.19 = (s32[1024]{0:T(1024)S(1)}, s32[1024]{0:T(1024)}, u32[]{:S(2)}) copy-start(s32[1024]{0:T(1024)} %param.12) | copy-start | bytes 12292
  14.6 7.5 %copy-start.18 = (s32[1024]{0:T(1024)S(1)}, s32[1024]{0:T(1024)}, u32[]{:S(2)}) copy-start(s32[1024]{0:T(1024)} %param.11) | copy-start | bytes 12292
  14.6 60.7 %all-to-all-start = ((bf16[16,4,128,256]{2,3,1,0:T(8,128)(2,1)}), bf16[16,4,128,256]{2,3,1,0:T(8,128)(2,1)}, u32[]{:S(2)}, u32[]{:S(2)}) async-start(bf16[16,4,128,256]{2,3,1,0:T(8,128)(2,1)} %broadcast_in_dim.43), calls=%async_computation | async-start | bytes 8388608 | tf_op jit(solution)/shard_map/all_to_all | solution.py:125
  122.4 3.4 copy-start.1
  132.7 1.6 copy-start.8
  134.4 3.7 copy-start.3
  144.8 1.7 copy-start.5
  144.8 3.0 copy-start
  155.4 33.1 %all-to-all-start.1 = ((bf16[16,5,2,16,256]{4,3,2,1,0:T(8,128)(2,1)}), bf16[16,5,2,16,256]{4,3,2,1,0:T(8,128)(2,1)S(1)}, u32[]{:S(2)}, u32[]{:S(2)}) async-start(bf16[16,5,2,16,256]{4,3,2,1,0:T(8,128)(2,1)} %fusion.31), calls=%async_computation.1 | async-start | bytes 2621440 | tf_op jit(solution)/shard_map/all_to_all | solution.py:85
  168.1 2.8 copy-start.6
  170.0 0.8 copy-start.12
  170.0 1.0 copy-start.13
  170.0 1.5 copy-start.14
  171.5 1.3 copy-start.11
  171.5 1.3 slice-start
  172.8 4.1 %copy-start.7 = (bf16[1024,2,128]{2,0,1:T(8,128)(2,1)S(1)}, bf16[1024,2,128]{2,0,1:T(8,128)(2,1)}, u32[]{:S(2)}) copy-start(bf16[1024,2,128]{2,0,1:T(8,128)(2,1)} %copy-done.5) | copy-start | bytes 1572868
  176.9 5.5 %copy-start.4 = (bf16[1,1024,256]{1,2,0:T(8,128)(2,1)S(1)}, bf16[1,1024,256]{1,2,0:T(8,128)(2,1)}, u32[]{:S(2)}) copy-start(bf16[1,1024,256]{1,2,0:T(8,128)(2,1)} %copy-done.3) | copy-start | bytes 1572868
  182.4 2.8 copy-start.15
  191.6 62.2 %copy-start.2 = (bf16[64,2,16,256]{3,2,1,0:T(8,128)(2,1)}, bf16[64,2,16,256]{3,2,1,0:T(8,128)(2,1)S(1)}, u32[]{:S(2)}) copy-start(bf16[64,2,16,256]{3,2,1,0:T(8,128)(2,1)S(1)} %scatter_fusion) | copy-start | bytes 3145732
  253.9 1.0 copy-start.9
  290.0 32.2 %all-to-all-start.5 = ((bf16[8,64,2048]{2,1,0:T(8,128)(2,1)}), bf16[8,64,2048]{2,1,0:T(8,128)(2,1)S(1)}, u32[]{:S(2)}, u32[]{:S(2)}) async-start(bf16[8,64,2048]{2,1,0:T(8,128)(2,1)} %broadcast_in_dim.56), calls=%async_computation.5 | async-start | bytes 4194304 | tf_op jit(solution)/shard_map/all_to_all | solution.py:107
  322.2 1.3 copy-start.10
  323.5 32.2 %all-to-all-start.4 = ((bf16[8,64,2048]{2,1,0:T(8,128)(2,1)}), bf16[8,64,2048]{2,1,0:T(8,128)(2,1)S(1)}, u32[]{:S(2)}, u32[]{:S(2)}) async-start(bf16[8,64,2048]{2,1,0:T(8,128)(2,1)} %bitcast.113), calls=%async_computation.4 | async-start | bytes 4194304 | tf_op jit(solution)/shard_map/all_to_all | solution.py:113
  355.7 34.3 %all-to-all-start.6 = ((bf16[8,64,2048]{2,1,0:T(8,128)(2,1)}), bf16[8,64,2048]{2,1,0:T(8,128)(2,1)}, u32[]{:S(2)}, u32[]{:S(2)}) async-start(bf16[8,64,2048]{2,1,0:T(8,128)(2,1)} %bitcast.115), calls=%async_computation.6 | async-start | bytes 4194304 | tf_op jit(solution)/shard_map/all_to_all | solution.py:113
Sparse Core Ops, SparseCore 0:
  10.3 112.0 all-gather.2
  124.0 135.1 all-gather.4

commit v13 on v10

--- a/solution.py
+++ b/solution.py
@@ -120,22 +120,25 @@
     tok_group = segment.shape[0]
     share_rows = stream.shape[0]
     local_cols = w_qkv.shape[2]
-    attn_w = lax.all_gather(
-        jnp.concatenate([w_qkv, jnp.transpose(w_out)[None]], axis=0), "dp", axis=1, tiled=True
-    )
+    qkv_w = lax.all_gather(w_qkv, "dp", axis=1, tiled=True)
+    out_local = jnp.transpose(w_out)
+    owners = lax.axis_size("dp")
+    out_w = lax.all_to_all(
+        jnp.broadcast_to(out_local[None], (owners,) + out_local.shape), "dp", 0, 0, tiled=True
+    ).reshape(owners * out_local.shape[0], out_local.shape[1])
     mlp_w = lax.all_gather(
         jnp.concatenate([w_gate_up, jnp.transpose(w_down)[None]], axis=0), "dp", axis=1, tiled=True
     )
     full_stream = gather_rows(stream, "tensor")
     normed = layer_norm(full_stream).astype(jnp.bfloat16)
     local_heads = local_cols // HD
-    projected = jnp.einsum("td,cdf->ctf", normed, attn_w[:3], preferred_element_type=jnp.float32)
+    projected = jnp.einsum("td,cdf->ctf", normed, qkv_w, preferred_element_type=jnp.float32)
     query = rotate(projected[0].reshape(tok_group, local_heads, HD), position).astype(jnp.bfloat16)
     keys = rotate(projected[1].reshape(tok_group, local_heads, HD), position).astype(jnp.bfloat16)
     values = projected[2].reshape(tok_group, local_heads, HD).astype(jnp.bfloat16)
     kv_cache = write_cache(keys, values, page_table)
     context = attend(query, keys, values, segment)
-    attn_part = jnp.einsum("tr,dr->td", context, attn_w[3], preferred_element_type=jnp.float32)
+    attn_part = jnp.einsum("tr,dr->td", context, out_w, preferred_element_type=jnp.float32)
     attn_part, kv_cache = lax.optimization_barrier((attn_part.astype(jnp.bfloat16), kv_cache))
     attn_mine = sum_rows(attn_part, "tensor")
     mid = (stream.astype(jnp.float32) + attn_mine).astype(jnp.bfloat16)

time: 369 us -> 385 us (1.043)
  starting transfers between devices: 26.6 us -> 35.8 us
  local copies, waits for them, and re-layouts: 28.4 us -> 33.3 us
    all_to_all x1, waiting for transfers between devices: 1.1 us -> 13.9 us  [write_cache(): lax.all_to_all(outgoing, 'dp', split_axis=0, concat_axis=0, tiled=True)]
    all_to_all x0 -> x1, starting transfers between devices: none -> 8.77 us  [body(): lax.all_to_all(jnp.broadcast_to(out_local[None], (owners,) + out_local.sh...]
    all_gather x1, waiting for transfers between devices: 8.61 us -> 0.01 us  [body(): qkv_w = lax.all_gather(w_qkv, 'dp', axis=1, tiled=True)]
    unnamed x56 -> x44, local copies, waits for them, and re-layouts: 12.7 us -> 15.3 us
  transfers between devices with their start and end apart: 7 -> 8, of which waited for: 6 -> 5; matrix products, arithmetic and copies ran while one was open for 27% -> 28% of each run, Pallas kernels for 0% -> 0%
where the time goes in v13:
time: 385 us; the launch traced here: 383 us
  waiting for transfers between devices  122 us (32%)
  blocking collectives  95.8 us (25%)
  matrix products  49.5 us (13%)
  starting transfers between devices  35.8 us (9%)
  local copies, waits for them, and re-layouts  33.3 us (9%)
  other arithmetic  31.8 us (8%)
  between operations  14.5 us (4%)
    all_to_all x2, waiting for transfers between devices, gather_rows(): gathered = lax.all_to_all(copies, axis_name, 0, 0, tiled=True)  65.6 us
    all_to_all x1, blocking collectives, sum_rows(): lax.all_to_all(terms.reshape(count, terms.shape[0] // count, terms.shape[...  64.3 us
    all_to_all x2, waiting for transfers between devices, sum_rows(): lax.all_to_all(terms.reshape(count, terms.shape[0] // count, terms.shape[...  42.9 us
    all_to_all x1, blocking collectives, gather_rows(): gathered = lax.all_to_all(copies, axis_name, 0, 0, tiled=True)  31.4 us
    dot_general x2, matrix products, body(): jnp.einsum('td,cdf->ctf', rows, mlp_w[:2], preferred_element_type=jnp.flo...  15.3 us
    unnamed x44, local copies, waits for them, and re-layouts  15.3 us
    all_to_all x1, waiting for transfers between devices, write_cache(): lax.all_to_all(outgoing, 'dp', split_axis=0, concat_axis=0, tiled=True)  13.9 us
    dot_general x2, matrix products, body(): jnp.einsum('tf,df->td', hidden, mlp_w[2], preferred_element_type=jnp.floa...  12.3 us
  transfers between devices with their start and end apart: 8, of which 5 were waited for; matrix products, arithmetic and copies ran while one was open for 28% of the time, Pallas kernels for 0%

profile of v13, /device:TPU:1, one launch (start us, length us, event | category | flops | bytes accessed | tf_op | source)
XLA Modules:
  0.0 383.2 jit_solution(17731292822121835563)
XLA Ops:
  7.2 1.8 copy.91
  9.1 1.3 copy.107
  10.4 2.0 pad_maximum_fusion
  12.4 2.5 broadcast_in_dim.42
  14.9 8.3 %all-to-all-start = ((bf16[8,128,2048]{2,1,0:T(8,128)(2,1)}), bf16[8,128,2048]{2,1,0:T(8,128)(2,1)}, u32[]{:S(2)}, u32[]{:S(2)}) async-start(bf16[8,128,2048]{2,1,0:T(8,128)(2,1)} %broadcast_in_dim.42), calls=%async_computation | async-start | bytes 8388608 | tf_op jit(solution)/shard_map/all_to_all | solution.py:107
  23.4 1.0 compare_and_fusion
  24.4 1.4 fusion.24
  25.8 1.9 multiply_cosine_fusion
  27.7 50.8 %all-to-all-done = bf16[8,128,2048]{2,1,0:T(8,128)(2,1)} async-done(((bf16[8,128,2048]{2,1,0:T(8,128)(2,1)}), bf16[8,128,2048]{2,1,0:T(8,128)(2,1)}, u32[]{:S(2)}, u32[]{:S(2)}) %all-to-all-start) | async-done | bytes 4194336 | tf_op jit(solution)/shard_map/all_to_all | solution.py:107
  78.5 1.1 broadcast_in_dim.47
  79.6 8.8 %all-to-all-start.1 = ((bf16[16,128,256]{2,1,0:T(8,128)(2,1)}), bf16[16,128,256]{2,1,0:T(8,128)(2,1)S(1)}, u32[]{:S(2)}, u32[]{:S(2)}) async-start(bf16[16,128,256]{2,1,0:T(8,128)(2,1)} %broadcast_in_dim.47), calls=%async_computation.1 | async-start | bytes 2097152 | tf_op jit(solution)/shard_map/all_to_all | solution.py:126
  88.4 2.8 convert_reduce_fusion.1
  91.2 3.4 multiply_reduce_fusion
  94.6 4.1 %fusion.3 = bf16[1024,2048]{1,0:T(8,128)(2,1)} fusion(bf16[8,128,2048]{2,1,0:T(8,128)(2,1)} %all-to-all-done, f32[1024]{0:T(1024)S(1)} %rsqrt_bitcast_fusion, f32[1024]{0:T(1024)S(1)} %get-tuple-element.46), kind=kLoop, calls=%fused_computation.7 | loop fusion | flops 8388608 | bytes 8396800 | tf_op jit(solution)/shard_map/convert_element_type | solution.py:133
  98.8 6.2 %fusion.27 = f32[3,1024,256]{1,2,0:T(8,128)S(1)} fusion(bf16[3,2048,256]{1,2,0:T(8,128)(2,1)} %all-gather.3.cloned.1.call-done, bf16[1024,2048]{1,0:T(8,128)(2,1)} %fusion.3), kind=kOutput, calls=%fused_computation.44 | convolution fusion | flops 3221225472 | bytes 10485760 | tf_op jit(solution)/shard_map/td,cdf->ctf/dot_general | solution.py:135
  105.0 0.9 slice.213
  105.8 1.1 fusion.83
  106.9 1.1 fusion.84
  108.0 1.4 copy.111
  109.4 2.4 copy.112
  111.8 1.5 multiply_subtract_fusion
  113.6 0.8 copy-done.4
  114.4 0.5 copy.98
  115.0 1.2 convert_element_type.130
  116.1 1.0 copy.99
  117.2 1.3 maximum_bitcast_fusion
  118.5 2.0 sort.17
  120.6 0.8 gather_fusion.1
  121.4 2.3 fusion.85
  123.7 2.4 copy.109
  126.2 2.4 copy.110
  128.5 2.8 subtract_convert_fusion
  131.5 0.6 gather_fusion
  132.2 1.2 fusion.30
  133.7 0.4 copy-done.11
  134.0 0.5 fusion.58
  134.6 1.1 fusion.90
  135.9 4.0 %fusion.40 = bf16[512,2,128]{0,2,1:T(8,128)(2,1)} fusion(bf16[512,2,128]{0,2,1:T(8,128)(2,1)S(1)} %bitcast.103, f32[512,2]{0,1:T(2,128)S(1)} %bitcast.115, f32[2,512,512]{1,2,0:T(8,128)} %copy-done.9, pred[512,512]{0,1:T(8,128)(4,1)S(1)} %copy-done.12), kind=kOutput, calls=%fused_computation.55 | convolution fusion | flops 137627136 | bytes 2887680 | tf_op jit(solution)/shard_map/hqk,khd->qhd/dot_general | solution.py:55
  139.9 5.7 %all-to-all-start.2 = ((bf16[16,5,2,16,256]{4,3,2,1,0:T(8,128)(2,1)}), bf16[16,5,2,16,256]{4,3,2,1,0:T(8,128)(2,1)S(1)}, u32[]{:S(2)}, u32[]{:S(2)}) async-start(bf16[16,5,2,16,256]{4,3,2,1,0:T(8,128)(2,1)} %fusion.30), calls=%async_computation.2 | async-start | bytes 2621440 | tf_op jit(solution)/shard_map/all_to_all | solution.py:85
  145.6 5.5 %fusion.89 = (f32[2,512]{1,0:T(2,128)S(1)}, bf16[2,512,1024]{2,1,0:T(8,128)(2,1)}) fusion(pred[512,1024]{1,0:T(8,128)(4,1)} %fusion.24, bf16[1024,2,128]{2,0,1:T(8,128)(2,1)S(1)} %copy-done.5, bf16[1024,2,64]{2,0,1:T(8,128)(2,1)} %get-tuple-element.31, bf16[1024,2,64]{2,0,1:T(8,128)(2,1)} %get-tuple-element.30), kind=kOutput, calls=%fused_computation.128 | convolution fusion | flops 545260544 | bytes 3674112 | tf_op jit(solution)/shard_map/sub | solution.py:53
  151.1 2.5 fusion.41
  153.7 3.3 convolution_convert_fusion
  157.0 13.9 %all-to-all-done.2 = bf16[16,5,2,16,256]{4,3,2,1,0:T(8,128)(2,1)S(1)} async-done(((bf16[16,5,2,16,256]{4,3,2,1,0:T(8,128)(2,1)}), bf16[16,5,2,16,256]{4,3,2,1,0:T(8,128)(2,1)S(1)}, u32[]{:S(2)}, u32[]{:S(2)}) %all-to-all-start.2) | async-done | bytes 1310752 | tf_op jit(solution)/shard_map/all_to_all | solution.py:85
  171.5 2.5 scatter_fusion
  174.0 64.3 %all_to_all.40 = bf16[8,128,2048]{2,1,0:T(8,128)(2,1)S(1)} all-to-all(bf16[8,128,2048]{2,1,0:T(8,128)(2,1)} %bitcast.95), channel_id=1, replica_groups=mesh['dp'=16,'tensor'=8] {'tensor'}, dimensions={0} | all-to-all | bytes 8388608 | tf_op jit(solution)/shard_map/all_to_all | solution.py:113
  238.4 0.7 convert_reduce_fusion
  239.1 0.3 copy-done.7
  239.9 0.3 fusion.45
  240.5 31.4 %all_to_all.41 = bf16[8,64,2048]{2,1,0:T(8,128)(2,1)} all-to-all(bf16[8,64,2048]{2,1,0:T(8,128)(2,1)S(1)} %broadcast_in_dim.55), channel_id=1, replica_groups=mesh['dp'=16,'tensor'=8] {'tensor'}, dimensions={0} | all-to-all | bytes 4194304 | tf_op jit(solution)/shard_map/all_to_all | solution.py:107
  272.0 1.6 broadcast_in_dim.56
  273.5 3.6 all-to-all-start.6
  277.2 7.6 %convolution_bitcast_fusion.1 = f32[2,512,1024]{1,2,0:T(8,128)S(1)} fusion(bf16[3,2048,1024]{1,2,0:T(8,128)(2,1)} %all-gather.5.cloned.1.call-done, bf16[512,2048,1]{1,0,2:T(8,128)(2,1)} %bitcast.106), kind=kOutput, calls=%fused_computation.28 | convolution fusion | flops 4294967296 | bytes 18874368 | tf_op jit(solution)/shard_map/td,cdf->ctf/dot_general | solution.py:151
  284.8 6.1 %fusion.12 = bf16[512,2048]{1,0:T(8,128)(2,1)} fusion(bf16[3,2048,1024]{1,2,0:T(8,128)(2,1)} %all-gather.5.cloned.1.call-done, f32[2,512,1024]{1,2,0:T(8,128)S(1)} %convolution_bitcast_fusion.1), kind=kOutput, calls=%fused_computation.23 | convolution fusion | flops 2151677952 | bytes 10485760 | tf_op jit(solution)/shard_map/tf,df->td/dot_general | solution.py:153
  291.0 14.7 %all-to-all-done.6 = bf16[8,64,2048]{2,1,0:T(8,128)(2,1)S(1)} async-done(((bf16[8,64,2048]{2,1,0:T(8,128)(2,1)}), bf16[8,64,2048]{2,1,0:T(8,128)(2,1)S(1)}, u32[]{:S(2)}, u32[]{:S(2)}) %all-to-all-start.6) | async-done | bytes 2097184 | tf_op jit(solution)/shard_map/all_to_all | solution.py:107
  305.7 1.3 copy-done.8
  307.0 3.9 %all-to-all-start.5 = ((bf16[8,64,2048]{2,1,0:T(8,128)(2,1)}), bf16[8,64,2048]{2,1,0:T(8,128)(2,1)S(1)}, u32[]{:S(2)}, u32[]{:S(2)}) async-start(bf16[8,64,2048]{2,1,0:T(8,128)(2,1)} %bitcast.105), calls=%async_computation.5 | async-start | bytes 4194304 | tf_op jit(solution)/shard_map/all_to_all | solution.py:113
  310.9 7.6 %convolution_bitcast_fusion = f32[2,512,1024]{1,2,0:T(8,128)S(1)} fusion(bf16[3,2048,1024]{1,2,0:T(8,128)(2,1)} %all-gather.5.cloned.1.call-done, bf16[512,2048,1]{1,0,2:T(8,128)(2,1)} %bitcast.104), kind=kOutput, calls=%fused_computation.27 | convolution fusion | flops 4294967296 | bytes 18874368 | tf_op jit(solution)/shard_map/td,cdf->ctf/dot_general | solution.py:151
  318.5 6.1 %fusion.13 = bf16[512,2048]{1,0:T(8,128)(2,1)} fusion(bf16[3,2048,1024]{1,2,0:T(8,128)(2,1)} %all-gather.5.cloned.1.call-done, f32[2,512,1024]{1,2,0:T(8,128)S(1)} %convolution_bitcast_fusion), kind=kOutput, calls=%fused_computation.24 | convolution fusion | flops 2151677952 | bytes 10485760 | tf_op jit(solution)/shard_map/tf,df->td/dot_general | solution.py:153
  324.6 14.5 %all-to-all-done.5 = bf16[8,64,2048]{2,1,0:T(8,128)(2,1)S(1)} async-done(((bf16[8,64,2048]{2,1,0:T(8,128)(2,1)}), bf16[8,64,2048]{2,1,0:T(8,128)(2,1)S(1)}, u32[]{:S(2)}, u32[]{:S(2)}) %all-to-all-start.5) | async-done | bytes 2097184 | tf_op jit(solution)/shard_map/all_to_all | solution.py:113
  339.2 5.6 %all-to-all-start.7 = ((bf16[8,64,2048]{2,1,0:T(8,128)(2,1)}), bf16[8,64,2048]{2,1,0:T(8,128)(2,1)}, u32[]{:S(2)}, u32[]{:S(2)}) async-start(bf16[8,64,2048]{2,1,0:T(8,128)(2,1)} %bitcast.107), calls=%async_computation.7 | async-start | bytes 4194304 | tf_op jit(solution)/shard_map/all_to_all | solution.py:113
  344.7 0.3 convert_reduce_fusion.3
  345.1 28.4 %all-to-all-done.7 = bf16[8,64,2048]{2,1,0:T(8,128)(2,1)} async-done(((bf16[8,64,2048]{2,1,0:T(8,128)(2,1)}), bf16[8,64,2048]{2,1,0:T(8,128)(2,1)}, u32[]{:S(2)}, u32[]{:S(2)}) %all-to-all-start.7) | async-done | bytes 2097184 | tf_op jit(solution)/shard_map/all_to_all | solution.py:113
  373.4 2.0 convert_reduce_fusion.2
  375.4 0.9 fusion.46
  (77 shorter events, 2.9 us)
Async XLA Ops:
  7.2 5.2 %copy-start.6 = (bf16[128,2048]{1,0:T(8,128)(2,1)S(1)}, bf16[128,2048]{1,0:T(8,128)(2,1)}, u32[]{:S(2)}) copy-start(bf16[128,2048]{1,0:T(8,128)(2,1)} %param.10) | copy-start | bytes 1572868
  7.2 91.6 %all-gather.3.cloned.1.call-start = ((), (), s32[]{:S(2)}) async-start(), calls=%async_computation.8 | async-start | bytes 3342336 | tf_op jit(solution)/shard_map/all_gather | solution.py:123
  9.0 268.1 %all-gather.5.cloned.1.call-start = ((), (), s32[]{:S(2)}) async-start(), calls=%async_computation.9 | async-start | bytes 13369344 | tf_op jit(solution)/shard_map/all_gather | solution.py:129
  14.9 8.3 %copy-start.16 = (s32[1024]{0:T(1024)S(1)}, s32[1024]{0:T(1024)}, u32[]{:S(2)}) copy-start(s32[1024]{0:T(1024)} %param.12) | copy-start | bytes 12292
  14.9 8.4 %copy-start.14 = (bf16[256,128]{1,0:T(8,128)(2,1)S(1)}, bf16[256,128]{1,0:T(8,128)(2,1)}, u32[]{:S(2)}) copy-start(bf16[256,128]{1,0:T(8,128)(2,1)} %param.14) | copy-start | bytes 196612
  14.9 8.5 %copy-start.15 = (s32[1024]{0:T(1024)S(1)}, s32[1024]{0:T(1024)}, u32[]{:S(2)}) copy-start(s32[1024]{0:T(1024)} %param.11) | copy-start | bytes 12292
  14.9 63.6 %all-to-all-start = ((bf16[8,128,2048]{2,1,0:T(8,128)(2,1)}), bf16[8,128,2048]{2,1,0:T(8,128)(2,1)}, u32[]{:S(2)}, u32[]{:S(2)}) async-start(bf16[8,128,2048]{2,1,0:T(8,128)(2,1)} %broadcast_in_dim.42), calls=%async_computation | async-start | bytes 8388608 | tf_op jit(solution)/shard_map/all_to_all | solution.py:107
  79.6 60.4 %all-to-all-start.1 = ((bf16[16,128,256]{2,1,0:T(8,128)(2,1)}), bf16[16,128,256]{2,1,0:T(8,128)(2,1)S(1)}, u32[]{:S(2)}, u32[]{:S(2)}) async-start(bf16[16,128,256]{2,1,0:T(8,128)(2,1)} %broadcast_in_dim.47), calls=%async_computation.1 | async-start | bytes 2097152 | tf_op jit(solution)/shard_map/all_to_all | solution.py:126
  113.3 2.8 copy-start.2
  113.6 0.8 copy-start.4
  115.0 3.5 copy-start
  132.2 1.3 copy-start.5
  132.2 1.5 copy-start.10
  132.2 1.8 copy-start.11
  133.4 1.1 copy-start.12
  134.6 1.3 copy-start.9
  134.6 1.3 slice-start
  139.9 30.9 %all-to-all-start.2 = ((bf16[16,5,2,16,256]{4,3,2,1,0:T(8,128)(2,1)}), bf16[16,5,2,16,256]{4,3,2,1,0:T(8,128)(2,1)S(1)}, u32[]{:S(2)}, u32[]{:S(2)}) async-start(bf16[16,5,2,16,256]{4,3,2,1,0:T(8,128)(2,1)} %fusion.30), calls=%async_computation.2 | async-start | bytes 2621440 | tf_op jit(solution)/shard_map/all_to_all | solution.py:85
  145.6 5.5 %copy-start.3 = (bf16[1,1024,256]{1,2,0:T(8,128)(2,1)S(1)}, bf16[1,1024,256]{1,2,0:T(8,128)(2,1)}, u32[]{:S(2)}) copy-start(bf16[1,1024,256]{1,2,0:T(8,128)(2,1)} %slice.213) | copy-start | bytes 1572868
  151.1 2.5 copy-start.13
  174.0 64.3 %copy-start.1 = (bf16[64,2,16,256]{3,2,1,0:T(8,128)(2,1)}, bf16[64,2,16,256]{3,2,1,0:T(8,128)(2,1)S(1)}, u32[]{:S(2)}) copy-start(bf16[64,2,16,256]{3,2,1,0:T(8,128)(2,1)S(1)} %scatter_fusion) | copy-start | bytes 3145732
  238.4 1.0 copy-start.7
  273.5 32.2 %all-to-all-start.6 = ((bf16[8,64,2048]{2,1,0:T(8,128)(2,1)}), bf16[8,64,2048]{2,1,0:T(8,128)(2,1)S(1)}, u32[]{:S(2)}, u32[]{:S(2)}) async-start(bf16[8,64,2048]{2,1,0:T(8,128)(2,1)} %broadcast_in_dim.56), calls=%async_computation.6 | async-start | bytes 4194304 | tf_op jit(solution)/shard_map/all_to_all | solution.py:107
  305.7 1.3 copy-start.8
  307.0 32.2 %all-to-all-start.5 = ((bf16[8,64,2048]{2,1,0:T(8,128)(2,1)}), bf16[8,64,2048]{2,1,0:T(8,128)(2,1)S(1)}, u32[]{:S(2)}, u32[]{:S(2)}) async-start(bf16[8,64,2048]{2,1,0:T(8,128)(2,1)} %bitcast.105), calls=%async_computation.5 | async-start | bytes 4194304 | tf_op jit(solution)/shard_map/all_to_all | solution.py:113
  339.2 34.3 %all-to-all-start.7 = ((bf16[8,64,2048]{2,1,0:T(8,128)(2,1)}), bf16[8,64,2048]{2,1,0:T(8,128)(2,1)}, u32[]{:S(2)}, u32[]{:S(2)}) async-start(bf16[8,64,2048]{2,1,0:T(8,128)(2,1)} %bitcast.107), calls=%async_computation.7 | async-start | bytes 4194304 | tf_op jit(solution)/shard_map/all_to_all | solution.py:113
Sparse Core Ops, SparseCore 0:
  10.2 82.7 all-gather.2
  94.6 104.2 all-gather.4

commit v14 on v10

--- a/solution.py
+++ b/solution.py
@@ -73,7 +73,6 @@
     base = 128
     stacked = jnp.stack([keys.reshape(tokens, width), values.reshape(tokens, width)], axis=0)
     stacked = stacked.reshape(2, pages, page_size, width).transpose(1, 0, 2, 3)
-    page_table, stacked = lax.optimization_barrier((page_table, stacked))
     order = jnp.argsort(page_table // pages, stable=True)
     sorted_ids = page_table[order].reshape(owners, per_owner)
     code = jnp.stack([sorted_ids // base, sorted_ids % base], axis=-1).astype(jnp.bfloat16)

time: 369 us -> 369 us (level)
  no operation moved by 1% of the time
where the time goes in v14:
time: 369 us; the launch traced here: 368 us
  waiting for transfers between devices  117 us (32%)
  blocking collectives  98.7 us (27%)
  matrix products  50.9 us (14%)
  local copies, waits for them, and re-layouts  30 us (8%)
  other arithmetic  30 us (8%)
  starting transfers between devices  27 us (7%)
  between operations  14.5 us (4%)
    all_to_all x1, blocking collectives, sum_rows(): lax.all_to_all(terms.reshape(count, terms.shape[0] // count, terms.shape[...  64.9 us
    all_to_all x2, waiting for transfers between devices, gather_rows(): gathered = lax.all_to_all(copies, axis_name, 0, 0, tiled=True)  63.6 us
    all_to_all x2, waiting for transfers between devices, sum_rows(): lax.all_to_all(terms.reshape(count, terms.shape[0] // count, terms.shape[...  43.1 us
    all_to_all x1, blocking collectives, gather_rows(): gathered = lax.all_to_all(copies, axis_name, 0, 0, tiled=True)  33.8 us
    dot_general x2, matrix products, body(): jnp.einsum('td,cdf->ctf', rows, mlp_w[:2], preferred_element_type=jnp.flo...  15.3 us
    all_to_all x2, starting transfers between devices, gather_rows(): gathered = lax.all_to_all(copies, axis_name, 0, 0, tiled=True)  13.9 us
    unnamed x56, local copies, waits for them, and re-layouts  13.5 us
    dot_general x2, matrix products, body(): jnp.einsum('tf,df->td', hidden, mlp_w[2], preferred_element_type=jnp.floa...  12.3 us
  transfers between devices with their start and end apart: 7, of which 6 were waited for; matrix products, arithmetic and copies ran while one was open for 27% of the time, Pallas kernels for 0%

profile of v14, /device:TPU:1, one launch (start us, length us, event | category | flops | bytes accessed | tf_op | source)
XLA Modules:
  0.0 367.9 jit_solution(16780017175871464369)
XLA Ops:
  7.2 1.1 copy.86
  8.4 1.6 pad_maximum_fusion.3
  10.1 1.3 copy.101
  11.4 1.0 pad_maximum_fusion
  12.4 2.5 broadcast_in_dim.43
  15.0 8.3 %all-to-all-start = ((bf16[8,128,2048]{2,1,0:T(8,128)(2,1)}), bf16[8,128,2048]{2,1,0:T(8,128)(2,1)}, u32[]{:S(2)}, u32[]{:S(2)}) async-start(bf16[8,128,2048]{2,1,0:T(8,128)(2,1)} %broadcast_in_dim.43), calls=%async_computation | async-start | bytes 8388608 | tf_op jit(solution)/shard_map/all_to_all | solution.py:106
  23.3 2.0 sort.17
  25.4 0.8 gather_fusion.1
  26.5 1.0 compare_and_fusion
  27.5 1.4 fusion.24
  28.9 1.9 multiply_cosine_fusion
  30.8 48.8 %all-to-all-done = bf16[8,128,2048]{2,1,0:T(8,128)(2,1)} async-done(((bf16[8,128,2048]{2,1,0:T(8,128)(2,1)}), bf16[8,128,2048]{2,1,0:T(8,128)(2,1)}, u32[]{:S(2)}, u32[]{:S(2)}) %all-to-all-start) | async-done | bytes 4194336 | tf_op jit(solution)/shard_map/all_to_all | solution.py:106
  79.6 2.9 convert_reduce_fusion.1
  82.5 3.4 multiply_reduce_fusion
  86.0 4.2 %fusion.3 = bf16[1024,2048]{1,0:T(8,128)(2,1)} fusion(bf16[8,128,2048]{2,1,0:T(8,128)(2,1)} %all-to-all-done, f32[1024]{0:T(1024)S(1)} %rsqrt_bitcast_fusion, f32[1024]{0:T(1024)S(1)} %get-tuple-element.42), kind=kLoop, calls=%fused_computation.7 | loop fusion | flops 8388608 | bytes 8396800 | tf_op jit(solution)/shard_map/convert_element_type | solution.py:129
  90.2 8.6 %all-gather.3.cloned.1.call-done = bf16[4,2048,256]{1,2,0:T(8,128)(2,1)} async-done(((bf16[4,128,256]{1,2,0:T(8,128)(2,1)}), bf16[4,2048,256]{1,2,0:T(8,128)(2,1)}) %all-gather.3.cloned.1.call-update) | async-done | bytes 4194320 | tf_op jit(solution)/shard_map/all_gather | solution.py:122
  98.8 6.2 %fusion.27 = f32[3,1024,256]{1,2,0:T(8,128)S(1)} fusion(bf16[4,2048,256]{1,2,0:T(8,128)(2,1)} %all-gather.3.cloned.1.call-done, bf16[1024,2048]{1,0:T(8,128)(2,1)} %fusion.3), kind=kOutput, calls=%fused_computation.44 | convolution fusion | flops 3221225472 | bytes 11534336 | tf_op jit(solution)/shard_map/td,cdf->ctf/dot_general | solution.py:131
  105.0 1.6 copy-done.8
  106.8 1.0 copy.93
  107.8 3.0 fusion.83
  110.7 0.9 fusion.84
  111.6 0.3 copy.105
  112.0 1.4 copy.106
  113.6 0.3 maximum_convert_fusion
  114.0 0.8 copy-done.5
  114.8 0.5 copy.92
  115.3 1.1 convert_element_type.130
  116.4 1.1 maximum_bitcast_fusion
  117.6 0.6 gather_fusion
  118.2 1.3 fusion.30
  119.5 3.9 %all-to-all-start.1 = ((bf16[16,5,2,16,256]{4,3,2,1,0:T(8,128)(2,1)}), bf16[16,5,2,16,256]{4,3,2,1,0:T(8,128)(2,1)S(1)}, u32[]{:S(2)}, u32[]{:S(2)}) async-start(bf16[16,5,2,16,256]{4,3,2,1,0:T(8,128)(2,1)} %fusion.30), calls=%async_computation.1 | async-start | bytes 2621440 | tf_op jit(solution)/shard_map/all_to_all | solution.py:84
  123.4 1.0 fusion.85
  124.5 1.4 copy.103
  125.8 2.4 copy.104
  128.2 1.6 subtract_convert_fusion
  129.8 0.8 copy-done.14
  130.7 0.5 fusion.58
  131.3 1.1 fusion.90
  132.6 4.5 %fusion.40 = bf16[512,2,128]{0,2,1:T(8,128)(2,1)} fusion(bf16[512,2,128]{0,2,1:T(8,128)(2,1)S(1)} %bitcast.104, f32[512,2]{0,1:T(2,128)S(1)} %bitcast.117, f32[2,512,512]{1,2,0:T(8,128)} %copy-done.12, pred[512,512]{0,1:T(8,128)(4,1)S(1)} %copy-done.18), kind=kOutput, calls=%fused_computation.55 | convolution fusion | flops 137627136 | bytes 2887680 | tf_op jit(solution)/shard_map/hqk,khd->qhd/dot_general | solution.py:55
  137.1 5.2 %fusion.89 = (f32[2,512]{1,0:T(2,128)S(1)}, bf16[2,512,1024]{2,1,0:T(8,128)(2,1)}) fusion(pred[512,1024]{1,0:T(8,128)(4,1)} %fusion.24, bf16[1024,2,128]{2,0,1:T(8,128)(2,1)S(1)} %copy-done.7, bf16[1024,2,64]{2,0,1:T(8,128)(2,1)S(1)} %copy-done.17, bf16[1024,2,64]{2,0,1:T(8,128)(2,1)S(1)} %copy-done.15), kind=kOutput, calls=%fused_computation.130 | convolution fusion | flops 545260544 | bytes 3674112 | tf_op jit(solution)/shard_map/sub | solution.py:53
  142.3 2.5 fusion.41
  144.8 4.5 %convolution_convert_fusion = bf16[1024,2048]{1,0:T(8,128)(2,1)} fusion(bf16[1024,256]{0,1:T(8,128)(2,1)S(1)} %bitcast.105, bf16[4,2048,256]{1,2,0:T(8,128)(2,1)} %all-gather.3.cloned.1.call-done), kind=kOutput, calls=%fused_computation.19 | convolution fusion | flops 1075838976 | bytes 5767168 | tf_op jit(solution)/shard_map/tr,dr->td/dot_general | solution.py:137
  149.3 1.4 all-to-all-done.1
  151.3 2.5 scatter_fusion
  153.8 64.9 %all_to_all.35 = bf16[8,128,2048]{2,1,0:T(8,128)(2,1)S(1)} all-to-all(bf16[8,128,2048]{2,1,0:T(8,128)(2,1)} %bitcast.98), channel_id=1, replica_groups=mesh['dp'=16,'tensor'=8] {'tensor'}, dimensions={0} | all-to-all | bytes 8388608 | tf_op jit(solution)/shard_map/all_to_all | solution.py:112
  218.7 0.7 convert_reduce_fusion
  219.5 0.3 copy-done.10
  220.3 0.3 fusion.45
  220.9 33.8 %all_to_all.36 = bf16[8,64,2048]{2,1,0:T(8,128)(2,1)} all-to-all(bf16[8,64,2048]{2,1,0:T(8,128)(2,1)S(1)} %broadcast_in_dim.55), channel_id=1, replica_groups=mesh['dp'=16,'tensor'=8] {'tensor'}, dimensions={0} | all-to-all | bytes 4194304 | tf_op jit(solution)/shard_map/all_to_all | solution.py:106
  254.7 1.6 broadcast_in_dim.56
  256.3 5.7 %all-to-all-start.5 = ((bf16[8,64,2048]{2,1,0:T(8,128)(2,1)}), bf16[8,64,2048]{2,1,0:T(8,128)(2,1)S(1)}, u32[]{:S(2)}, u32[]{:S(2)}) async-start(bf16[8,64,2048]{2,1,0:T(8,128)(2,1)} %broadcast_in_dim.56), calls=%async_computation.5 | async-start | bytes 4194304 | tf_op jit(solution)/shard_map/all_to_all | solution.py:106
  262.0 7.6 %convolution_bitcast_fusion.1 = f32[2,512,1024]{1,2,0:T(8,128)S(1)} fusion(bf16[3,2048,1024]{1,2,0:T(8,128)(2,1)} %all-gather.5.cloned.1.call-done, bf16[512,2048,1]{1,0,2:T(8,128)(2,1)} %bitcast.108), kind=kOutput, calls=%fused_computation.28 | convolution fusion | flops 4294967296 | bytes 18874368 | tf_op jit(solution)/shard_map/td,cdf->ctf/dot_general | solution.py:147
  269.6 6.1 %fusion.12 = bf16[512,2048]{1,0:T(8,128)(2,1)} fusion(bf16[3,2048,1024]{1,2,0:T(8,128)(2,1)} %all-gather.5.cloned.1.call-done, f32[2,512,1024]{1,2,0:T(8,128)S(1)} %convolution_bitcast_fusion.1), kind=kOutput, calls=%fused_computation.23 | convolution fusion | flops 2151677952 | bytes 10485760 | tf_op jit(solution)/shard_map/tf,df->td/dot_general | solution.py:149
  275.8 14.8 %all-to-all-done.5 = bf16[8,64,2048]{2,1,0:T(8,128)(2,1)S(1)} async-done(((bf16[8,64,2048]{2,1,0:T(8,128)(2,1)}), bf16[8,64,2048]{2,1,0:T(8,128)(2,1)S(1)}, u32[]{:S(2)}, u32[]{:S(2)}) %all-to-all-start.5) | async-done | bytes 2097184 | tf_op jit(solution)/shard_map/all_to_all | solution.py:106
  290.6 1.3 copy-done.11
  291.9 4.7 %all-to-all-start.4 = ((bf16[8,64,2048]{2,1,0:T(8,128)(2,1)}), bf16[8,64,2048]{2,1,0:T(8,128)(2,1)S(1)}, u32[]{:S(2)}, u32[]{:S(2)}) async-start(bf16[8,64,2048]{2,1,0:T(8,128)(2,1)} %bitcast.107), calls=%async_computation.4 | async-start | bytes 4194304 | tf_op jit(solution)/shard_map/all_to_all | solution.py:112
  296.6 7.6 %convolution_bitcast_fusion = f32[2,512,1024]{1,2,0:T(8,128)S(1)} fusion(bf16[3,2048,1024]{1,2,0:T(8,128)(2,1)} %all-gather.5.cloned.1.call-done, bf16[512,2048,1]{1,0,2:T(8,128)(2,1)} %bitcast.106), kind=kOutput, calls=%fused_computation.27 | convolution fusion | flops 4294967296 | bytes 18874368 | tf_op jit(solution)/shard_map/td,cdf->ctf/dot_general | solution.py:147
  304.2 6.1 %fusion.13 = bf16[512,2048]{1,0:T(8,128)(2,1)} fusion(bf16[3,2048,1024]{1,2,0:T(8,128)(2,1)} %all-gather.5.cloned.1.call-done, f32[2,512,1024]{1,2,0:T(8,128)S(1)} %convolution_bitcast_fusion), kind=kOutput, calls=%fused_computation.24 | convolution fusion | flops 2151677952 | bytes 10485760 | tf_op jit(solution)/shard_map/tf,df->td/dot_general | solution.py:149
  310.3 14.8 %all-to-all-done.4 = bf16[8,64,2048]{2,1,0:T(8,128)(2,1)S(1)} async-done(((bf16[8,64,2048]{2,1,0:T(8,128)(2,1)}), bf16[8,64,2048]{2,1,0:T(8,128)(2,1)S(1)}, u32[]{:S(2)}, u32[]{:S(2)}) %all-to-all-start.4) | async-done | bytes 2097184 | tf_op jit(solution)/shard_map/all_to_all | solution.py:112
  325.2 4.3 %all-to-all-start.6 = ((bf16[8,64,2048]{2,1,0:T(8,128)(2,1)}), bf16[8,64,2048]{2,1,0:T(8,128)(2,1)}, u32[]{:S(2)}, u32[]{:S(2)}) async-start(bf16[8,64,2048]{2,1,0:T(8,128)(2,1)} %bitcast.109), calls=%async_computation.6 | async-start | bytes 4194304 | tf_op jit(solution)/shard_map/all_to_all | solution.py:112
  329.5 0.3 convert_reduce_fusion.3
  329.9 28.3 %all-to-all-done.6 = bf16[8,64,2048]{2,1,0:T(8,128)(2,1)} async-done(((bf16[8,64,2048]{2,1,0:T(8,128)(2,1)}), bf16[8,64,2048]{2,1,0:T(8,128)(2,1)}, u32[]{:S(2)}, u32[]{:S(2)}) %all-to-all-start.6) | async-done | bytes 2097184 | tf_op jit(solution)/shard_map/all_to_all | solution.py:112
  358.1 2.0 convert_reduce_fusion.2
  360.1 0.9 fusion.46
  (86 shorter events, 2.8 us)
Async XLA Ops:
  7.2 4.2 %copy-start.19 = (bf16[1024,128]{1,0:T(8,128)(2,1)S(1)}, bf16[1024,128]{1,0:T(8,128)(2,1)}, u32[]{:S(2)}) copy-start(bf16[1024,128]{1,0:T(8,128)(2,1)} %param.16) | copy-start | bytes 786436
  7.2 91.7 %all-gather.3.cloned.1.call-start = ((), (), s32[]{:S(2)}) async-start(), calls=%async_computation.7 | async-start | bytes 4456448 | tf_op jit(solution)/shard_map/all_gather | solution.py:122
  8.3 4.1 %copy-start.9 = (bf16[128,2048]{1,0:T(8,128)(2,1)S(1)}, bf16[128,2048]{1,0:T(8,128)(2,1)}, u32[]{:S(2)}) copy-start(bf16[128,2048]{1,0:T(8,128)(2,1)} %param.10) | copy-start | bytes 1572868
  10.0 252.0 %all-gather.5.cloned.1.call-start = ((), (), s32[]{:S(2)}) async-start(), calls=%async_computation.8 | async-start | bytes 13369344 | tf_op jit(solution)/shard_map/all_gather | solution.py:125
  15.0 8.3 %copy-start.22 = (s32[1024]{0:T(1024)S(1)}, s32[1024]{0:T(1024)}, u32[]{:S(2)}) copy-start(s32[1024]{0:T(1024)} %param.12) | copy-start | bytes 12292
  15.0 8.3 %copy-start = (s32[64]{0:T(128)S(1)}, s32[64]{0:T(128)}, u32[]{:S(2)}) copy-start(s32[64]{0:T(128)} %param.17) | copy-start | bytes 772
  15.0 11.5 %copy-start.21 = (s32[1024]{0:T(1024)S(1)}, s32[1024]{0:T(1024)}, u32[]{:S(2)}) copy-start(s32[1024]{0:T(1024)} %param.11) | copy-start | bytes 12292
  15.0 64.6 %all-to-all-start = ((bf16[8,128,2048]{2,1,0:T(8,128)(2,1)}), bf16[8,128,2048]{2,1,0:T(8,128)(2,1)}, u32[]{:S(2)}, u32[]{:S(2)}) async-start(bf16[8,128,2048]{2,1,0:T(8,128)(2,1)} %broadcast_in_dim.43), calls=%async_computation | async-start | bytes 8388608 | tf_op jit(solution)/shard_map/all_to_all | solution.py:106
  105.0 1.6 copy-start.8
  106.7 4.0 %copy-start.3 = (bf16[1,1024,256]{1,2,0:T(8,128)(2,1)}, bf16[1,1024,256]{1,2,0:T(8,128)(2,1)S(1)}, u32[]{:S(2)}) copy-start(bf16[1,1024,256]{1,2,0:T(8,128)(2,1)S(1)} %slice.224) | copy-start | bytes 1572868
  113.6 2.8 copy-start.13
  113.9 0.8 copy-start.5
  119.5 4.0 %copy-start.2 = (f32[1,1024,256]{1,2,0:T(8,128)S(1)}, f32[1,1024,256]{1,2,0:T(8,128)}, u32[]{:S(2)}) copy-start(f32[1,1024,256]{1,2,0:T(8,128)} %get-tuple-element.25) | copy-start | bytes 3145732
  119.5 31.2 %all-to-all-start.1 = ((bf16[16,5,2,16,256]{4,3,2,1,0:T(8,128)(2,1)}), bf16[16,5,2,16,256]{4,3,2,1,0:T(8,128)(2,1)S(1)}, u32[]{:S(2)}, u32[]{:S(2)}) async-start(bf16[16,5,2,16,256]{4,3,2,1,0:T(8,128)(2,1)} %fusion.30), calls=%async_computation.1 | async-start | bytes 2621440 | tf_op jit(solution)/shard_map/all_to_all | solution.py:84
  128.2 2.5 copy-start.6
  129.7 0.8 copy-start.14
  129.8 1.0 copy-start.16
  129.8 1.5 copy-start.18
  131.2 1.3 copy-start.12
  131.3 1.3 slice-start
  132.6 4.5 %copy-start.7 = (bf16[1024,2,128]{2,0,1:T(8,128)(2,1)S(1)}, bf16[1024,2,128]{2,0,1:T(8,128)(2,1)}, u32[]{:S(2)}) copy-start(bf16[1024,2,128]{2,0,1:T(8,128)(2,1)} %copy-done.5) | copy-start | bytes 1572868
  132.6 4.5 %copy-start.15 = (bf16[1024,2,64]{2,0,1:T(8,128)(2,1)S(1)}, bf16[1024,2,64]{2,0,1:T(8,128)(2,1)}, u32[]{:S(2)}) copy-start(bf16[1024,2,64]{2,0,1:T(8,128)(2,1)} %copy-done.14) | copy-start | bytes 786436
  132.6 4.5 %copy-start.17 = (bf16[1024,2,64]{2,0,1:T(8,128)(2,1)S(1)}, bf16[1024,2,64]{2,0,1:T(8,128)(2,1)}, u32[]{:S(2)}) copy-start(bf16[1024,2,64]{2,0,1:T(8,128)(2,1)} %copy-done.16) | copy-start | bytes 786436
  137.1 5.2 %copy-start.4 = (bf16[1,1024,256]{1,2,0:T(8,128)(2,1)S(1)}, bf16[1,1024,256]{1,2,0:T(8,128)(2,1)}, u32[]{:S(2)}) copy-start(bf16[1,1024,256]{1,2,0:T(8,128)(2,1)} %copy-done.3) | copy-start | bytes 1572868
  142.3 2.5 copy-start.20
  153.8 64.9 %copy-start.1 = (bf16[64,2,16,256]{3,2,1,0:T(8,128)(2,1)}, bf16[64,2,16,256]{3,2,1,0:T(8,128)(2,1)S(1)}, u32[]{:S(2)}) copy-start(bf16[64,2,16,256]{3,2,1,0:T(8,128)(2,1)S(1)} %scatter_fusion) | copy-start | bytes 3145732
  218.7 1.0 copy-start.10
  256.3 34.3 %all-to-all-start.5 = ((bf16[8,64,2048]{2,1,0:T(8,128)(2,1)}), bf16[8,64,2048]{2,1,0:T(8,128)(2,1)S(1)}, u32[]{:S(2)}, u32[]{:S(2)}) async-start(bf16[8,64,2048]{2,1,0:T(8,128)(2,1)} %broadcast_in_dim.56), calls=%async_computation.5 | async-start | bytes 4194304 | tf_op jit(solution)/shard_map/all_to_all | solution.py:106
  290.6 1.3 copy-start.11
  291.9 33.3 %all-to-all-start.4 = ((bf16[8,64,2048]{2,1,0:T(8,128)(2,1)}), bf16[8,64,2048]{2,1,0:T(8,128)(2,1)S(1)}, u32[]{:S(2)}, u32[]{:S(2)}) async-start(bf16[8,64,2048]{2,1,0:T(8,128)(2,1)} %bitcast.107), calls=%async_computation.4 | async-start | bytes 4194304 | tf_op jit(solution)/shard_map/all_to_all | solution.py:112
  325.2 33.0 %all-to-all-start.6 = ((bf16[8,64,2048]{2,1,0:T(8,128)(2,1)}), bf16[8,64,2048]{2,1,0:T(8,128)(2,1)}, u32[]{:S(2)}, u32[]{:S(2)}) async-start(bf16[8,64,2048]{2,1,0:T(8,128)(2,1)} %bitcast.109), calls=%async_computation.6 | async-start | bytes 4194304 | tf_op jit(solution)/shard_map/all_to_all | solution.py:112
Sparse Core Ops, SparseCore 0:
  10.2 88.6 all-gather.2
  100.4 154.3 all-gather.4
